TPU v7x, 32 devices: a whole 2x2x4 slice. The times are simulated.
32 devices in a mesh: ens: 2 (over x), gx: 16 (over z, y, core).
Axes of the slice: x: 2, y: 2, z: 4, core: 2. Of those that a mesh axis runs over, the one named last changes fastest.
Arguments:
- misfit: float32 [4, 16, 128, 512], P('ens', None, 'gx'), parts along dimension 0, may hold values from -8 to 8
- adjoint_guess: float32 [4, 16, 128, 512], P('ens', None, 'gx'), parts along dimension 0, may hold values from -4 to 4
- viscosity: float32 [32, 128, 512], P('ens', 'gx'), parts along dimension 0, may hold values from 0.3 to 3
- friction: float32 [128, 1024], P('gx', 'ens'), parts along dimension 1, may hold values from 0.1 to 10
- ice_mask: int32 [128, 1024], P('gx', 'ens'), parts along dimension 1, may hold values from 0 to 2
- forward_bed: float32 [4, 128, 512], P('ens', 'gx'), parts along dimension 0, may hold values from -6 to 6
Outputs:
- adjoint: float32 [4, 16, 128, 512], P('ens', None, 'gx'), parts along dimension 0
- friction_gradient: float32 [128, 1024], P('gx', 'ens'), parts along dimension 1
There are 2 independent parts, one for each index of `ens`. A program takes and returns all parts, laid end to end along the dimension named above; each array names one. Nothing has to cross between parts.
All inputs are finite; a program needn't handle non-finite values.
Results may differ from a plain program's by a relative error of at most 0.0003.
Values sent between devices are 32-bit elements; how exact they have to be, the bound alone decides.
No kernel may reach another device: no remote copies, remote signals or barrier semaphores. Data moves between devices by JAX's collectives and lax.ppermute only.
A program may use at most 64 MiB of HBM per device.

v0:
```python
import functools

import jax
import jax.numpy as jnp
from jax import lax
from jax.experimental import pallas as pl
from jax.experimental.pallas import tpu as pltpu
from jax.sharding import PartitionSpec as P

NU = 2
COARSE_SWEEPS = 6


horizontal_scale = 1.0
vertical_scale = 4.0
relax_weight = 0.8


def with_halo(cells, sides, width):
    for axis, dim in sides:
        count = lax.axis_size(axis)
        ends = count - 1
        head = lax.slice_in_dim(cells, 0, width, axis=dim)
        tail = lax.slice_in_dim(cells, cells.shape[dim] - width, cells.shape[dim], axis=dim)
        cells = jnp.concatenate(
            [
                lax.ppermute(tail, axis, [(i, (i + 1) % count) for i in range(ends)]),
                cells,
                lax.ppermute(head, axis, [((i + 1) % count, i) for i in range(ends)]),
            ],
            axis=dim,
        )
    return cells


def trade(parts, width):
    count = lax.axis_size("gx")
    ends = count - 1
    heads = [lax.slice_in_dim(a, 0, width, axis=dim) for a, dim in parts]
    tails = [lax.slice_in_dim(a, a.shape[dim] - width, a.shape[dim], axis=dim) for a, dim in parts]
    pack = lambda pieces: jnp.concatenate([p.reshape(-1) for p in pieces])
    from_left = lax.ppermute(pack(tails), "gx", [(i, i + 1) for i in range(ends)])
    from_right = lax.ppermute(pack(heads), "gx", [(i + 1, i) for i in range(ends)])
    out = []
    offset = 0
    for (a, dim), h in zip(parts, heads):
        size = h.size
        left = from_left[offset : offset + size].reshape(h.shape)
        right = from_right[offset : offset + size].reshape(h.shape)
        offset += size
        out.append(jnp.concatenate([left, a, right], axis=dim))
    return out


def block_mean(field, factor):
    lead = field.shape[:-2]
    rows, cols = (field.shape[-2], field.shape[-1])
    shaped = field.reshape(lead + (rows // factor, factor, cols // factor, factor))
    return shaped.mean(axis=(-3, -1))


def reaction_field(friction, ice_mask, layers):
    open_water = (ice_mask == 0).astype(jnp.float32)
    grounded = (ice_mask == 2).astype(jnp.float32)
    bottom = (jnp.arange(layers) == 0).astype(jnp.float32).reshape(layers, 1, 1)
    return 0.02 + 2.0 * open_water[None] + bottom * (grounded * friction)[None]


def build_operator(eta_level, react_level, level_index):
    scale = horizontal_scale / 4.0**level_index
    weight_x = jnp.array([4.0, 1.0], jnp.float32).reshape(2, 1, 1, 1) * scale
    weight_y = jnp.array([1.0, 4.0], jnp.float32).reshape(2, 1, 1, 1) * scale
    inner = eta_level[:, 1:-1, :]
    face_x = weight_x * (0.5 * (eta_level[:, 1:, :] + eta_level[:, :-1, :]))[None]
    padded = jnp.pad(inner, ((0, 0), (0, 0), (1, 1)))
    face_y = weight_y * (0.5 * (padded[:, :, 1:] + padded[:, :, :-1]))[None]
    face_z = vertical_scale * 0.5 * (inner[1:] + inner[:-1])
    vertical = jnp.pad(face_z, ((1, 1), (0, 0), (0, 0)))
    diagonal = face_x[:, :, 1:] + face_x[:, :, :-1] + face_y[..., 1:] + face_y[..., :-1]
    diagonal = diagonal + (vertical[1:] + vertical[:-1] + react_level)[None]
    layers = diagonal.shape[1]
    inverses = []
    ratios = []
    for layer in range(layers):
        pivot = diagonal[:, layer]
        if layer > 0:
            pivot = pivot - face_z[layer - 1] * ratios[-1]
        inverse = 1.0 / pivot
        inverses.append(inverse)
        if layer < layers - 1:
            ratios.append(face_z[layer] * inverse)
    return (face_x, face_y, face_z, react_level, jnp.stack(inverses, 1), jnp.stack(ratios, 1))


def lane_ops(operator):
    face_x, face_y, face_z, react_level, inverses, ratios = operator
    return (face_x[:, :, :-1], face_x[:, :, 1:], face_y[..., :-1], face_y[..., 1:], face_z, react_level, inverses, ratios)


def sweep_kernel(w_ref, b_ref, fxl_ref, fxr_ref, fyl_ref, fyr_ref, fz_ref, re_ref, inv_ref, rat_ref, mask_ref, out_ref,
                 *, rows, cut_w, cut_b, cut_op, mode):
    layers = out_ref.shape[1]
    cols = out_ref.shape[3]
    lane = lax.broadcasted_iota(jnp.int32, (rows, cols), 1)
    probe = pltpu.roll(lane, 1, 1)
    forward_roll = probe == jnp.where(lane == 0, cols - 1, lane - 1)
    first_col = lane == 0
    last_col = lane == cols - 1

    def cell(ref, k, cut):
        return ref[0, k, pl.ds(cut, rows), :]

    def field(k):
        return w_ref[0, k, pl.ds(cut_w + 1, rows), :]

    def applied(k):
        w = field(k)
        west = w_ref[0, k, pl.ds(cut_w, rows), :]
        east = w_ref[0, k, pl.ds(cut_w + 2, rows), :]
        result = -(cell(fxr_ref, k, cut_op) * (east - w) - cell(fxl_ref, k, cut_op) * (w - west))
        ahead = pltpu.roll(w, 1, 1)
        behind = pltpu.roll(w, cols - 1, 1)
        south = jnp.where(forward_roll, ahead, behind)
        north = jnp.where(forward_roll, behind, ahead)
        south = jnp.where(first_col, 0.0, south)
        north = jnp.where(last_col, 0.0, north)
        result = result - (cell(fyr_ref, k, cut_op) * (north - w) - cell(fyl_ref, k, cut_op) * (w - south))
        up = fz_ref[k, pl.ds(cut_op, rows), :] * (field(k + 1) - w) if k < layers - 1 else 0.0
        down = fz_ref[k - 1, pl.ds(cut_op, rows), :] * (w - field(k - 1)) if k > 0 else 0.0
        result = result - (up - down)
        return result + re_ref[k, pl.ds(cut_op, rows), :] * w

    if mode == "residual":
        for k in range(layers):
            out_ref[0, k] = cell(b_ref, k, cut_b) - applied(k)
        return
    keep = mask_ref[...] > 0.5
    previous = None
    for k in range(layers):
        residual = cell(b_ref, k, cut_b)
        if mode == "sweep":
            residual = residual - applied(k)
        if k == 0:
            forward = residual * cell(inv_ref, 0, cut_op)
        else:
            forward = (residual + fz_ref[k - 1, pl.ds(cut_op, rows), :] * previous) * cell(inv_ref, k, cut_op)
        out_ref[0, k] = forward
        previous = forward
    back = previous
    for k in range(layers - 1, -1, -1):
        if k < layers - 1:
            back = out_ref[0, k] + rat_ref[0, k, pl.ds(cut_op, rows), :] * back
        if mode == "sweep":
            value = field(k) + relax_weight * back
        else:
            value = relax_weight * back
        out_ref[0, k] = jnp.where(keep, value, 0.0)


def kernel_sweep(field_rim, target, lanes, cut_b, cut_op, mask, mode="sweep", cut_w=0, rows=None):
    parts, layers, rows_rim, cols = field_rim.shape
    rows = rows_rim - 2 if rows is None else rows
    fxl, fxr, fyl, fyr, fz, re, inv, rat = lanes
    per_part = lambda a: pl.BlockSpec((1,) + a.shape[1:], lambda c: (c,) + (0,) * (a.ndim - 1))
    whole = lambda a: pl.BlockSpec(a.shape, lambda c: (0,) * a.ndim)
    operands = [field_rim, target, fxl, fxr, fyl, fyr, fz, re, inv, rat, mask]
    specs = [per_part(field_rim), per_part(target), per_part(fxl), per_part(fxr), per_part(fyl), per_part(fyr),
             whole(fz), whole(re), per_part(inv), per_part(rat), whole(mask)]
    body = functools.partial(sweep_kernel, rows=rows, cut_w=cut_w, cut_b=cut_b, cut_op=cut_op, mode=mode)
    return pl.pallas_call(
        body,
        grid=(parts,),
        in_specs=specs,
        out_specs=pl.BlockSpec((1, layers, rows, cols), lambda c: (c, 0, 0, 0)),
        out_shape=jax.ShapeDtypeStruct((parts, layers, rows, cols), jnp.float32),
    )(*operands)


def build_kernel(eta_ref, re_ref, fxl_ref, fxr_ref, fyl_ref, fyr_ref, fz_ref, reo_ref, inv_ref, rat_ref,
                 *, rows, cut_re, scale):
    component = pl.program_id(0)
    layers = eta_ref.shape[0]
    cols = eta_ref.shape[2]
    lane = lax.broadcasted_iota(jnp.int32, (rows, cols), 1)
    probe = pltpu.roll(lane, 1, 1)
    forward_roll = probe == jnp.where(lane == 0, cols - 1, lane - 1)
    first_col = lane == 0
    last_col = lane == cols - 1
    weight_x = jnp.where(component == 0, 4.0, 1.0) * scale
    weight_y = jnp.where(component == 0, 1.0, 4.0) * scale

    def inner(k):
        return eta_ref[k, pl.ds(1, rows), :]

    faces_z = [vertical_scale * 0.5 * (inner(k + 1) + inner(k)) for k in range(layers - 1)]
    ratio = None
    for k in range(layers):
        middle = inner(k)
        west = eta_ref[k, pl.ds(0, rows), :]
        east = eta_ref[k, pl.ds(2, rows), :]
        ahead = pltpu.roll(middle, 1, 1)
        behind = pltpu.roll(middle, cols - 1, 1)
        south = jnp.where(first_col, 0.0, jnp.where(forward_roll, ahead, behind))
        north = jnp.where(last_col, 0.0, jnp.where(forward_roll, behind, ahead))
        face_w = weight_x * (0.5 * (middle + west))
        face_e = weight_x * (0.5 * (east + middle))
        face_s = weight_y * (0.5 * (middle + south))
        face_n = weight_y * (0.5 * (north + middle))
        react = re_ref[min(k, re_ref.shape[0] - 1), pl.ds(cut_re, rows), :]
        up = faces_z[k] if k < layers - 1 else 0.0
        down = faces_z[k - 1] if k > 0 else 0.0
        diagonal = face_e + face_w + face_n + face_s
        diagonal = diagonal + (up + down + react)
        if k > 0:
            diagonal = diagonal - faces_z[k - 1] * ratio
        inverse = 1.0 / diagonal
        fxl_ref[0, k] = face_w
        fxr_ref[0, k] = face_e
        fyl_ref[0, k] = face_s
        fyr_ref[0, k] = face_n
        reo_ref[k] = react
        inv_ref[0, k] = inverse
        if k < layers - 1:
            ratio = faces_z[k] * inverse
            fz_ref[k] = faces_z[k]
            rat_ref[0, k] = ratio


def kernel_operator(eta_level, react_level, level_index, cut_re=0):
    layers, rows_eta, cols = eta_level.shape
    rows = rows_eta - 2
    whole = lambda a: pl.BlockSpec(a.shape, lambda c: (0,) * a.ndim)
    per_part = lambda shape: pl.BlockSpec((1,) + shape, lambda c: (c,) + (0,) * len(shape))
    cell = (layers, rows, cols)
    faces = (layers - 1, rows, cols)
    body = functools.partial(build_kernel, rows=rows, cut_re=cut_re, scale=horizontal_scale / 4.0**level_index)
    shapes = [(2,) + cell] * 4 + [faces, cell, (2,) + cell, (2,) + faces]
    specs = [per_part(cell)] * 4 + [
        pl.BlockSpec(faces, lambda c: (0, 0, 0)),
        pl.BlockSpec(cell, lambda c: (0, 0, 0)),
        per_part(cell),
        per_part(faces),
    ]
    return tuple(
        pl.pallas_call(
            body,
            grid=(2,),
            in_specs=[whole(eta_level), whole(react_level)],
            out_specs=specs,
            out_shape=[jax.ShapeDtypeStruct(s, jnp.float32) for s in shapes],
        )(eta_level, react_level)
    )


def rows_inside(cells, halo, extent, cols):
    return jnp.broadcast_to(inside(cells, halo, extent)[0, 0], (extent, cols)).astype(jnp.float32)


def shrink(operator, cut):
    if cut == 0:
        return operator
    face_x, face_y, face_z, react_level, inverses, ratios = operator
    rows = face_y.shape[2]
    return (
        face_x[:, :, cut : rows + 1 - cut],
        face_y[:, :, cut : rows - cut],
        face_z[:, cut : rows - cut],
        react_level[:, cut : rows - cut],
        inverses[:, :, cut : rows - cut],
        ratios[:, :, cut : rows - cut],
    )


def apply_operator(field_rim, operator):
    face_x, face_y, face_z, react_level, inverses, ratios = operator
    field = field_rim[:, :, 1:-1, :]
    flux_x = face_x * (field_rim[:, :, 1:, :] - field_rim[:, :, :-1, :])
    result = -(flux_x[:, :, 1:] - flux_x[:, :, :-1])
    padded = jnp.pad(field, ((0, 0), (0, 0), (0, 0), (1, 1)))
    flux_y = face_y * (padded[..., 1:] - padded[..., :-1])
    result = result - (flux_y[..., 1:] - flux_y[..., :-1])
    flux_z = face_z[None] * (field[:, 1:] - field[:, :-1])
    flux_z = jnp.pad(flux_z, ((0, 0), (1, 1), (0, 0), (0, 0)))
    result = result - (flux_z[:, 1:] - flux_z[:, :-1])
    return result + react_level[None] * field


def line_solve(residual, operator):
    face_z, inverses, ratios = (operator[2], operator[4], operator[5])
    layers = residual.shape[1]
    forward = [residual[:, 0] * inverses[:, 0]]
    for layer in range(1, layers):
        forward.append((residual[:, layer] + face_z[layer - 1] * forward[-1]) * inverses[:, layer])
    backward = [forward[-1]]
    for layer in range(layers - 2, -1, -1):
        backward.append(forward[layer] + ratios[:, layer] * backward[-1])
    return jnp.stack(backward[::-1], 1)


def sweep(field_rim, target, operator):
    field = field_rim[:, :, 1:-1, :]
    return field + relax_weight * line_solve(target - apply_operator(field_rim, operator), operator)


def restrict(field):
    return block_mean(field, 2)


def prolong(field):
    return jnp.repeat(jnp.repeat(field, 2, axis=2), 2, axis=3)


def pad_rim(field):
    return jnp.pad(field, ((0, 0), (0, 0), (1, 1), (0, 0)))


def inside(cells, halo, extent):
    count = lax.axis_size("gx")
    first = lax.axis_index("gx") * cells - halo
    index = first + jnp.arange(extent)
    return ((index >= 0) & (index < count * cells)).reshape(1, 1, extent, 1)


def keep_inside(field, cells, halo):
    return jnp.where(inside(cells, halo, field.shape[2]), field, 0.0)


def window(full, dim, start, size, pad):
    widths = [(0, 0)] * full.ndim
    widths[dim] = (pad, pad)
    return lax.dynamic_slice_in_dim(jnp.pad(full, widths), start, size, axis=dim)


def nearby(cells, dim, hops):
    count = lax.axis_size("gx")
    lows = []
    highs = []
    for step in range(1, hops + 1):
        lows.insert(0, lax.ppermute(cells, "gx", [(i, i + step) for i in range(count - step)]))
        highs.append(lax.ppermute(cells, "gx", [(i + step, i) for i in range(count - step)]))
    return jnp.concatenate(lows + [cells] + highs, axis=dim)


def shards(misfit, adjoint_guess, viscosity, friction, ice_mask, forward_bed):
    layers, cells, cols = viscosity.shape
    where = lax.axis_index("gx")
    react_fine = reaction_field(friction, ice_mask, layers)
    react_pair = react_fine[:2]

    eta_1 = block_mean(viscosity, 2)
    eta_2 = block_mean(viscosity, 4)
    react_1 = block_mean(react_pair, 2)
    react_2 = block_mean(react_pair, 4)
    pieces = [eta_1, react_1, eta_2, react_2]
    packed = jnp.concatenate([p.reshape(-1) for p in pieces])
    gathered = lax.all_gather(packed[None], "gx", axis=0, tiled=True)
    count = gathered.shape[0]
    unpacked = []
    offset = 0
    for p in pieces:
        block = gathered[:, offset : offset + p.size].reshape((count,) + p.shape)
        offset += p.size
        unpacked.append(jnp.moveaxis(block, 0, 1).reshape((p.shape[0], count * p.shape[1], p.shape[2])))
    eta_1_all, react_1_all, eta_2_all, react_2_all = unpacked

    halo = 4
    eta_wide, guess_wide, misfit_wide, react_wide = trade(
        [(viscosity, 1), (adjoint_guess, 2), (misfit, 2), (react_pair, 1)], halo
    )
    op_0 = kernel_operator(eta_wide, react_wide, 0, 1)
    fine = kernel_sweep(guess_wide, misfit_wide, op_0, 1, 0, rows_inside(cells, 3, cells + 6, cols))
    fine = kernel_sweep(fine, misfit_wide, op_0, 2, 1, rows_inside(cells, 2, cells + 4, cols))
    residual = kernel_sweep(fine, misfit_wide, op_0, 4, 3, rows_inside(cells, 0, cells, cols), "residual", 1, cells)
    middle_rhs = restrict(residual)

    half = cells // 2
    wide = cols // 2
    rhs_wide = with_halo(middle_rhs, (("gx", 2),), half)
    eta_1_wide = window(eta_1_all, 1, where * half, 3 * half + 2, half + 1)
    react_1_wide = window(react_1_all, 1, where * half, 3 * half, half)
    op_1 = kernel_operator(eta_1_wide, react_1_wide, 1)
    middle = kernel_sweep(rhs_wide, rhs_wide, op_1, 0, 0, rows_inside(half, half, 3 * half, wide), "zero", 0, 3 * half)
    middle = kernel_sweep(middle, rhs_wide, op_1, 1, 1, rows_inside(half, half - 1, 3 * half - 2, wide))
    residual = kernel_sweep(middle, rhs_wide, op_1, half, half, rows_inside(half, 0, half, wide), "residual", half - 2, half)
    coarse_rhs = restrict(residual)

    quarter = cells // 4
    narrow = cols // 4
    reach = 3
    span = reach + COARSE_SWEEPS - 1
    coarse_rhs_near = nearby(coarse_rhs, 2, span // quarter)
    eta_2_near = window(eta_2_all, 1, where * quarter, quarter + 2 * span + 2, span + 1)
    react_2_near = window(react_2_all, 1, where * quarter, quarter + 2 * span, span)
    op_2 = kernel_operator(eta_2_near, react_2_near, 2)
    extent = quarter + 2 * span
    coarse_mask = rows_inside(quarter, span, extent, narrow)
    coarse = kernel_sweep(coarse_rhs_near, coarse_rhs_near, op_2, 0, 0, coarse_mask, "zero", 0, extent)
    for turn in range(COARSE_SWEEPS - 1):
        coarse = kernel_sweep(pad_rim(coarse), coarse_rhs_near, op_2, 0, 0, coarse_mask)
    coarse_near = coarse[:, :, span - reach : span + quarter + reach]

    lift = prolong(coarse_near)
    trim = 2 * reach - (half - 1)
    middle = middle + lift[:, :, trim : lift.shape[2] - trim]
    middle = kernel_sweep(middle, rhs_wide, op_1, 2, 2, rows_inside(half, half - 2, 3 * half - 4, wide))
    middle = kernel_sweep(middle, rhs_wide, op_1, 3, 3, rows_inside(half, half - 3, 3 * half - 6, wide))
    fine = fine + prolong(middle)
    fine = kernel_sweep(fine, misfit_wide, op_0, 3, 2, rows_inside(cells, 1, cells + 2, cols))
    fine = kernel_sweep(fine, misfit_wide, op_0, 4, 3, rows_inside(cells, 0, cells, cols))
    grounded = (ice_mask == 2).astype(jnp.float32)
    gradient = -grounded * (forward_bed[0] * fine[0, 0] + forward_bed[1] * fine[1, 0])
    return (fine, gradient)


def solution(mesh):
    placed = (
        P("ens", None, "gx", None),
        P("ens", None, "gx", None),
        P("ens", "gx", None),
        P("gx", "ens"),
        P("gx", "ens"),
        P("ens", "gx", None),
    )
    return jax.shard_map(
        shards,
        mesh=mesh,
        in_specs=placed,
        out_specs=(P("ens", None, "gx", None), P("gx", "ens")),
        check_vma=False,
    )
```

profile of v0, /device:TPU:10, one launch (start us, length us, event | category | flops | bytes accessed | tf_op | source)
XLA Modules:
  0.0 218.4 jit_solution(17310483759007696938)
XLA Ops:
  13.8 4.5 %collective-permute-start.1 = (f32[167936]{0:T(1024)}, f32[167936]{0:T(1024)}, u32[]{:S(2)}, u32[]{:S(2)}) collective-permute-start(f32[167936]{0:T(1024)} %pad_maximum_fusion.3), channel_id=1, source_target_pairs={{1,0},{2,1},{3,2},{4,3},{5,4},{6,5},{7,6},{8,7},{9,8},{10,9},{11,1... | collective-permute-start | bytes 2015240 | tf_op jit(solution)/shard_map/ppermute | solution.py:43
  18.3 3.4 %reshape.240 = f32[2,4,2,256,2]{4,3,2,1,0:T(8,128)} reshape(f32[2,8,512]{2,1,0:T(8,128)S(1)} %slice.163) | data formatting | bytes 65536 | tf_op jit(solution)/shard_map/reshape | solution.py:58
  36.8 5.1 %shard_map.77 = (f32[2,16,14,512]{3,2,1,0:T(8,128)}, f32[2,16,14,512]{3,2,1,0:T(8,128)}, f32[2,16,14,512]{3,2,1,0:T(8,128)}, f32[2,16,14,512]{3,2,1,0:T(8,128)},...) custom-call(f32[16,16,512]{2,1,0:T(8,128)} %pad_maximum_fusion.4.eta_, ...), custom_call_target="tpu_custom_call" | custom-call | tf_op jit(solution)/shard_map/pallas_call | solution.py:245
  44.4 5.8 %shard_map.78.w_ref = f32[2,16,14,512]{3,2,1,0:T(8,128)} custom-call(f32[2,16,16,512]{3,2,1,0:T(8,128)} %get-tuple-element.65.w_ref, f32[2,16,16,512]{3,2,1,0:T(8,128)} %get-tuple-element.66.b_ref, f32[2,16,14,512]{3,2,1,0:T(8,128)} %get-tuple-element.26.fxl_ref, f32[2,16,14,512]{3,2,1,0:T(8,128)} %get-tuple-element.27.fxr_ref, ...), custom_call_target="tpu_custom_call" | custom-call | tf_op jit(solution)/shard_map/pallas_call | solution.py:170
  50.8 5.8 %shard_map.79.w_ref = f32[2,16,12,512]{3,2,1,0:T(8,128)} custom-call(f32[2,16,14,512]{3,2,1,0:T(8,128)} %shard_map.78.w_ref, f32[2,16,16,512]{3,2,1,0:T(8,128)} %get-tuple-element.66.b_ref, f32[2,16,14,512]{3,2,1,0:T(8,128)} %get-tuple-element.26.fxl_ref, f32[2,16,14,512]{3,2,1,0:T(8,128)} %get-tuple-element.27.fxr_ref, ...), custom_call_target="tpu_custom_call" | custom-call | tf_op jit(solution)/shard_map/pallas_call | solution.py:170
  57.3 5.1 %shard_map.80 = f32[2,16,8,512]{3,2,1,0:T(8,128)} custom-call(f32[2,16,12,512]{3,2,1,0:T(8,128)} %shard_map.79.w_ref, f32[2,16,16,512]{3,2,1,0:T(8,128)} %get-tuple-element.66.b_ref, f32[2,16,14,512]{3,2,1,0:T(8,128)} %get-tuple-element.26.fxl_ref, f32[2,16,14,512]{3,2,1,0:T(8,128)} %get-tuple-element.27.fxr_ref, ...), custom_call_target="tpu_custom_call" | custom-call | tf_op jit(solution)/shard_map/pallas_call | solution.py:170
  62.4 3.6 %copy.69 = f32[2,16,8,512]{1,3,2,0:T(8,128)} copy(f32[2,16,8,512]{3,2,1,0:T(8,128)} %shard_map.80) | data formatting | bytes 1048576 | tf_op jit(solution)/shard_map/pallas_call | solution.py:170
  66.0 5.8 %reduce_sum.54 = f32[2,16,4,256]{1,3,2,0:T(8,128)S(1)} reduce(f32[2,16,4,2,256,2]{1,5,4,3,2,0:T(2,128)} %bitcast.67, f32[]{:T(128)} %constant.24.clone.1), dimensions={3,5}, to_apply=%region_0.0 | reduce | flops 98304 | bytes 655364 | tf_op jit(solution)/shard_map/reduce_sum | solution.py:59
  75.2 3.4 %collective-permute-start.3 = (f32[2,16,4,256]{3,2,1,0:T(4,128)S(1)}, f32[2,16,4,256]{3,2,1,0:T(4,128)S(1)}, u32[]{:S(2)}, u32[]{:S(2)}) collective-permute-start(f32[2,16,4,256]{3,2,1,0:T(4,128)S(1)} %broadcast_multiply_fusion), channel_id=1, source_target_pairs={{1,0},{2,1},{3,2},{4,3},{5,4},{6,5},{7,6},{8,7},{9,8},{10,9},{11,1... | collective-permute-start | bytes 393224 | tf_op jit(solution)/shard_map/ppermute | solution.py:29
  90.9 3.3 %shard_map.81 = (f32[2,16,12,256]{3,2,1,0:T(8,128)}, f32[2,16,12,256]{3,2,1,0:T(8,128)}, f32[2,16,12,256]{3,2,1,0:T(8,128)}, f32[2,16,12,256]{3,2,1,0:T(8,128)},...) custom-call(f32[16,14,256]{2,1,0:T(8,128)} %pad_dynamic-slice_fusion., ...), custom_call_target="tpu_custom_call" | custom-call | tf_op jit(solution)/shard_map/pallas_call | solution.py:245
  94.8 3.1 %shard_map.82.w_ref = f32[2,16,12,256]{3,2,1,0:T(8,128)} custom-call(f32[2,16,12,256]{3,2,1,0:T(8,128)} %pad_maximum_fusion.5.w_ref.b_ref, f32[2,16,12,256]{3,2,1,0:T(8,128)} %pad_maximum_fusion.5.w_ref.b_ref, f32[2,16,12,256]{3,2,1,0:T(8,128)} %get-tuple-element.34.fxl_ref, f32[2,16,12,256]{3,2,1,0:T(8,128)} %get-tuple-element.35.fxr_ref, ...), custom_call_target="tpu_custom_call" | custom-call | tf_op jit(solution)/shard_map/pallas_call | solution.py:170
  98.6 3.6 %shard_map.83.w_ref = f32[2,16,10,256]{3,2,1,0:T(8,128)} custom-call(f32[2,16,12,256]{3,2,1,0:T(8,128)} %shard_map.82.w_ref, f32[2,16,12,256]{3,2,1,0:T(8,128)} %pad_maximum_fusion.5.w_ref.b_ref, f32[2,16,12,256]{3,2,1,0:T(8,128)} %get-tuple-element.34.fxl_ref, f32[2,16,12,256]{3,2,1,0:T(8,128)} %get-tuple-element.35.fxr_ref, ...), custom_call_target="tpu_custom_call" | custom-call | tf_op jit(solution)/shard_map/pallas_call | solution.py:170
  108.2 4.0 %collective-permute-start.10 = (f32[2,16,2,128]{3,2,1,0:T(2,128)S(1)}, f32[2,16,2,128]{3,2,1,0:T(2,128)S(1)}, u32[]{:S(2)}, u32[]{:S(2)}) collective-permute-start(f32[2,16,2,128]{3,2,1,0:T(2,128)S(1)} %broadcast_multiply_fusion.2), channel_id=1, source_target_pairs={{3,0},{4,1},{5,2},{6,3},{7,4},{8,5},{9,6},{10,7},{11,8},{12,9},{13... | collective-permute-start | bytes 98312 | tf_op jit(solution)/shard_map/ppermute | solution.py:340
  114.1 3.9 %collective-permute-start.4 = (f32[2,16,2,128]{3,2,1,0:T(2,128)S(1)}, f32[2,16,2,128]{3,2,1,0:T(2,128)S(1)}, u32[]{:S(2)}, u32[]{:S(2)}) collective-permute-start(f32[2,16,2,128]{3,2,1,0:T(2,128)S(1)} %broadcast_multiply_fusion.2), channel_id=1, source_target_pairs={{0,4},{1,5},{2,6},{3,7},{4,8},{5,9},{6,10},{7,11},{8,12},{9,13},{1... | collective-permute-start | bytes 98312 | tf_op jit(solution)/shard_map/ppermute | solution.py:339
  120.2 3.8 %collective-permute-start.6 = (f32[2,16,2,128]{3,2,1,0:T(2,128)S(1)}, f32[2,16,2,128]{3,2,1,0:T(2,128)S(1)}, u32[]{:S(2)}, u32[]{:S(2)}) collective-permute-start(f32[2,16,2,128]{3,2,1,0:T(2,128)S(1)} %broadcast_multiply_fusion.2), channel_id=1, source_target_pairs={{0,2},{1,3},{2,4},{3,5},{4,6},{5,7},{6,8},{7,9},{8,10},{9,11},{10,... | collective-permute-start | bytes 98312 | tf_op jit(solution)/shard_map/ppermute | solution.py:339
  127.6 4.0 %collective-permute-start.8 = (f32[2,16,2,128]{3,2,1,0:T(2,128)S(1)}, f32[2,16,2,128]{3,2,1,0:T(2,128)S(1)}, u32[]{:S(2)}, u32[]{:S(2)}) collective-permute-start(f32[2,16,2,128]{3,2,1,0:T(2,128)S(1)} %broadcast_multiply_fusion.2), channel_id=1, source_target_pairs={{1,0},{2,1},{3,2},{4,3},{5,4},{6,5},{7,6},{8,7},{9,8},{10,9},{11,1... | collective-permute-start | bytes 98312 | tf_op jit(solution)/shard_map/ppermute | solution.py:340
  169.5 3.1 %slice.170 = f32[2,16,10,256]{2,1,3,0:T(8,128)} slice(f32[2,16,16,256]{2,1,3,0:T(8,128)S(1)} %bitcast.68), slice={[0:2], [0:16], [3:13], [0:256]} | slice | bytes 655360 | tf_op jit(solution)/shard_map/slice | solution.py:404
  172.7 3.6 %copy.90 = f32[2,16,10,256]{3,2,1,0:T(8,128)S(1)} copy(f32[2,16,10,256]{2,1,3,0:T(8,128)} %slice.170) | data formatting | bytes 655360
  177.8 3.4 %shard_map.92.w_ref = f32[2,16,8,256]{3,2,1,0:T(8,128)} custom-call(f32[2,16,10,256]{3,2,1,0:T(8,128)} %add.186.w_ref, f32[2,16,12,256]{3,2,1,0:T(8,128)} %pad_maximum_fusion.5.w_ref.b_ref, f32[2,16,12,256]{3,2,1,0:T(8,128)} %get-tuple-element.34.fxl_ref, f32[2,16,12,256]{3,2,1,0:T(8,128)} %get-tuple-element.35.fxr_ref, ...), custom_call_target="tpu_custom_call" | custom-call | tf_op jit(solution)/shard_map/pallas_call | solution.py:170
  181.9 3.3 %shard_map.93 = f32[2,16,6,256]{3,2,1,0:T(8,128)} custom-call(f32[2,16,8,256]{3,2,1,0:T(8,128)} %shard_map.92.w_ref, f32[2,16,12,256]{3,2,1,0:T(8,128)} %pad_maximum_fusion.5.w_ref.b_ref, f32[2,16,12,256]{3,2,1,0:T(8,128)} %get-tuple-element.34.fxl_ref, f32[2,16,12,256]{3,2,1,0:T(8,128)} %get-tuple-element.35.fxr_ref, ...), custom_call_target="tpu_custom_call" | custom-call | tf_op jit(solution)/shard_map/pallas_call | solution.py:170
  187.3 4.5 %broadcast_in_dim.83 = f32[2,16,12,256,2]{1,4,3,2,0:T(2,128)} broadcast(f32[2,16,12,256]{1,3,2,0:T(8,128)S(1)} %copy.87), dimensions={0,1,2,3} | broadcast | bytes 1179648 | tf_op jit(solution)/shard_map/broadcast_in_dim | solution.py:310
  191.8 5.0 %copy.88 = f32[2,16,12,512]{3,2,1,0:T(8,128)S(1)} copy(f32[2,16,12,512]{1,3,2,0:T(8,128)} %bitcast.64) | data formatting | bytes 1572864 | tf_op jit(solution)/shard_map/reshape | solution.py:310
  198.6 6.0 %shard_map.94.w_ref = f32[2,16,10,512]{3,2,1,0:T(8,128)} custom-call(f32[2,16,12,512]{3,2,1,0:T(8,128)} %add.191.w_ref, f32[2,16,16,512]{3,2,1,0:T(8,128)} %get-tuple-element.66.b_ref, f32[2,16,14,512]{3,2,1,0:T(8,128)} %get-tuple-element.26.fxl_ref, f32[2,16,14,512]{3,2,1,0:T(8,128)} %get-tuple-element.27.fxr_ref, ...), custom_call_target="tpu_custom_call" | custom-call | tf_op jit(solution)/shard_map/pallas_call | solution.py:170
  204.6 5.6 %shard_map.95 = f32[2,16,8,512]{3,2,1,0:T(8,128)} custom-call(f32[2,16,10,512]{3,2,1,0:T(8,128)} %shard_map.94.w_ref, f32[2,16,16,512]{3,2,1,0:T(8,128)} %get-tuple-element.66.b_ref, f32[2,16,14,512]{3,2,1,0:T(8,128)} %get-tuple-element.26.fxl_ref, f32[2,16,14,512]{3,2,1,0:T(8,128)} %get-tuple-element.27.fxr_ref, ...), custom_call_target="tpu_custom_call" | custom-call | tf_op jit(solution)/shard_map/pallas_call | solution.py:170
  (159 shorter events, 101.0 us)
Async XLA Ops:
  7.2 2.4 %copy-start.3 = (f32[2,16,8,512]{3,2,1,0:T(8,128)S(1)}, f32[2,16,8,512]{3,2,1,0:T(8,128)}, u32[]{:S(2)}) copy-start(f32[2,16,8,512]{3,2,1,0:T(8,128)} %param.6) | copy-start | bytes 1572868
  7.2 2.6 %copy-start.2 = (f32[16,8,512]{2,1,0:T(8,128)S(1)}, f32[16,8,512]{2,1,0:T(8,128)}, u32[]{:S(2)}) copy-start(f32[16,8,512]{2,1,0:T(8,128)} %param.8) | copy-start | bytes 786436
  7.2 74.8 %all-gather.4.cloned.1.call-start = ((), (), s32[]{:S(2)}) async-start(), calls=%async_computation | async-start | bytes 1566720 | tf_op jit(solution)/shard_map/all_gather | solution.py:356
  10.7 18.5 %collective-permute-start = (f32[167936]{0:T(1024)}, f32[167936]{0:T(1024)}, u32[]{:S(2)}, u32[]{:S(2)}) collective-permute-start(f32[167936]{0:T(1024)} %pad_maximum_fusion.2), channel_id=1, source_target_pairs={{0,1},{1,2},{2,3},{3,4},{4,5},{5,6},{6,7},{7,8},{8,9},{9,10},{10,1... | collective-permute-start | bytes 2015240 | tf_op jit(solution)/shard_map/ppermute | solution.py:42
  13.8 16.2 %collective-permute-start.1 = (f32[167936]{0:T(1024)}, f32[167936]{0:T(1024)}, u32[]{:S(2)}, u32[]{:S(2)}) collective-permute-start(f32[167936]{0:T(1024)} %pad_maximum_fusion.3), channel_id=1, source_target_pairs={{1,0},{2,1},{3,2},{4,3},{5,4},{6,5},{7,6},{8,7},{9,8},{10,9},{11,1... | collective-permute-start | bytes 2015240 | tf_op jit(solution)/shard_map/ppermute | solution.py:43
  33.8 8.1 %copy-start.4 = (f32[2,16,8,512]{3,2,1,0:T(8,128)S(1)}, f32[2,16,8,512]{3,2,1,0:T(8,128)}, u32[]{:S(2)}) copy-start(f32[2,16,8,512]{3,2,1,0:T(8,128)} %param.6) | copy-start | bytes 1572868
  33.8 8.1 %copy-start.5 = (f32[2,16,8,512]{3,2,1,0:T(8,128)S(1)}, f32[2,16,8,512]{3,2,1,0:T(8,128)}, u32[]{:S(2)}) copy-start(f32[2,16,8,512]{3,2,1,0:T(8,128)} %param.7) | copy-start | bytes 1572868
  72.1 7.2 %collective-permute-start.2 = (f32[2,16,4,256]{3,2,1,0:T(4,128)S(1)}, f32[2,16,4,256]{3,2,1,0:T(4,128)S(1)}, u32[]{:S(2)}, u32[]{:S(2)}) collective-permute-start(f32[2,16,4,256]{3,2,1,0:T(4,128)S(1)} %broadcast_multiply_fusion), channel_id=1, source_target_pairs={{0,1},{1,2},{2,3},{3,4},{4,5},{5,6},{6,7},{7,8},{8,9},{9,10},{10,1... | collective-permute-start | bytes 393224 | tf_op jit(solution)/shard_map/ppermute | solution.py:27
  75.2 5.9 %collective-permute-start.3 = (f32[2,16,4,256]{3,2,1,0:T(4,128)S(1)}, f32[2,16,4,256]{3,2,1,0:T(4,128)S(1)}, u32[]{:S(2)}, u32[]{:S(2)}) collective-permute-start(f32[2,16,4,256]{3,2,1,0:T(4,128)S(1)} %broadcast_multiply_fusion), channel_id=1, source_target_pairs={{1,0},{2,1},{3,2},{4,3},{5,4},{6,5},{7,6},{8,7},{9,8},{10,9},{11,1... | collective-permute-start | bytes 393224 | tf_op jit(solution)/shard_map/ppermute | solution.py:29
  108.2 16.9 %collective-permute-start.10 = (f32[2,16,2,128]{3,2,1,0:T(2,128)S(1)}, f32[2,16,2,128]{3,2,1,0:T(2,128)S(1)}, u32[]{:S(2)}, u32[]{:S(2)}) collective-permute-start(f32[2,16,2,128]{3,2,1,0:T(2,128)S(1)} %broadcast_multiply_fusion.2), channel_id=1, source_target_pairs={{3,0},{4,1},{5,2},{6,3},{7,4},{8,5},{9,6},{10,7},{11,8},{12,9},{13... | collective-permute-start | bytes 98312 | tf_op jit(solution)/shard_map/ppermute | solution.py:340
  112.2 15.4 %collective-permute-start.11 = (f32[2,16,2,128]{3,2,1,0:T(2,128)S(1)}, f32[2,16,2,128]{3,2,1,0:T(2,128)S(1)}, u32[]{:S(2)}, u32[]{:S(2)}) collective-permute-start(f32[2,16,2,128]{3,2,1,0:T(2,128)S(1)} %broadcast_multiply_fusion.2), channel_id=1, source_target_pairs={{4,0},{5,1},{6,2},{7,3},{8,4},{9,5},{10,6},{11,7},{12,8},{13,9},{1... | collective-permute-start | bytes 98312 | tf_op jit(solution)/shard_map/ppermute | solution.py:340
  114.1 17.5 %collective-permute-start.4 = (f32[2,16,2,128]{3,2,1,0:T(2,128)S(1)}, f32[2,16,2,128]{3,2,1,0:T(2,128)S(1)}, u32[]{:S(2)}, u32[]{:S(2)}) collective-permute-start(f32[2,16,2,128]{3,2,1,0:T(2,128)S(1)} %broadcast_multiply_fusion.2), channel_id=1, source_target_pairs={{0,4},{1,5},{2,6},{3,7},{4,8},{5,9},{6,10},{7,11},{8,12},{9,13},{1... | collective-permute-start | bytes 98312 | tf_op jit(solution)/shard_map/ppermute | solution.py:339
  118.1 19.0 %collective-permute-start.5 = (f32[2,16,2,128]{3,2,1,0:T(2,128)S(1)}, f32[2,16,2,128]{3,2,1,0:T(2,128)S(1)}, u32[]{:S(2)}, u32[]{:S(2)}) collective-permute-start(f32[2,16,2,128]{3,2,1,0:T(2,128)S(1)} %broadcast_multiply_fusion.2), channel_id=1, source_target_pairs={{0,3},{1,4},{2,5},{3,6},{4,7},{5,8},{6,9},{7,10},{8,11},{9,12},{10... | collective-permute-start | bytes 98312 | tf_op jit(solution)/shard_map/ppermute | solution.py:339
  120.2 16.8 %collective-permute-start.6 = (f32[2,16,2,128]{3,2,1,0:T(2,128)S(1)}, f32[2,16,2,128]{3,2,1,0:T(2,128)S(1)}, u32[]{:S(2)}, u32[]{:S(2)}) collective-permute-start(f32[2,16,2,128]{3,2,1,0:T(2,128)S(1)} %broadcast_multiply_fusion.2), channel_id=1, source_target_pairs={{0,2},{1,3},{2,4},{3,5},{4,6},{5,7},{6,8},{7,9},{8,10},{9,11},{10,... | collective-permute-start | bytes 98312 | tf_op jit(solution)/shard_map/ppermute | solution.py:339
  125.2 11.9 %collective-permute-start.7 = (f32[2,16,2,128]{3,2,1,0:T(2,128)S(1)}, f32[2,16,2,128]{3,2,1,0:T(2,128)S(1)}, u32[]{:S(2)}, u32[]{:S(2)}) collective-permute-start(f32[2,16,2,128]{3,2,1,0:T(2,128)S(1)} %broadcast_multiply_fusion.2), channel_id=1, source_target_pairs={{0,1},{1,2},{2,3},{3,4},{4,5},{5,6},{6,7},{7,8},{8,9},{9,10},{10,1... | collective-permute-start | bytes 98312 | tf_op jit(solution)/shard_map/ppermute | solution.py:339
  127.6 9.4 %collective-permute-start.8 = (f32[2,16,2,128]{3,2,1,0:T(2,128)S(1)}, f32[2,16,2,128]{3,2,1,0:T(2,128)S(1)}, u32[]{:S(2)}, u32[]{:S(2)}) collective-permute-start(f32[2,16,2,128]{3,2,1,0:T(2,128)S(1)} %broadcast_multiply_fusion.2), channel_id=1, source_target_pairs={{1,0},{2,1},{3,2},{4,3},{5,4},{6,5},{7,6},{8,7},{9,8},{10,9},{11,1... | collective-permute-start | bytes 98312 | tf_op jit(solution)/shard_map/ppermute | solution.py:340
  131.7 5.8 %collective-permute-start.9 = (f32[2,16,2,128]{3,2,1,0:T(2,128)S(1)}, f32[2,16,2,128]{3,2,1,0:T(2,128)S(1)}, u32[]{:S(2)}, u32[]{:S(2)}) collective-permute-start(f32[2,16,2,128]{3,2,1,0:T(2,128)S(1)} %broadcast_multiply_fusion.2), channel_id=1, source_target_pairs={{2,0},{3,1},{4,2},{5,3},{6,4},{7,5},{8,6},{9,7},{10,8},{11,9},{12,... | collective-permute-start | bytes 98312 | tf_op jit(solution)/shard_map/ppermute | solution.py:340
  172.6 3.6 %copy-start.1 = (f32[2,16,10,256]{3,2,1,0:T(8,128)S(1)}, f32[2,16,10,256]{3,2,1,0:T(8,128)}, u32[]{:S(2)}) copy-start(f32[2,16,10,256]{3,2,1,0:T(8,128)} %shard_map.83.w_ref) | copy-start | bytes 983044
  191.8 5.0 %copy-start = (f32[2,16,12,512]{3,2,1,0:T(8,128)S(1)}, f32[2,16,12,512]{3,2,1,0:T(8,128)}, u32[]{:S(2)}) copy-start(f32[2,16,12,512]{3,2,1,0:T(8,128)} %shard_map.79.w_ref) | copy-start | bytes 2359300
  204.6 5.6 %copy-start.6 = (f32[2,8,512]{2,1,0:T(8,128)S(1)}, f32[2,8,512]{2,1,0:T(8,128)}, u32[]{:S(2)}) copy-start(f32[2,8,512]{2,1,0:T(8,128)} %param.11) | copy-start | bytes 98308
Sparse Core Ops, SparseCore 0:
  29.2 38.5 all-gather.3
where the time goes:
time: 220 us; the launch traced here: 218 us
  Pallas kernels  73.7 us (34%)
  local copies, waits for them, and re-layouts  68.2 us (31%)
  starting transfers between devices  37.2 us (17%)
  other arithmetic  21.6 us (10%)
  between operations  14.8 us (7%)
  waiting for transfers between devices  2.91 us (1%)
    pallas_call x16, Pallas kernels, kernel_sweep(): pl.pallas_call(body, grid=(parts,), in_specs=specs, out_specs=pl.BlockSpe...  62.7 us
    ppermute x4, starting transfers between devices, nearby(): lax.ppermute(cells, 'gx', [(i, i + step) for i in range(count - step)])  12.3 us
    ppermute x4, starting transfers between devices, nearby(): lax.ppermute(cells, 'gx', [(i + step, i) for i in range(count - step)])  12 us
    reduce_sum x6, other arithmetic, block_mean(): return shaped.mean(axis=(-3, -1))  11.1 us
    pallas_call x3, Pallas kernels, kernel_operator(): pl.pallas_call(body, grid=(2,), in_specs=[whole(eta_level), whole(react_l...  11 us
    pad x5, local copies, waits for them, and re-layouts, pad_rim(): return jnp.pad(field, ((0, 0), (0, 0), (1, 1), (0, 0)))  8.89 us
    reshape x3, local copies, waits for them, and re-layouts, prolong(): return jnp.repeat(jnp.repeat(field, 2, axis=2), 2, axis=3)  6.94 us
    unnamed x30, local copies, waits for them, and re-layouts  6.92 us
  transfers between devices with their start and end apart: 13, of which 3 were waited for; matrix products, arithmetic and copies ran while one was open for 16% of the time, Pallas kernels for 11%

commit v1 on v0

--- a/solution.py
+++ b/solution.py
@@ -99,6 +99,23 @@
 
 def sweep_kernel(w_ref, b_ref, fxl_ref, fxr_ref, fyl_ref, fyr_ref, fz_ref, re_ref, inv_ref, rat_ref, mask_ref, out_ref,
                  *, rows, cut_w, cut_b, cut_op, mode):
+    relax(w_ref, b_ref, (fxl_ref, fxr_ref, fyl_ref, fyr_ref, fz_ref, re_ref, inv_ref, rat_ref), mask_ref, out_ref,
+          rows=rows, cut_w=cut_w, cut_b=cut_b, cut_op=cut_op, mode=mode)
+
+
+def coarse_kernel(b_ref, fxl_ref, fxr_ref, fyl_ref, fyr_ref, fz_ref, re_ref, inv_ref, rat_ref, mask_ref, out_ref, w_ref,
+                  *, rows, turns):
+    lanes = (fxl_ref, fxr_ref, fyl_ref, fyr_ref, fz_ref, re_ref, inv_ref, rat_ref)
+    w_ref[...] = jnp.zeros(w_ref.shape, jnp.float32)
+    for turn in range(turns):
+        relax(w_ref, b_ref, lanes, mask_ref, out_ref, rows=rows, cut_w=7, cut_b=0, cut_op=0, mode="sweep")
+        if turn < turns - 1:
+            for k in range(out_ref.shape[1]):
+                w_ref[0, k, pl.ds(8, rows), :] = out_ref[0, k]
+
+
+def relax(w_ref, b_ref, lanes, mask_ref, out_ref, *, rows, cut_w, cut_b, cut_op, mode):
+    fxl_ref, fxr_ref, fyl_ref, fyr_ref, fz_ref, re_ref, inv_ref, rat_ref = lanes
     layers = out_ref.shape[1]
     cols = out_ref.shape[3]
     lane = lax.broadcasted_iota(jnp.int32, (rows, cols), 1)
@@ -252,6 +269,25 @@
     )
 
 
+def kernel_coarse(target, lanes, mask, turns):
+    parts, layers, rows, cols = target.shape
+    fxl, fxr, fyl, fyr, fz, re, inv, rat = lanes
+    per_part = lambda a: pl.BlockSpec((1,) + a.shape[1:], lambda c: (c,) + (0,) * (a.ndim - 1))
+    whole = lambda a: pl.BlockSpec(a.shape, lambda c: (0,) * a.ndim)
+    operands = [target, fxl, fxr, fyl, fyr, fz, re, inv, rat, mask]
+    specs = [per_part(target), per_part(fxl), per_part(fxr), per_part(fyl), per_part(fyr),
+             whole(fz), whole(re), per_part(inv), per_part(rat), whole(mask)]
+    body = functools.partial(coarse_kernel, rows=rows, turns=turns)
+    return pl.pallas_call(
+        body,
+        grid=(parts,),
+        in_specs=specs,
+        out_specs=pl.BlockSpec((1, layers, rows, cols), lambda c: (c, 0, 0, 0)),
+        out_shape=jax.ShapeDtypeStruct((parts, layers, rows, cols), jnp.float32),
+        scratch_shapes=[pltpu.VMEM((1, layers, rows + 16, cols), jnp.float32)],
+    )(*operands)
+
+
 def rows_inside(cells, halo, extent, cols):
     return jnp.broadcast_to(inside(cells, halo, extent)[0, 0], (extent, cols)).astype(jnp.float32)
 
@@ -394,9 +430,7 @@
     op_2 = kernel_operator(eta_2_near, react_2_near, 2)
     extent = quarter + 2 * span
     coarse_mask = rows_inside(quarter, span, extent, narrow)
-    coarse = kernel_sweep(coarse_rhs_near, coarse_rhs_near, op_2, 0, 0, coarse_mask, "zero", 0, extent)
-    for turn in range(COARSE_SWEEPS - 1):
-        coarse = kernel_sweep(pad_rim(coarse), coarse_rhs_near, op_2, 0, 0, coarse_mask)
+    coarse = kernel_coarse(coarse_rhs_near, op_2, coarse_mask, COARSE_SWEEPS)
     coarse_near = coarse[:, :, span - reach : span + quarter + reach]
 
     lift = prolong(coarse_near)

time: 220 us -> 198 us (0.900)
  Pallas kernels: 73.7 us -> 61.4 us
  local copies, waits for them, and re-layouts: 68.2 us -> 59.3 us
    pallas_call x16 -> x10, Pallas kernels: 62.7 us -> 44.7 us  [kernel_sweep(): pl.pallas_call(body, grid=(parts,), in_specs=specs, out_specs=pl.BlockSpe...]
    pad x5 -> x0, local copies, waits for them, and re-layouts: 8.89 us -> none  [pad_rim(): return jnp.pad(field, ((0, 0), (0, 0), (1, 1), (0, 0)))]
    pallas_call x0 -> x1, Pallas kernels: none -> 5.58 us  [kernel_coarse(): pl.pallas_call(body, grid=(parts,), in_specs=specs, out_specs=pl.BlockSpe...]
  transfers between devices with their start and end apart: 13 -> 13, of which waited for: 3 -> 3; matrix products, arithmetic and copies ran while one was open for 16% -> 18% of each run, Pallas kernels for 11% -> 12%
where the time goes in v1:
time: 198 us; the launch traced here: 197 us
  Pallas kernels  61.4 us (31%)
  local copies, waits for them, and re-layouts  59.3 us (30%)
  starting transfers between devices  37.2 us (19%)
  other arithmetic  21.6 us (11%)
  between operations  14.8 us (7%)
  waiting for transfers between devices  2.9 us (1%)
    pallas_call x10, Pallas kernels, kernel_sweep(): pl.pallas_call(body, grid=(parts,), in_specs=specs, out_specs=pl.BlockSpe...  44.7 us
    ppermute x4, starting transfers between devices, nearby(): lax.ppermute(cells, 'gx', [(i, i + step) for i in range(count - step)])  12.3 us
    ppermute x4, starting transfers between devices, nearby(): lax.ppermute(cells, 'gx', [(i + step, i) for i in range(count - step)])  12 us
    reduce_sum x6, other arithmetic, block_mean(): return shaped.mean(axis=(-3, -1))  11.1 us
    pallas_call x3, Pallas kernels, kernel_operator(): pl.pallas_call(body, grid=(2,), in_specs=[whole(eta_level), whole(react_l...  11.1 us
    reshape x3, local copies, waits for them, and re-layouts, prolong(): return jnp.repeat(jnp.repeat(field, 2, axis=2), 2, axis=3)  6.94 us
    unnamed x30, local copies, waits for them, and re-layouts  6.92 us
    broadcast_in_dim x10, local copies, waits for them, and re-layouts, rows_inside(): jnp.broadcast_to(inside(cells, halo, extent)[0, 0], (extent, cols))  6.7 us
  transfers between devices with their start and end apart: 13, of which 3 were waited for; matrix products, arithmetic and copies ran while one was open for 18% of the time, Pallas kernels for 12%

profile of v1, /device:TPU:10, one launch (start us, length us, event | category | flops | bytes accessed | tf_op | source)
XLA Modules:
  0.0 197.2 jit_solution(7592421582906637838)
XLA Ops:
  13.8 4.5 %collective-permute-start.1 = (f32[167936]{0:T(1024)}, f32[167936]{0:T(1024)}, u32[]{:S(2)}, u32[]{:S(2)}) collective-permute-start(f32[167936]{0:T(1024)} %pad_maximum_fusion.3), channel_id=1, source_target_pairs={{1,0},{2,1},{3,2},{4,3},{5,4},{6,5},{7,6},{8,7},{9,8},{10,9},{11,1... | collective-permute-start | bytes 2015240 | tf_op jit(solution)/shard_map/ppermute | solution.py:43
  18.3 3.4 %reshape.240 = f32[2,4,2,256,2]{4,3,2,1,0:T(8,128)} reshape(f32[2,8,512]{2,1,0:T(8,128)S(1)} %slice.163) | data formatting | bytes 65536 | tf_op jit(solution)/shard_map/reshape | solution.py:58
  36.8 5.1 %shard_map.77 = (f32[2,16,14,512]{3,2,1,0:T(8,128)}, f32[2,16,14,512]{3,2,1,0:T(8,128)}, f32[2,16,14,512]{3,2,1,0:T(8,128)}, f32[2,16,14,512]{3,2,1,0:T(8,128)},...) custom-call(f32[16,16,512]{2,1,0:T(8,128)} %pad_maximum_fusion.4.eta_, ...), custom_call_target="tpu_custom_call" | custom-call | tf_op jit(solution)/shard_map/pallas_call | solution.py:262
  44.4 5.8 %shard_map.78.w_ref = f32[2,16,14,512]{3,2,1,0:T(8,128)} custom-call(f32[2,16,16,512]{3,2,1,0:T(8,128)} %get-tuple-element.65.w_ref, f32[2,16,16,512]{3,2,1,0:T(8,128)} %get-tuple-element.66.b_ref, f32[2,16,14,512]{3,2,1,0:T(8,128)} %get-tuple-element.26.fxl_ref, f32[2,16,14,512]{3,2,1,0:T(8,128)} %get-tuple-element.27.fxr_ref, ...), custom_call_target="tpu_custom_call" | custom-call | tf_op jit(solution)/shard_map/pallas_call | solution.py:187
  50.8 5.8 %shard_map.79.w_ref = f32[2,16,12,512]{3,2,1,0:T(8,128)} custom-call(f32[2,16,14,512]{3,2,1,0:T(8,128)} %shard_map.78.w_ref, f32[2,16,16,512]{3,2,1,0:T(8,128)} %get-tuple-element.66.b_ref, f32[2,16,14,512]{3,2,1,0:T(8,128)} %get-tuple-element.26.fxl_ref, f32[2,16,14,512]{3,2,1,0:T(8,128)} %get-tuple-element.27.fxr_ref, ...), custom_call_target="tpu_custom_call" | custom-call | tf_op jit(solution)/shard_map/pallas_call | solution.py:187
  57.3 5.1 %shard_map.80 = f32[2,16,8,512]{3,2,1,0:T(8,128)} custom-call(f32[2,16,12,512]{3,2,1,0:T(8,128)} %shard_map.79.w_ref, f32[2,16,16,512]{3,2,1,0:T(8,128)} %get-tuple-element.66.b_ref, f32[2,16,14,512]{3,2,1,0:T(8,128)} %get-tuple-element.26.fxl_ref, f32[2,16,14,512]{3,2,1,0:T(8,128)} %get-tuple-element.27.fxr_ref, ...), custom_call_target="tpu_custom_call" | custom-call | tf_op jit(solution)/shard_map/pallas_call | solution.py:187
  62.4 3.6 %copy.69 = f32[2,16,8,512]{1,3,2,0:T(8,128)} copy(f32[2,16,8,512]{3,2,1,0:T(8,128)} %shard_map.80) | data formatting | bytes 1048576 | tf_op jit(solution)/shard_map/pallas_call | solution.py:187
  66.0 5.8 %reduce_sum.54 = f32[2,16,4,256]{1,3,2,0:T(8,128)S(1)} reduce(f32[2,16,4,2,256,2]{1,5,4,3,2,0:T(2,128)} %bitcast.67, f32[]{:T(128)} %constant.24.clone.1), dimensions={3,5}, to_apply=%region_0.0 | reduce | flops 98304 | bytes 655364 | tf_op jit(solution)/shard_map/reduce_sum | solution.py:59
  75.2 3.4 %collective-permute-start.3 = (f32[2,16,4,256]{3,2,1,0:T(4,128)S(1)}, f32[2,16,4,256]{3,2,1,0:T(4,128)S(1)}, u32[]{:S(2)}, u32[]{:S(2)}) collective-permute-start(f32[2,16,4,256]{3,2,1,0:T(4,128)S(1)} %broadcast_multiply_fusion), channel_id=1, source_target_pairs={{1,0},{2,1},{3,2},{4,3},{5,4},{6,5},{7,6},{8,7},{9,8},{10,9},{11,1... | collective-permute-start | bytes 393224 | tf_op jit(solution)/shard_map/ppermute | solution.py:29
  90.9 3.3 %shard_map.81 = (f32[2,16,12,256]{3,2,1,0:T(8,128)}, f32[2,16,12,256]{3,2,1,0:T(8,128)}, f32[2,16,12,256]{3,2,1,0:T(8,128)}, f32[2,16,12,256]{3,2,1,0:T(8,128)},...) custom-call(f32[16,14,256]{2,1,0:T(8,128)} %pad_dynamic-slice_fusion., ...), custom_call_target="tpu_custom_call" | custom-call | tf_op jit(solution)/shard_map/pallas_call | solution.py:262
  94.8 3.1 %shard_map.82.w_ref = f32[2,16,12,256]{3,2,1,0:T(8,128)} custom-call(f32[2,16,12,256]{3,2,1,0:T(8,128)} %pad_maximum_fusion.5.w_ref.b_ref, f32[2,16,12,256]{3,2,1,0:T(8,128)} %pad_maximum_fusion.5.w_ref.b_ref, f32[2,16,12,256]{3,2,1,0:T(8,128)} %get-tuple-element.34.fxl_ref, f32[2,16,12,256]{3,2,1,0:T(8,128)} %get-tuple-element.35.fxr_ref, ...), custom_call_target="tpu_custom_call" | custom-call | tf_op jit(solution)/shard_map/pallas_call | solution.py:187
  98.6 3.6 %shard_map.83.w_ref = f32[2,16,10,256]{3,2,1,0:T(8,128)} custom-call(f32[2,16,12,256]{3,2,1,0:T(8,128)} %shard_map.82.w_ref, f32[2,16,12,256]{3,2,1,0:T(8,128)} %pad_maximum_fusion.5.w_ref.b_ref, f32[2,16,12,256]{3,2,1,0:T(8,128)} %get-tuple-element.34.fxl_ref, f32[2,16,12,256]{3,2,1,0:T(8,128)} %get-tuple-element.35.fxr_ref, ...), custom_call_target="tpu_custom_call" | custom-call | tf_op jit(solution)/shard_map/pallas_call | solution.py:187
  108.2 4.0 %collective-permute-start.10 = (f32[2,16,2,128]{3,2,1,0:T(2,128)S(1)}, f32[2,16,2,128]{3,2,1,0:T(2,128)S(1)}, u32[]{:S(2)}, u32[]{:S(2)}) collective-permute-start(f32[2,16,2,128]{3,2,1,0:T(2,128)S(1)} %broadcast_multiply_fusion.2), channel_id=1, source_target_pairs={{3,0},{4,1},{5,2},{6,3},{7,4},{8,5},{9,6},{10,7},{11,8},{12,9},{13... | collective-permute-start | bytes 98312 | tf_op jit(solution)/shard_map/ppermute | solution.py:376
  114.1 3.9 %collective-permute-start.4 = (f32[2,16,2,128]{3,2,1,0:T(2,128)S(1)}, f32[2,16,2,128]{3,2,1,0:T(2,128)S(1)}, u32[]{:S(2)}, u32[]{:S(2)}) collective-permute-start(f32[2,16,2,128]{3,2,1,0:T(2,128)S(1)} %broadcast_multiply_fusion.2), channel_id=1, source_target_pairs={{0,4},{1,5},{2,6},{3,7},{4,8},{5,9},{6,10},{7,11},{8,12},{9,13},{1... | collective-permute-start | bytes 98312 | tf_op jit(solution)/shard_map/ppermute | solution.py:375
  120.2 3.8 %collective-permute-start.6 = (f32[2,16,2,128]{3,2,1,0:T(2,128)S(1)}, f32[2,16,2,128]{3,2,1,0:T(2,128)S(1)}, u32[]{:S(2)}, u32[]{:S(2)}) collective-permute-start(f32[2,16,2,128]{3,2,1,0:T(2,128)S(1)} %broadcast_multiply_fusion.2), channel_id=1, source_target_pairs={{0,2},{1,3},{2,4},{3,5},{4,6},{5,7},{6,8},{7,9},{8,10},{9,11},{10,... | collective-permute-start | bytes 98312 | tf_op jit(solution)/shard_map/ppermute | solution.py:375
  127.6 4.0 %collective-permute-start.8 = (f32[2,16,2,128]{3,2,1,0:T(2,128)S(1)}, f32[2,16,2,128]{3,2,1,0:T(2,128)S(1)}, u32[]{:S(2)}, u32[]{:S(2)}) collective-permute-start(f32[2,16,2,128]{3,2,1,0:T(2,128)S(1)} %broadcast_multiply_fusion.2), channel_id=1, source_target_pairs={{1,0},{2,1},{3,2},{4,3},{5,4},{6,5},{7,6},{8,7},{9,8},{10,9},{11,1... | collective-permute-start | bytes 98312 | tf_op jit(solution)/shard_map/ppermute | solution.py:376
  140.4 5.6 %shard_map.86 = f32[2,16,18,128]{3,2,1,0:T(8,128)} custom-call(f32[2,16,18,128]{3,2,1,0:T(8,128)} %concatenate.35.b_ref, f32[2,16,18,128]{3,2,1,0:T(8,128)} %get-tuple-element.42.fxl_ref, f32[2,16,18,128]{3,2,1,0:T(8,128)} %get-tuple-element.43.fxr_ref, f32[2,16,18,128]{3,2,1,0:T(8,128)} %get-tuple-element.44.fyl_ref, ...), custom_call_target="tpu_custom_call" | custom-call | tf_op jit(solution)/shard_map/pallas_call | solution.py:281
  151.4 3.6 %copy.90 = f32[2,16,10,256]{3,2,1,0:T(8,128)S(1)} copy(f32[2,16,10,256]{2,1,3,0:T(8,128)} %slice.170) | data formatting | bytes 655360
  156.6 3.4 %shard_map.87.w_ref = f32[2,16,8,256]{3,2,1,0:T(8,128)} custom-call(f32[2,16,10,256]{3,2,1,0:T(8,128)} %add.176.w_ref, f32[2,16,12,256]{3,2,1,0:T(8,128)} %pad_maximum_fusion.5.w_ref.b_ref, f32[2,16,12,256]{3,2,1,0:T(8,128)} %get-tuple-element.34.fxl_ref, f32[2,16,12,256]{3,2,1,0:T(8,128)} %get-tuple-element.35.fxr_ref, ...), custom_call_target="tpu_custom_call" | custom-call | tf_op jit(solution)/shard_map/pallas_call | solution.py:187
  160.7 3.3 %shard_map.88 = f32[2,16,6,256]{3,2,1,0:T(8,128)} custom-call(f32[2,16,8,256]{3,2,1,0:T(8,128)} %shard_map.87.w_ref, f32[2,16,12,256]{3,2,1,0:T(8,128)} %pad_maximum_fusion.5.w_ref.b_ref, f32[2,16,12,256]{3,2,1,0:T(8,128)} %get-tuple-element.34.fxl_ref, f32[2,16,12,256]{3,2,1,0:T(8,128)} %get-tuple-element.35.fxr_ref, ...), custom_call_target="tpu_custom_call" | custom-call | tf_op jit(solution)/shard_map/pallas_call | solution.py:187
  166.0 4.5 %broadcast_in_dim.83 = f32[2,16,12,256,2]{1,4,3,2,0:T(2,128)} broadcast(f32[2,16,12,256]{1,3,2,0:T(8,128)S(1)} %copy.87), dimensions={0,1,2,3} | broadcast | bytes 1179648 | tf_op jit(solution)/shard_map/broadcast_in_dim | solution.py:346
  170.5 5.0 %copy.88 = f32[2,16,12,512]{3,2,1,0:T(8,128)S(1)} copy(f32[2,16,12,512]{1,3,2,0:T(8,128)} %bitcast.64) | data formatting | bytes 1572864 | tf_op jit(solution)/shard_map/reshape | solution.py:346
  177.4 6.0 %shard_map.89.w_ref = f32[2,16,10,512]{3,2,1,0:T(8,128)} custom-call(f32[2,16,12,512]{3,2,1,0:T(8,128)} %add.181.w_ref, f32[2,16,16,512]{3,2,1,0:T(8,128)} %get-tuple-element.66.b_ref, f32[2,16,14,512]{3,2,1,0:T(8,128)} %get-tuple-element.26.fxl_ref, f32[2,16,14,512]{3,2,1,0:T(8,128)} %get-tuple-element.27.fxr_ref, ...), custom_call_target="tpu_custom_call" | custom-call | tf_op jit(solution)/shard_map/pallas_call | solution.py:187
  183.4 5.6 %shard_map.90 = f32[2,16,8,512]{3,2,1,0:T(8,128)} custom-call(f32[2,16,10,512]{3,2,1,0:T(8,128)} %shard_map.89.w_ref, f32[2,16,16,512]{3,2,1,0:T(8,128)} %get-tuple-element.66.b_ref, f32[2,16,14,512]{3,2,1,0:T(8,128)} %get-tuple-element.26.fxl_ref, f32[2,16,14,512]{3,2,1,0:T(8,128)} %get-tuple-element.27.fxr_ref, ...), custom_call_target="tpu_custom_call" | custom-call | tf_op jit(solution)/shard_map/pallas_call | solution.py:187
  (149 shorter events, 77.3 us)
Async XLA Ops:
  7.2 2.4 %copy-start.3 = (f32[2,16,8,512]{3,2,1,0:T(8,128)S(1)}, f32[2,16,8,512]{3,2,1,0:T(8,128)}, u32[]{:S(2)}) copy-start(f32[2,16,8,512]{3,2,1,0:T(8,128)} %param.6) | copy-start | bytes 1572868
  7.2 2.6 %copy-start.2 = (f32[16,8,512]{2,1,0:T(8,128)S(1)}, f32[16,8,512]{2,1,0:T(8,128)}, u32[]{:S(2)}) copy-start(f32[16,8,512]{2,1,0:T(8,128)} %param.8) | copy-start | bytes 786436
  7.2 74.8 %all-gather.4.cloned.1.call-start = ((), (), s32[]{:S(2)}) async-start(), calls=%async_computation | async-start | bytes 1566720 | tf_op jit(solution)/shard_map/all_gather | solution.py:392
  10.7 18.5 %collective-permute-start = (f32[167936]{0:T(1024)}, f32[167936]{0:T(1024)}, u32[]{:S(2)}, u32[]{:S(2)}) collective-permute-start(f32[167936]{0:T(1024)} %pad_maximum_fusion.2), channel_id=1, source_target_pairs={{0,1},{1,2},{2,3},{3,4},{4,5},{5,6},{6,7},{7,8},{8,9},{9,10},{10,1... | collective-permute-start | bytes 2015240 | tf_op jit(solution)/shard_map/ppermute | solution.py:42
  13.8 16.2 %collective-permute-start.1 = (f32[167936]{0:T(1024)}, f32[167936]{0:T(1024)}, u32[]{:S(2)}, u32[]{:S(2)}) collective-permute-start(f32[167936]{0:T(1024)} %pad_maximum_fusion.3), channel_id=1, source_target_pairs={{1,0},{2,1},{3,2},{4,3},{5,4},{6,5},{7,6},{8,7},{9,8},{10,9},{11,1... | collective-permute-start | bytes 2015240 | tf_op jit(solution)/shard_map/ppermute | solution.py:43
  33.8 8.1 %copy-start.4 = (f32[2,16,8,512]{3,2,1,0:T(8,128)S(1)}, f32[2,16,8,512]{3,2,1,0:T(8,128)}, u32[]{:S(2)}) copy-start(f32[2,16,8,512]{3,2,1,0:T(8,128)} %param.6) | copy-start | bytes 1572868
  33.8 8.1 %copy-start.5 = (f32[2,16,8,512]{3,2,1,0:T(8,128)S(1)}, f32[2,16,8,512]{3,2,1,0:T(8,128)}, u32[]{:S(2)}) copy-start(f32[2,16,8,512]{3,2,1,0:T(8,128)} %param.7) | copy-start | bytes 1572868
  72.1 7.2 %collective-permute-start.2 = (f32[2,16,4,256]{3,2,1,0:T(4,128)S(1)}, f32[2,16,4,256]{3,2,1,0:T(4,128)S(1)}, u32[]{:S(2)}, u32[]{:S(2)}) collective-permute-start(f32[2,16,4,256]{3,2,1,0:T(4,128)S(1)} %broadcast_multiply_fusion), channel_id=1, source_target_pairs={{0,1},{1,2},{2,3},{3,4},{4,5},{5,6},{6,7},{7,8},{8,9},{9,10},{10,1... | collective-permute-start | bytes 393224 | tf_op jit(solution)/shard_map/ppermute | solution.py:27
  75.2 5.9 %collective-permute-start.3 = (f32[2,16,4,256]{3,2,1,0:T(4,128)S(1)}, f32[2,16,4,256]{3,2,1,0:T(4,128)S(1)}, u32[]{:S(2)}, u32[]{:S(2)}) collective-permute-start(f32[2,16,4,256]{3,2,1,0:T(4,128)S(1)} %broadcast_multiply_fusion), channel_id=1, source_target_pairs={{1,0},{2,1},{3,2},{4,3},{5,4},{6,5},{7,6},{8,7},{9,8},{10,9},{11,1... | collective-permute-start | bytes 393224 | tf_op jit(solution)/shard_map/ppermute | solution.py:29
  108.2 16.9 %collective-permute-start.10 = (f32[2,16,2,128]{3,2,1,0:T(2,128)S(1)}, f32[2,16,2,128]{3,2,1,0:T(2,128)S(1)}, u32[]{:S(2)}, u32[]{:S(2)}) collective-permute-start(f32[2,16,2,128]{3,2,1,0:T(2,128)S(1)} %broadcast_multiply_fusion.2), channel_id=1, source_target_pairs={{3,0},{4,1},{5,2},{6,3},{7,4},{8,5},{9,6},{10,7},{11,8},{12,9},{13... | collective-permute-start | bytes 98312 | tf_op jit(solution)/shard_map/ppermute | solution.py:376
  112.2 15.4 %collective-permute-start.11 = (f32[2,16,2,128]{3,2,1,0:T(2,128)S(1)}, f32[2,16,2,128]{3,2,1,0:T(2,128)S(1)}, u32[]{:S(2)}, u32[]{:S(2)}) collective-permute-start(f32[2,16,2,128]{3,2,1,0:T(2,128)S(1)} %broadcast_multiply_fusion.2), channel_id=1, source_target_pairs={{4,0},{5,1},{6,2},{7,3},{8,4},{9,5},{10,6},{11,7},{12,8},{13,9},{1... | collective-permute-start | bytes 98312 | tf_op jit(solution)/shard_map/ppermute | solution.py:376
  114.1 17.5 %collective-permute-start.4 = (f32[2,16,2,128]{3,2,1,0:T(2,128)S(1)}, f32[2,16,2,128]{3,2,1,0:T(2,128)S(1)}, u32[]{:S(2)}, u32[]{:S(2)}) collective-permute-start(f32[2,16,2,128]{3,2,1,0:T(2,128)S(1)} %broadcast_multiply_fusion.2), channel_id=1, source_target_pairs={{0,4},{1,5},{2,6},{3,7},{4,8},{5,9},{6,10},{7,11},{8,12},{9,13},{1... | collective-permute-start | bytes 98312 | tf_op jit(solution)/shard_map/ppermute | solution.py:375
  118.1 19.0 %collective-permute-start.5 = (f32[2,16,2,128]{3,2,1,0:T(2,128)S(1)}, f32[2,16,2,128]{3,2,1,0:T(2,128)S(1)}, u32[]{:S(2)}, u32[]{:S(2)}) collective-permute-start(f32[2,16,2,128]{3,2,1,0:T(2,128)S(1)} %broadcast_multiply_fusion.2), channel_id=1, source_target_pairs={{0,3},{1,4},{2,5},{3,6},{4,7},{5,8},{6,9},{7,10},{8,11},{9,12},{10... | collective-permute-start | bytes 98312 | tf_op jit(solution)/shard_map/ppermute | solution.py:375
  120.2 16.8 %collective-permute-start.6 = (f32[2,16,2,128]{3,2,1,0:T(2,128)S(1)}, f32[2,16,2,128]{3,2,1,0:T(2,128)S(1)}, u32[]{:S(2)}, u32[]{:S(2)}) collective-permute-start(f32[2,16,2,128]{3,2,1,0:T(2,128)S(1)} %broadcast_multiply_fusion.2), channel_id=1, source_target_pairs={{0,2},{1,3},{2,4},{3,5},{4,6},{5,7},{6,8},{7,9},{8,10},{9,11},{10,... | collective-permute-start | bytes 98312 | tf_op jit(solution)/shard_map/ppermute | solution.py:375
  125.1 11.9 %collective-permute-start.7 = (f32[2,16,2,128]{3,2,1,0:T(2,128)S(1)}, f32[2,16,2,128]{3,2,1,0:T(2,128)S(1)}, u32[]{:S(2)}, u32[]{:S(2)}) collective-permute-start(f32[2,16,2,128]{3,2,1,0:T(2,128)S(1)} %broadcast_multiply_fusion.2), channel_id=1, source_target_pairs={{0,1},{1,2},{2,3},{3,4},{4,5},{5,6},{6,7},{7,8},{8,9},{9,10},{10,1... | collective-permute-start | bytes 98312 | tf_op jit(solution)/shard_map/ppermute | solution.py:375
  127.6 9.4 %collective-permute-start.8 = (f32[2,16,2,128]{3,2,1,0:T(2,128)S(1)}, f32[2,16,2,128]{3,2,1,0:T(2,128)S(1)}, u32[]{:S(2)}, u32[]{:S(2)}) collective-permute-start(f32[2,16,2,128]{3,2,1,0:T(2,128)S(1)} %broadcast_multiply_fusion.2), channel_id=1, source_target_pairs={{1,0},{2,1},{3,2},{4,3},{5,4},{6,5},{7,6},{8,7},{9,8},{10,9},{11,1... | collective-permute-start | bytes 98312 | tf_op jit(solution)/shard_map/ppermute | solution.py:376
  131.6 5.8 %collective-permute-start.9 = (f32[2,16,2,128]{3,2,1,0:T(2,128)S(1)}, f32[2,16,2,128]{3,2,1,0:T(2,128)S(1)}, u32[]{:S(2)}, u32[]{:S(2)}) collective-permute-start(f32[2,16,2,128]{3,2,1,0:T(2,128)S(1)} %broadcast_multiply_fusion.2), channel_id=1, source_target_pairs={{2,0},{3,1},{4,2},{5,3},{6,4},{7,5},{8,6},{9,7},{10,8},{11,9},{12,... | collective-permute-start | bytes 98312 | tf_op jit(solution)/shard_map/ppermute | solution.py:376
  151.4 3.6 %copy-start.1 = (f32[2,16,10,256]{3,2,1,0:T(8,128)S(1)}, f32[2,16,10,256]{3,2,1,0:T(8,128)}, u32[]{:S(2)}) copy-start(f32[2,16,10,256]{3,2,1,0:T(8,128)} %shard_map.83.w_ref) | copy-start | bytes 983044
  170.5 5.0 %copy-start = (f32[2,16,12,512]{3,2,1,0:T(8,128)S(1)}, f32[2,16,12,512]{3,2,1,0:T(8,128)}, u32[]{:S(2)}) copy-start(f32[2,16,12,512]{3,2,1,0:T(8,128)} %shard_map.79.w_ref) | copy-start | bytes 2359300
  183.4 5.6 %copy-start.6 = (f32[2,8,512]{2,1,0:T(8,128)S(1)}, f32[2,8,512]{2,1,0:T(8,128)}, u32[]{:S(2)}) copy-start(f32[2,8,512]{2,1,0:T(8,128)} %param.11) | copy-start | bytes 98308
Sparse Core Ops, SparseCore 0:
  29.2 38.5 all-gather.3

commit v2 on v1

--- a/solution.py
+++ b/solution.py
@@ -343,7 +343,10 @@
 
 
 def prolong(field):
-    return jnp.repeat(jnp.repeat(field, 2, axis=2), 2, axis=3)
+    cols = field.shape[3]
+    spread = (jnp.arange(cols)[:, None] == jnp.arange(2 * cols)[None, :] // 2).astype(jnp.float32)
+    wide = jnp.einsum("ckxy,yz->ckxz", field, spread, precision=lax.Precision.HIGHEST)
+    return jnp.repeat(wide, 2, axis=2)
 
 
 def pad_rim(field):

time: 198 us -> 181 us (0.914)
  local copies, waits for them, and re-layouts: 59.3 us -> 39.5 us
  matrix products: 0 us -> 2.54 us
    reshape x3 -> x1, local copies, waits for them, and re-layouts: 6.94 us -> 0.37 us  [prolong(): return jnp.repeat(wide, 2, axis=2)]
    broadcast_in_dim x4 -> x2, local copies, waits for them, and re-layouts: 4.87 us -> 0.35 us  [prolong(): return jnp.repeat(wide, 2, axis=2)]
    slice x3 -> x0, local copies, waits for them, and re-layouts: 4.1 us -> none  [the longest x1 3.1 us: shards(): middle = middle + lift[:, :, trim:lift.shape[2] - trim]]
    unnamed x30 -> x29, local copies, waits for them, and re-layouts: 6.92 us -> 3.28 us
    dot_general x0 -> x2, matrix products: none -> 2.54 us  [prolong(): jnp.einsum('ckxy,yz->ckxz', field, spread, precision=lax.Precision.HIGHEST)]
    pallas_call x3 -> x2, local copies, waits for them, and re-layouts: 5.81 us -> 4.87 us  [kernel_sweep(): pl.pallas_call(body, grid=(parts,), in_specs=specs, out_specs=pl.BlockSpe...]
  transfers between devices with their start and end apart: 13 -> 13, of which waited for: 3 -> 3; matrix products, arithmetic and copies ran while one was open for 18% -> 20% of each run, Pallas kernels for 12% -> 13%
where the time goes in v2:
time: 181 us; the launch traced here: 180 us
  Pallas kernels  61.4 us (34%)
  local copies, waits for them, and re-layouts  39.5 us (22%)
  starting transfers between devices  37.2 us (21%)
  other arithmetic  21.9 us (12%)
  between operations  14.8 us (8%)
  waiting for transfers between devices  2.94 us (2%)
  matrix products  2.54 us (1%)
    pallas_call x10, Pallas kernels, kernel_sweep(): pl.pallas_call(body, grid=(parts,), in_specs=specs, out_specs=pl.BlockSpe...  44.9 us
    ppermute x4, starting transfers between devices, nearby(): lax.ppermute(cells, 'gx', [(i, i + step) for i in range(count - step)])  12.2 us
    ppermute x4, starting transfers between devices, nearby(): lax.ppermute(cells, 'gx', [(i + step, i) for i in range(count - step)])  12 us
    reduce_sum x6, other arithmetic, block_mean(): return shaped.mean(axis=(-3, -1))  11.1 us
    pallas_call x3, Pallas kernels, kernel_operator(): pl.pallas_call(body, grid=(2,), in_specs=[whole(eta_level), whole(react_l...  11 us
    broadcast_in_dim x10, local copies, waits for them, and re-layouts, rows_inside(): jnp.broadcast_to(inside(cells, halo, extent)[0, 0], (extent, cols))  6.71 us
    pallas_call x1, Pallas kernels, kernel_coarse(): pl.pallas_call(body, grid=(parts,), in_specs=specs, out_specs=pl.BlockSpe...  5.63 us
    pallas_call x2, local copies, waits for them, and re-layouts, kernel_sweep(): pl.pallas_call(body, grid=(parts,), in_specs=specs, out_specs=pl.BlockSpe...  4.87 us
  transfers between devices with their start and end apart: 13, of which 3 were waited for; matrix products, arithmetic and copies ran while one was open for 20% of the time, Pallas kernels for 13%

profile of v2, /device:TPU:10, one launch (start us, length us, event | category | flops | bytes accessed | tf_op | source)
XLA Modules:
  0.0 180.3 jit_solution(5402516010547887689)
XLA Ops:
  13.8 4.5 %collective-permute-start.1 = (f32[167936]{0:T(1024)}, f32[167936]{0:T(1024)}, u32[]{:S(2)}, u32[]{:S(2)}) collective-permute-start(f32[167936]{0:T(1024)} %pad_maximum_fusion.3), channel_id=1, source_target_pairs={{1,0},{2,1},{3,2},{4,3},{5,4},{6,5},{7,6},{8,7},{9,8},{10,9},{11,1... | collective-permute-start | bytes 2015240 | tf_op jit(solution)/shard_map/ppermute | solution.py:43
  18.3 3.4 %reshape.308 = f32[2,4,2,256,2]{4,3,2,1,0:T(8,128)} reshape(f32[2,8,512]{2,1,0:T(8,128)S(1)} %slice.163) | data formatting | bytes 65536 | tf_op jit(solution)/shard_map/reshape | solution.py:58
  36.8 5.0 %shard_map.77 = (f32[2,16,14,512]{3,2,1,0:T(8,128)}, f32[2,16,14,512]{3,2,1,0:T(8,128)}, f32[2,16,14,512]{3,2,1,0:T(8,128)}, f32[2,16,14,512]{3,2,1,0:T(8,128)},...) custom-call(f32[16,16,512]{2,1,0:T(8,128)} %pad_maximum_fusion.4.eta_, ...), custom_call_target="tpu_custom_call" | custom-call | tf_op jit(solution)/shard_map/pallas_call | solution.py:262
  44.3 5.7 %shard_map.78.w_ref = f32[2,16,14,512]{3,2,1,0:T(8,128)} custom-call(f32[2,16,16,512]{3,2,1,0:T(8,128)} %get-tuple-element.65.w_ref, f32[2,16,16,512]{3,2,1,0:T(8,128)} %get-tuple-element.66.b_ref, f32[2,16,14,512]{3,2,1,0:T(8,128)} %get-tuple-element.26.fxl_ref, f32[2,16,14,512]{3,2,1,0:T(8,128)} %get-tuple-element.27.fxr_ref, ...), custom_call_target="tpu_custom_call" | custom-call | tf_op jit(solution)/shard_map/pallas_call | solution.py:187
  50.7 5.9 %shard_map.79.w_ref = f32[2,16,12,512]{3,2,1,0:T(8,128)} custom-call(f32[2,16,14,512]{3,2,1,0:T(8,128)} %shard_map.78.w_ref, f32[2,16,16,512]{3,2,1,0:T(8,128)} %get-tuple-element.66.b_ref, f32[2,16,14,512]{3,2,1,0:T(8,128)} %get-tuple-element.26.fxl_ref, f32[2,16,14,512]{3,2,1,0:T(8,128)} %get-tuple-element.27.fxr_ref, ...), custom_call_target="tpu_custom_call" | custom-call | tf_op jit(solution)/shard_map/pallas_call | solution.py:187
  57.3 5.1 %shard_map.80 = f32[2,16,8,512]{3,2,1,0:T(8,128)} custom-call(f32[2,16,12,512]{3,2,1,0:T(8,128)} %shard_map.79.w_ref, f32[2,16,16,512]{3,2,1,0:T(8,128)} %get-tuple-element.66.b_ref, f32[2,16,14,512]{3,2,1,0:T(8,128)} %get-tuple-element.26.fxl_ref, f32[2,16,14,512]{3,2,1,0:T(8,128)} %get-tuple-element.27.fxr_ref, ...), custom_call_target="tpu_custom_call" | custom-call | tf_op jit(solution)/shard_map/pallas_call | solution.py:187
  62.3 3.6 %copy.46 = f32[2,16,8,512]{1,3,2,0:T(8,128)} copy(f32[2,16,8,512]{3,2,1,0:T(8,128)} %shard_map.80) | data formatting | bytes 1048576 | tf_op jit(solution)/shard_map/pallas_call | solution.py:187
  66.0 5.8 %reduce_sum.54 = f32[2,16,4,256]{1,3,2,0:T(8,128)S(1)} reduce(f32[2,16,4,2,256,2]{1,5,4,3,2,0:T(2,128)} %bitcast.73, f32[]{:T(128)} %constant.39.clone.1), dimensions={3,5}, to_apply=%region_0.0 | reduce | flops 98304 | bytes 655364 | tf_op jit(solution)/shard_map/reduce_sum | solution.py:59
  72.1 3.1 %collective-permute-start.2 = (f32[2,16,4,256]{3,2,1,0:T(4,128)S(1)}, f32[2,16,4,256]{3,2,1,0:T(4,128)S(1)}, u32[]{:S(2)}, u32[]{:S(2)}) collective-permute-start(f32[2,16,4,256]{3,2,1,0:T(4,128)S(1)} %broadcast_multiply_fusion), channel_id=1, source_target_pairs={{0,1},{1,2},{2,3},{3,4},{4,5},{5,6},{6,7},{7,8},{8,9},{9,10},{10,1... | collective-permute-start | bytes 393224 | tf_op jit(solution)/shard_map/ppermute | solution.py:27
  75.2 3.4 %collective-permute-start.3 = (f32[2,16,4,256]{3,2,1,0:T(4,128)S(1)}, f32[2,16,4,256]{3,2,1,0:T(4,128)S(1)}, u32[]{:S(2)}, u32[]{:S(2)}) collective-permute-start(f32[2,16,4,256]{3,2,1,0:T(4,128)S(1)} %broadcast_multiply_fusion), channel_id=1, source_target_pairs={{1,0},{2,1},{3,2},{4,3},{5,4},{6,5},{7,6},{8,7},{9,8},{10,9},{11,1... | collective-permute-start | bytes 393224 | tf_op jit(solution)/shard_map/ppermute | solution.py:29
  90.9 3.3 %shard_map.81 = (f32[2,16,12,256]{3,2,1,0:T(8,128)}, f32[2,16,12,256]{3,2,1,0:T(8,128)}, f32[2,16,12,256]{3,2,1,0:T(8,128)}, f32[2,16,12,256]{3,2,1,0:T(8,128)},...) custom-call(f32[16,14,256]{2,1,0:T(8,128)} %pad_dynamic-slice_fusion., ...), custom_call_target="tpu_custom_call" | custom-call | tf_op jit(solution)/shard_map/pallas_call | solution.py:262
  94.8 3.1 %shard_map.82.w_ref = f32[2,16,12,256]{3,2,1,0:T(8,128)} custom-call(f32[2,16,12,256]{3,2,1,0:T(8,128)} %pad_maximum_fusion.5.w_ref.b_ref, f32[2,16,12,256]{3,2,1,0:T(8,128)} %pad_maximum_fusion.5.w_ref.b_ref, f32[2,16,12,256]{3,2,1,0:T(8,128)} %get-tuple-element.34.fxl_ref, f32[2,16,12,256]{3,2,1,0:T(8,128)} %get-tuple-element.35.fxr_ref, ...), custom_call_target="tpu_custom_call" | custom-call | tf_op jit(solution)/shard_map/pallas_call | solution.py:187
  98.6 3.6 %shard_map.83.w_ref = f32[2,16,10,256]{3,2,1,0:T(8,128)} custom-call(f32[2,16,12,256]{3,2,1,0:T(8,128)} %shard_map.82.w_ref, f32[2,16,12,256]{3,2,1,0:T(8,128)} %pad_maximum_fusion.5.w_ref.b_ref, f32[2,16,12,256]{3,2,1,0:T(8,128)} %get-tuple-element.34.fxl_ref, f32[2,16,12,256]{3,2,1,0:T(8,128)} %get-tuple-element.35.fxr_ref, ...), custom_call_target="tpu_custom_call" | custom-call | tf_op jit(solution)/shard_map/pallas_call | solution.py:187
  102.8 3.1 %shard_map.84 = f32[2,16,4,256]{3,2,1,0:T(4,128)} custom-call(f32[2,16,10,256]{3,2,1,0:T(8,128)} %shard_map.83.w_ref, f32[2,16,12,256]{3,2,1,0:T(8,128)} %pad_maximum_fusion.5.w_ref.b_ref, f32[2,16,12,256]{3,2,1,0:T(8,128)} %get-tuple-element.34.fxl_ref, f32[2,16,12,256]{3,2,1,0:T(8,128)} %get-tuple-element.35.fxr_ref, ...), custom_call_target="tpu_custom_call" | custom-call | tf_op jit(solution)/shard_map/pallas_call | solution.py:187
  108.2 4.0 %collective-permute-start.10 = (f32[2,16,2,128]{3,2,1,0:T(2,128)S(1)}, f32[2,16,2,128]{3,2,1,0:T(2,128)S(1)}, u32[]{:S(2)}, u32[]{:S(2)}) collective-permute-start(f32[2,16,2,128]{3,2,1,0:T(2,128)S(1)} %broadcast_multiply_fusion.2), channel_id=1, source_target_pairs={{3,0},{4,1},{5,2},{6,3},{7,4},{8,5},{9,6},{10,7},{11,8},{12,9},{13... | collective-permute-start | bytes 98312 | tf_op jit(solution)/shard_map/ppermute | solution.py:379
  114.1 3.9 %collective-permute-start.4 = (f32[2,16,2,128]{3,2,1,0:T(2,128)S(1)}, f32[2,16,2,128]{3,2,1,0:T(2,128)S(1)}, u32[]{:S(2)}, u32[]{:S(2)}) collective-permute-start(f32[2,16,2,128]{3,2,1,0:T(2,128)S(1)} %broadcast_multiply_fusion.2), channel_id=1, source_target_pairs={{0,4},{1,5},{2,6},{3,7},{4,8},{5,9},{6,10},{7,11},{8,12},{9,13},{1... | collective-permute-start | bytes 98312 | tf_op jit(solution)/shard_map/ppermute | solution.py:378
  120.2 3.8 %collective-permute-start.6 = (f32[2,16,2,128]{3,2,1,0:T(2,128)S(1)}, f32[2,16,2,128]{3,2,1,0:T(2,128)S(1)}, u32[]{:S(2)}, u32[]{:S(2)}) collective-permute-start(f32[2,16,2,128]{3,2,1,0:T(2,128)S(1)} %broadcast_multiply_fusion.2), channel_id=1, source_target_pairs={{0,2},{1,3},{2,4},{3,5},{4,6},{5,7},{6,8},{7,9},{8,10},{9,11},{10,... | collective-permute-start | bytes 98312 | tf_op jit(solution)/shard_map/ppermute | solution.py:378
  127.6 4.0 %collective-permute-start.8 = (f32[2,16,2,128]{3,2,1,0:T(2,128)S(1)}, f32[2,16,2,128]{3,2,1,0:T(2,128)S(1)}, u32[]{:S(2)}, u32[]{:S(2)}) collective-permute-start(f32[2,16,2,128]{3,2,1,0:T(2,128)S(1)} %broadcast_multiply_fusion.2), channel_id=1, source_target_pairs={{1,0},{2,1},{3,2},{4,3},{5,4},{6,5},{7,6},{8,7},{9,8},{10,9},{11,1... | collective-permute-start | bytes 98312 | tf_op jit(solution)/shard_map/ppermute | solution.py:379
  134.3 2.6 %shard_map.85 = (f32[2,16,18,128]{3,2,1,0:T(8,128)}, f32[2,16,18,128]{3,2,1,0:T(8,128)}, f32[2,16,18,128]{3,2,1,0:T(8,128)}, f32[2,16,18,128]{3,2,1,0:T(8,128)},...) custom-call(f32[16,20,128]{2,1,0:T(8,128)} %pad_dynamic-slice_fusion., ...), custom_call_target="tpu_custom_call" | custom-call | tf_op jit(solution)/shard_map/pallas_call | solution.py:262
  140.3 5.6 %shard_map.86 = f32[2,16,18,128]{3,2,1,0:T(8,128)} custom-call(f32[2,16,18,128]{3,2,1,0:T(8,128)} %concatenate.35.b_ref, f32[2,16,18,128]{3,2,1,0:T(8,128)} %get-tuple-element.42.fxl_ref, f32[2,16,18,128]{3,2,1,0:T(8,128)} %get-tuple-element.43.fxr_ref, f32[2,16,18,128]{3,2,1,0:T(8,128)} %get-tuple-element.44.fyl_ref, ...), custom_call_target="tpu_custom_call" | custom-call | tf_op jit(solution)/shard_map/pallas_call | solution.py:281
  149.4 3.4 %shard_map.87.w_ref = f32[2,16,8,256]{3,2,1,0:T(8,128)} custom-call(f32[2,16,10,256]{3,2,1,0:T(8,128)} %slice_add_fusion.w_ref, f32[2,16,12,256]{3,2,1,0:T(8,128)} %pad_maximum_fusion.5.w_ref.b_ref, f32[2,16,12,256]{3,2,1,0:T(8,128)} %get-tuple-element.34.fxl_ref, f32[2,16,12,256]{3,2,1,0:T(8,128)} %get-tuple-element.35.fxr_ref, ...), custom_call_target="tpu_custom_call" | custom-call | tf_op jit(solution)/shard_map/pallas_call | solution.py:187
  153.5 3.4 %shard_map.88 = f32[2,16,6,256]{3,2,1,0:T(8,128)} custom-call(f32[2,16,8,256]{3,2,1,0:T(8,128)} %shard_map.87.w_ref, f32[2,16,12,256]{3,2,1,0:T(8,128)} %pad_maximum_fusion.5.w_ref.b_ref, f32[2,16,12,256]{3,2,1,0:T(8,128)} %get-tuple-element.34.fxl_ref, f32[2,16,12,256]{3,2,1,0:T(8,128)} %get-tuple-element.35.fxr_ref, ...), custom_call_target="tpu_custom_call" | custom-call | tf_op jit(solution)/shard_map/pallas_call | solution.py:187
  160.5 6.0 %shard_map.89.w_ref = f32[2,16,10,512]{3,2,1,0:T(8,128)} custom-call(f32[2,16,12,512]{3,2,1,0:T(8,128)} %copy_add_fusion.w_ref, f32[2,16,16,512]{3,2,1,0:T(8,128)} %get-tuple-element.66.b_ref, f32[2,16,14,512]{3,2,1,0:T(8,128)} %get-tuple-element.26.fxl_ref, f32[2,16,14,512]{3,2,1,0:T(8,128)} %get-tuple-element.27.fxr_ref, ...), custom_call_target="tpu_custom_call" | custom-call | tf_op jit(solution)/shard_map/pallas_call | solution.py:187
  166.5 5.6 %shard_map.90 = f32[2,16,8,512]{3,2,1,0:T(8,128)} custom-call(f32[2,16,10,512]{3,2,1,0:T(8,128)} %shard_map.89.w_ref, f32[2,16,16,512]{3,2,1,0:T(8,128)} %get-tuple-element.66.b_ref, f32[2,16,14,512]{3,2,1,0:T(8,128)} %get-tuple-element.26.fxl_ref, f32[2,16,14,512]{3,2,1,0:T(8,128)} %get-tuple-element.27.fxr_ref, ...), custom_call_target="tpu_custom_call" | custom-call | tf_op jit(solution)/shard_map/pallas_call | solution.py:187
  (144 shorter events, 64.4 us)
Async XLA Ops:
  7.2 2.4 %copy-start.3 = (f32[2,16,8,512]{3,2,1,0:T(8,128)S(1)}, f32[2,16,8,512]{3,2,1,0:T(8,128)}, u32[]{:S(2)}) copy-start(f32[2,16,8,512]{3,2,1,0:T(8,128)} %param.6) | copy-start | bytes 1572868
  7.2 2.6 %copy-start.2 = (f32[16,8,512]{2,1,0:T(8,128)S(1)}, f32[16,8,512]{2,1,0:T(8,128)}, u32[]{:S(2)}) copy-start(f32[16,8,512]{2,1,0:T(8,128)} %param.8) | copy-start | bytes 786436
  7.2 74.8 %all-gather.4.cloned.1.call-start = ((), (), s32[]{:S(2)}) async-start(), calls=%async_computation | async-start | bytes 1566720 | tf_op jit(solution)/shard_map/all_gather | solution.py:395
  10.8 18.5 %collective-permute-start = (f32[167936]{0:T(1024)}, f32[167936]{0:T(1024)}, u32[]{:S(2)}, u32[]{:S(2)}) collective-permute-start(f32[167936]{0:T(1024)} %pad_maximum_fusion.2), channel_id=1, source_target_pairs={{0,1},{1,2},{2,3},{3,4},{4,5},{5,6},{6,7},{7,8},{8,9},{9,10},{10,1... | collective-permute-start | bytes 2015240 | tf_op jit(solution)/shard_map/ppermute | solution.py:42
  13.8 16.2 %collective-permute-start.1 = (f32[167936]{0:T(1024)}, f32[167936]{0:T(1024)}, u32[]{:S(2)}, u32[]{:S(2)}) collective-permute-start(f32[167936]{0:T(1024)} %pad_maximum_fusion.3), channel_id=1, source_target_pairs={{1,0},{2,1},{3,2},{4,3},{5,4},{6,5},{7,6},{8,7},{9,8},{10,9},{11,1... | collective-permute-start | bytes 2015240 | tf_op jit(solution)/shard_map/ppermute | solution.py:43
  33.8 8.0 %copy-start.4 = (f32[2,16,8,512]{3,2,1,0:T(8,128)S(1)}, f32[2,16,8,512]{3,2,1,0:T(8,128)}, u32[]{:S(2)}) copy-start(f32[2,16,8,512]{3,2,1,0:T(8,128)} %param.6) | copy-start | bytes 1572868
  33.9 8.0 %copy-start.5 = (f32[2,16,8,512]{3,2,1,0:T(8,128)S(1)}, f32[2,16,8,512]{3,2,1,0:T(8,128)}, u32[]{:S(2)}) copy-start(f32[2,16,8,512]{3,2,1,0:T(8,128)} %param.7) | copy-start | bytes 1572868
  72.1 7.2 %collective-permute-start.2 = (f32[2,16,4,256]{3,2,1,0:T(4,128)S(1)}, f32[2,16,4,256]{3,2,1,0:T(4,128)S(1)}, u32[]{:S(2)}, u32[]{:S(2)}) collective-permute-start(f32[2,16,4,256]{3,2,1,0:T(4,128)S(1)} %broadcast_multiply_fusion), channel_id=1, source_target_pairs={{0,1},{1,2},{2,3},{3,4},{4,5},{5,6},{6,7},{7,8},{8,9},{9,10},{10,1... | collective-permute-start | bytes 393224 | tf_op jit(solution)/shard_map/ppermute | solution.py:27
  75.2 5.9 %collective-permute-start.3 = (f32[2,16,4,256]{3,2,1,0:T(4,128)S(1)}, f32[2,16,4,256]{3,2,1,0:T(4,128)S(1)}, u32[]{:S(2)}, u32[]{:S(2)}) collective-permute-start(f32[2,16,4,256]{3,2,1,0:T(4,128)S(1)} %broadcast_multiply_fusion), channel_id=1, source_target_pairs={{1,0},{2,1},{3,2},{4,3},{5,4},{6,5},{7,6},{8,7},{9,8},{10,9},{11,1... | collective-permute-start | bytes 393224 | tf_op jit(solution)/shard_map/ppermute | solution.py:29
  108.2 16.9 %collective-permute-start.10 = (f32[2,16,2,128]{3,2,1,0:T(2,128)S(1)}, f32[2,16,2,128]{3,2,1,0:T(2,128)S(1)}, u32[]{:S(2)}, u32[]{:S(2)}) collective-permute-start(f32[2,16,2,128]{3,2,1,0:T(2,128)S(1)} %broadcast_multiply_fusion.2), channel_id=1, source_target_pairs={{3,0},{4,1},{5,2},{6,3},{7,4},{8,5},{9,6},{10,7},{11,8},{12,9},{13... | collective-permute-start | bytes 98312 | tf_op jit(solution)/shard_map/ppermute | solution.py:379
  112.2 15.4 %collective-permute-start.11 = (f32[2,16,2,128]{3,2,1,0:T(2,128)S(1)}, f32[2,16,2,128]{3,2,1,0:T(2,128)S(1)}, u32[]{:S(2)}, u32[]{:S(2)}) collective-permute-start(f32[2,16,2,128]{3,2,1,0:T(2,128)S(1)} %broadcast_multiply_fusion.2), channel_id=1, source_target_pairs={{4,0},{5,1},{6,2},{7,3},{8,4},{9,5},{10,6},{11,7},{12,8},{13,9},{1... | collective-permute-start | bytes 98312 | tf_op jit(solution)/shard_map/ppermute | solution.py:379
  114.1 17.5 %collective-permute-start.4 = (f32[2,16,2,128]{3,2,1,0:T(2,128)S(1)}, f32[2,16,2,128]{3,2,1,0:T(2,128)S(1)}, u32[]{:S(2)}, u32[]{:S(2)}) collective-permute-start(f32[2,16,2,128]{3,2,1,0:T(2,128)S(1)} %broadcast_multiply_fusion.2), channel_id=1, source_target_pairs={{0,4},{1,5},{2,6},{3,7},{4,8},{5,9},{6,10},{7,11},{8,12},{9,13},{1... | collective-permute-start | bytes 98312 | tf_op jit(solution)/shard_map/ppermute | solution.py:378
  118.0 18.9 %collective-permute-start.5 = (f32[2,16,2,128]{3,2,1,0:T(2,128)S(1)}, f32[2,16,2,128]{3,2,1,0:T(2,128)S(1)}, u32[]{:S(2)}, u32[]{:S(2)}) collective-permute-start(f32[2,16,2,128]{3,2,1,0:T(2,128)S(1)} %broadcast_multiply_fusion.2), channel_id=1, source_target_pairs={{0,3},{1,4},{2,5},{3,6},{4,7},{5,8},{6,9},{7,10},{8,11},{9,12},{10... | collective-permute-start | bytes 98312 | tf_op jit(solution)/shard_map/ppermute | solution.py:378
  120.2 16.8 %collective-permute-start.6 = (f32[2,16,2,128]{3,2,1,0:T(2,128)S(1)}, f32[2,16,2,128]{3,2,1,0:T(2,128)S(1)}, u32[]{:S(2)}, u32[]{:S(2)}) collective-permute-start(f32[2,16,2,128]{3,2,1,0:T(2,128)S(1)} %broadcast_multiply_fusion.2), channel_id=1, source_target_pairs={{0,2},{1,3},{2,4},{3,5},{4,6},{5,7},{6,8},{7,9},{8,10},{9,11},{10,... | collective-permute-start | bytes 98312 | tf_op jit(solution)/shard_map/ppermute | solution.py:378
  125.1 11.9 %collective-permute-start.7 = (f32[2,16,2,128]{3,2,1,0:T(2,128)S(1)}, f32[2,16,2,128]{3,2,1,0:T(2,128)S(1)}, u32[]{:S(2)}, u32[]{:S(2)}) collective-permute-start(f32[2,16,2,128]{3,2,1,0:T(2,128)S(1)} %broadcast_multiply_fusion.2), channel_id=1, source_target_pairs={{0,1},{1,2},{2,3},{3,4},{4,5},{5,6},{6,7},{7,8},{8,9},{9,10},{10,1... | collective-permute-start | bytes 98312 | tf_op jit(solution)/shard_map/ppermute | solution.py:378
  127.6 9.4 %collective-permute-start.8 = (f32[2,16,2,128]{3,2,1,0:T(2,128)S(1)}, f32[2,16,2,128]{3,2,1,0:T(2,128)S(1)}, u32[]{:S(2)}, u32[]{:S(2)}) collective-permute-start(f32[2,16,2,128]{3,2,1,0:T(2,128)S(1)} %broadcast_multiply_fusion.2), channel_id=1, source_target_pairs={{1,0},{2,1},{3,2},{4,3},{5,4},{6,5},{7,6},{8,7},{9,8},{10,9},{11,1... | collective-permute-start | bytes 98312 | tf_op jit(solution)/shard_map/ppermute | solution.py:379
  131.6 5.8 %collective-permute-start.9 = (f32[2,16,2,128]{3,2,1,0:T(2,128)S(1)}, f32[2,16,2,128]{3,2,1,0:T(2,128)S(1)}, u32[]{:S(2)}, u32[]{:S(2)}) collective-permute-start(f32[2,16,2,128]{3,2,1,0:T(2,128)S(1)} %broadcast_multiply_fusion.2), channel_id=1, source_target_pairs={{2,0},{3,1},{4,2},{5,3},{6,4},{7,5},{8,6},{9,7},{10,8},{11,9},{12,... | collective-permute-start | bytes 98312 | tf_op jit(solution)/shard_map/ppermute | solution.py:379
  140.3 7.5 %copy-start.1 = (f32[2,16,10,256]{3,2,1,0:T(8,128)S(1)}, f32[2,16,10,256]{3,2,1,0:T(8,128)}, u32[]{:S(2)}) copy-start(f32[2,16,10,256]{3,2,1,0:T(8,128)} %shard_map.83.w_ref) | copy-start | bytes 983044
  153.5 4.8 %copy-start = (f32[2,16,12,512]{3,2,1,0:T(8,128)S(1)}, f32[2,16,12,512]{3,2,1,0:T(8,128)}, u32[]{:S(2)}) copy-start(f32[2,16,12,512]{3,2,1,0:T(8,128)} %shard_map.79.w_ref) | copy-start | bytes 2359300
  166.5 5.6 %copy-start.6 = (f32[2,8,512]{2,1,0:T(8,128)S(1)}, f32[2,8,512]{2,1,0:T(8,128)}, u32[]{:S(2)}) copy-start(f32[2,8,512]{2,1,0:T(8,128)} %param.11) | copy-start | bytes 98308
Sparse Core Ops, SparseCore 0:
  29.2 38.5 all-gather.3

commit v3 on v2

--- a/solution.py
+++ b/solution.py
@@ -53,10 +53,14 @@
 
 
 def block_mean(field, factor):
-    lead = field.shape[:-2]
-    rows, cols = (field.shape[-2], field.shape[-1])
-    shaped = field.reshape(lead + (rows // factor, factor, cols // factor, factor))
-    return shaped.mean(axis=(-3, -1))
+    while factor > 1:
+        lead = field.shape[:-2]
+        rows, cols = (field.shape[-2], field.shape[-1])
+        pairs = (jnp.arange(cols)[:, None] // 2 == jnp.arange(cols // 2)[None, :]).astype(jnp.float32)
+        field = jnp.einsum("...y,yz->...z", field, pairs, precision=lax.Precision.HIGHEST)
+        field = 0.25 * field.reshape(lead + (rows // 2, 2, cols // 2)).sum(axis=-2)
+        factor //= 2
+    return field
 
 
 def reaction_field(friction, ice_mask, layers):

time: 181 us -> 170 us (0.939)
  local copies, waits for them, and re-layouts: 39.5 us -> 25.6 us
  other arithmetic: 21.9 us -> 10.9 us
  waiting for transfers between devices: 2.94 us -> 8.43 us
  matrix products: 2.54 us -> 6.78 us
  starting transfers between devices: 37.2 us -> 40.9 us
    reduce_sum x6 -> x4, other arithmetic: 11.1 us -> 0.4 us  [block_mean(): field = 0.25 * field.reshape(lead + (rows // 2, 2, cols // 2)).sum(axis=-2)]
    pallas_call x2 -> x0, local copies, waits for them, and re-layouts: 4.87 us -> none  [kernel_sweep(): pl.pallas_call(body, grid=(parts,), in_specs=specs, out_specs=pl.BlockSpe...]
    ppermute x1, starting transfers between devices: 3.11 us -> 7.55 us  [with_halo(): lax.ppermute(tail, axis, [(i, (i + 1) % count) for i in range(ends)])]
    reshape x2, local copies, waits for them, and re-layouts: 4.5 us -> 0.16 us  [block_mean(): field = 0.25 * field.reshape(lead + (rows // 2, 2, cols // 2)).sum(axis=-2)]
    dot_general x0 -> x6, matrix products: none -> 4.09 us  [block_mean(): jnp.einsum('...y,yz->...z', field, pairs, precision=lax.Precision.HIGHEST)]
    ppermute x1, waiting for transfers between devices: 0.01 us -> 3.82 us  [trade(): lax.ppermute(pack(tails), 'gx', [(i, i + 1) for i in range(ends)])]
    slice x5, local copies, waits for them, and re-layouts: 2.76 us -> 0.11 us  [trade(): left = from_left[offset:offset + size].reshape(h.shape)]
  transfers between devices with their start and end apart: 13 -> 13, of which waited for: 3 -> 4; matrix products, arithmetic and copies ran while one was open for 20% -> 8% of each run, Pallas kernels for 13% -> 14%
where the time goes in v3:
time: 170 us; the launch traced here: 169 us
  Pallas kernels  61.4 us (36%)
  starting transfers between devices  40.9 us (24%)
  local copies, waits for them, and re-layouts  25.6 us (15%)
  between operations  14.9 us (9%)
  other arithmetic  10.9 us (6%)
  waiting for transfers between devices  8.43 us (5%)
  matrix products  6.78 us (4%)
    pallas_call x10, Pallas kernels, kernel_sweep(): pl.pallas_call(body, grid=(parts,), in_specs=specs, out_specs=pl.BlockSpe...  44.9 us
    ppermute x4, starting transfers between devices, nearby(): lax.ppermute(cells, 'gx', [(i + step, i) for i in range(count - step)])  12.6 us
    ppermute x4, starting transfers between devices, nearby(): lax.ppermute(cells, 'gx', [(i, i + step) for i in range(count - step)])  12.2 us
    pallas_call x3, Pallas kernels, kernel_operator(): pl.pallas_call(body, grid=(2,), in_specs=[whole(eta_level), whole(react_l...  11 us
    ppermute x1, starting transfers between devices, with_halo(): lax.ppermute(tail, axis, [(i, (i + 1) % count) for i in range(ends)])  7.55 us
    broadcast_in_dim x10, local copies, waits for them, and re-layouts, rows_inside(): jnp.broadcast_to(inside(cells, halo, extent)[0, 0], (extent, cols))  6.7 us
    pallas_call x1, Pallas kernels, kernel_coarse(): pl.pallas_call(body, grid=(parts,), in_specs=specs, out_specs=pl.BlockSpe...  5.58 us
    ppermute x1, starting transfers between devices, trade(): lax.ppermute(pack(heads), 'gx', [(i + 1, i) for i in range(ends)])  4.54 us
  transfers between devices with their start and end apart: 13, of which 4 were waited for; matrix products, arithmetic and copies ran while one was open for 8% of the time, Pallas kernels for 14%

profile of v3, /device:TPU:10, one launch (start us, length us, event | category | flops | bytes accessed | tf_op | source)
XLA Modules:
  0.0 169.0 jit_solution(2602493861669020797)
XLA Ops:
  13.6 4.5 %collective-permute-start.1 = (f32[167936]{0:T(1024)S(1)}, f32[167936]{0:T(1024)S(1)}, u32[]{:S(2)}, u32[]{:S(2)}) collective-permute-start(f32[167936]{0:T(1024)S(1)} %pad_maximum_fusion.3), channel_id=1, source_target_pairs={{1,0},{2,1},{3,2},{4,3},{5,4},{6,5},{7,6},{8,7},{9,8},{10,9},{11,1... | collective-permute-start | bytes 2015240 | tf_op jit(solution)/shard_map/ppermute | solution.py:43
  20.8 3.8 %collective-permute-done = f32[167936]{0:T(1024)S(1)} collective-permute-done((f32[167936]{0:T(1024)}, f32[167936]{0:T(1024)S(1)}, u32[]{:S(2)}, u32[]{:S(2)}) %collective-permute-start) | collective-permute-done | bytes 671776 | tf_op jit(solution)/shard_map/ppermute | solution.py:42
  30.4 5.0 %shard_map.77 = (f32[2,16,14,512]{3,2,1,0:T(8,128)}, f32[2,16,14,512]{3,2,1,0:T(8,128)}, f32[2,16,14,512]{3,2,1,0:T(8,128)}, f32[2,16,14,512]{3,2,1,0:T(8,128)},...) custom-call(f32[16,16,512]{2,1,0:T(8,128)} %pad_maximum_fusion.4.eta_, ...), custom_call_target="tpu_custom_call" | custom-call | tf_op jit(solution)/shard_map/pallas_call | solution.py:266
  37.8 5.7 %shard_map.78.w_ref = f32[2,16,14,512]{3,2,1,0:T(8,128)} custom-call(f32[2,16,16,512]{3,2,1,0:T(8,128)} %get-tuple-element.65.w_ref, f32[2,16,16,512]{3,2,1,0:T(8,128)} %get-tuple-element.66.b_ref, f32[2,16,14,512]{3,2,1,0:T(8,128)} %get-tuple-element.26.fxl_ref, f32[2,16,14,512]{3,2,1,0:T(8,128)} %get-tuple-element.27.fxr_ref, ...), custom_call_target="tpu_custom_call" | custom-call | tf_op jit(solution)/shard_map/pallas_call | solution.py:191
  44.3 6.0 %shard_map.79.w_ref = f32[2,16,12,512]{3,2,1,0:T(8,128)} custom-call(f32[2,16,14,512]{3,2,1,0:T(8,128)} %shard_map.78.w_ref, f32[2,16,16,512]{3,2,1,0:T(8,128)} %get-tuple-element.66.b_ref, f32[2,16,14,512]{3,2,1,0:T(8,128)} %get-tuple-element.26.fxl_ref, f32[2,16,14,512]{3,2,1,0:T(8,128)} %get-tuple-element.27.fxr_ref, ...), custom_call_target="tpu_custom_call" | custom-call | tf_op jit(solution)/shard_map/pallas_call | solution.py:191
  50.9 5.1 %shard_map.80 = f32[2,16,8,512]{3,2,1,0:T(8,128)} custom-call(f32[2,16,12,512]{3,2,1,0:T(8,128)} %shard_map.79.w_ref, f32[2,16,16,512]{3,2,1,0:T(8,128)} %get-tuple-element.66.b_ref, f32[2,16,14,512]{3,2,1,0:T(8,128)} %get-tuple-element.26.fxl_ref, f32[2,16,14,512]{3,2,1,0:T(8,128)} %get-tuple-element.27.fxr_ref, ...), custom_call_target="tpu_custom_call" | custom-call | tf_op jit(solution)/shard_map/pallas_call | solution.py:191
  58.1 7.6 %collective-permute-start.2 = (f32[2,16,4,256]{3,2,1,0:T(4,128)S(1)}, f32[2,16,4,256]{3,2,1,0:T(4,128)S(1)}, u32[]{:S(2)}, u32[]{:S(2)}) collective-permute-start(f32[2,16,4,256]{3,2,1,0:T(4,128)S(1)} %broadcast_multiply_fusion), channel_id=1, source_target_pairs={{0,1},{1,2},{2,3},{3,4},{4,5},{5,6},{6,7},{7,8},{8,9},{9,10},{10,1... | collective-permute-start | bytes 393224 | tf_op jit(solution)/shard_map/ppermute | solution.py:27
  67.8 2.3 %collective-permute-done.3 = f32[2,16,4,256]{3,2,1,0:T(4,128)S(1)} collective-permute-done((f32[2,16,4,256]{3,2,1,0:T(4,128)S(1)}, f32[2,16,4,256]{3,2,1,0:T(4,128)S(1)}, u32[]{:S(2)}, u32[]{:S(2)}) %collective-permute-start.3) | collective-permute-done | bytes 131104 | tf_op jit(solution)/shard_map/ppermute | solution.py:29
  74.2 2.5 %copy.34 = f32[16,16,4,256]{3,2,1,0:T(4,128)} copy(f32[16,16,4,256]{3,2,0,1:T(4,128)} %bitcast.104) | data formatting | bytes 2097152 | tf_op jit(solution)/shard_map/transpose | solution.py:406
  79.8 3.3 %shard_map.81 = (f32[2,16,12,256]{3,2,1,0:T(8,128)}, f32[2,16,12,256]{3,2,1,0:T(8,128)}, f32[2,16,12,256]{3,2,1,0:T(8,128)}, f32[2,16,12,256]{3,2,1,0:T(8,128)},...) custom-call(f32[16,14,256]{2,1,0:T(8,128)} %pad_dynamic-slice_fusion., ...), custom_call_target="tpu_custom_call" | custom-call | tf_op jit(solution)/shard_map/pallas_call | solution.py:266
  83.8 3.1 %shard_map.82.w_ref = f32[2,16,12,256]{3,2,1,0:T(8,128)} custom-call(f32[2,16,12,256]{3,2,1,0:T(8,128)} %pad_maximum_fusion.5.w_ref.b_ref, f32[2,16,12,256]{3,2,1,0:T(8,128)} %pad_maximum_fusion.5.w_ref.b_ref, f32[2,16,12,256]{3,2,1,0:T(8,128)} %get-tuple-element.34.fxl_ref, f32[2,16,12,256]{3,2,1,0:T(8,128)} %get-tuple-element.35.fxr_ref, ...), custom_call_target="tpu_custom_call" | custom-call | tf_op jit(solution)/shard_map/pallas_call | solution.py:191
  87.6 3.6 %shard_map.83.w_ref = f32[2,16,10,256]{3,2,1,0:T(8,128)} custom-call(f32[2,16,12,256]{3,2,1,0:T(8,128)} %shard_map.82.w_ref, f32[2,16,12,256]{3,2,1,0:T(8,128)} %pad_maximum_fusion.5.w_ref.b_ref, f32[2,16,12,256]{3,2,1,0:T(8,128)} %get-tuple-element.34.fxl_ref, f32[2,16,12,256]{3,2,1,0:T(8,128)} %get-tuple-element.35.fxr_ref, ...), custom_call_target="tpu_custom_call" | custom-call | tf_op jit(solution)/shard_map/pallas_call | solution.py:191
  91.8 3.1 %shard_map.84 = f32[2,16,4,256]{3,2,1,0:T(4,128)} custom-call(f32[2,16,10,256]{3,2,1,0:T(8,128)} %shard_map.83.w_ref, f32[2,16,12,256]{3,2,1,0:T(8,128)} %pad_maximum_fusion.5.w_ref.b_ref, f32[2,16,12,256]{3,2,1,0:T(8,128)} %get-tuple-element.34.fxl_ref, f32[2,16,12,256]{3,2,1,0:T(8,128)} %get-tuple-element.35.fxr_ref, ...), custom_call_target="tpu_custom_call" | custom-call | tf_op jit(solution)/shard_map/pallas_call | solution.py:191
  96.2 4.2 %collective-permute-start.10 = (f32[2,16,2,128]{3,2,1,0:T(2,128)S(1)}, f32[2,16,2,128]{3,2,1,0:T(2,128)S(1)}, u32[]{:S(2)}, u32[]{:S(2)}) collective-permute-start(f32[2,16,2,128]{3,2,1,0:T(2,128)S(1)} %copy_multiply_fusion), channel_id=1, source_target_pairs={{3,0},{4,1},{5,2},{6,3},{7,4},{8,5},{9,6},{10,7},{11,8},{12,9},{13... | collective-permute-start | bytes 98312 | tf_op jit(solution)/shard_map/ppermute | solution.py:383
  102.3 3.9 %collective-permute-start.4 = (f32[2,16,2,128]{3,2,1,0:T(2,128)S(1)}, f32[2,16,2,128]{3,2,1,0:T(2,128)S(1)}, u32[]{:S(2)}, u32[]{:S(2)}) collective-permute-start(f32[2,16,2,128]{3,2,1,0:T(2,128)S(1)} %copy_multiply_fusion), channel_id=1, source_target_pairs={{0,4},{1,5},{2,6},{3,7},{4,8},{5,9},{6,10},{7,11},{8,12},{9,13},{1... | collective-permute-start | bytes 98312 | tf_op jit(solution)/shard_map/ppermute | solution.py:382
  106.3 2.3 %collective-permute-start.5 = (f32[2,16,2,128]{3,2,1,0:T(2,128)S(1)}, f32[2,16,2,128]{3,2,1,0:T(2,128)S(1)}, u32[]{:S(2)}, u32[]{:S(2)}) collective-permute-start(f32[2,16,2,128]{3,2,1,0:T(2,128)S(1)} %copy_multiply_fusion), channel_id=1, source_target_pairs={{0,3},{1,4},{2,5},{3,6},{4,7},{5,8},{6,9},{7,10},{8,11},{9,12},{10... | collective-permute-start | bytes 98312 | tf_op jit(solution)/shard_map/ppermute | solution.py:382
  108.6 4.1 %collective-permute-start.6 = (f32[2,16,2,128]{3,2,1,0:T(2,128)S(1)}, f32[2,16,2,128]{3,2,1,0:T(2,128)S(1)}, u32[]{:S(2)}, u32[]{:S(2)}) collective-permute-start(f32[2,16,2,128]{3,2,1,0:T(2,128)S(1)} %copy_multiply_fusion), channel_id=1, source_target_pairs={{0,2},{1,3},{2,4},{3,5},{4,6},{5,7},{6,8},{7,9},{8,10},{9,11},{10,... | collective-permute-start | bytes 98312 | tf_op jit(solution)/shard_map/ppermute | solution.py:382
  115.8 4.5 %collective-permute-start.8 = (f32[2,16,2,128]{3,2,1,0:T(2,128)S(1)}, f32[2,16,2,128]{3,2,1,0:T(2,128)S(1)}, u32[]{:S(2)}, u32[]{:S(2)}) collective-permute-start(f32[2,16,2,128]{3,2,1,0:T(2,128)S(1)} %copy_multiply_fusion), channel_id=1, source_target_pairs={{1,0},{2,1},{3,2},{4,3},{5,4},{6,5},{7,6},{8,7},{9,8},{10,9},{11,1... | collective-permute-start | bytes 98312 | tf_op jit(solution)/shard_map/ppermute | solution.py:383
  122.9 2.7 %shard_map.85 = (f32[2,16,18,128]{3,2,1,0:T(8,128)}, f32[2,16,18,128]{3,2,1,0:T(8,128)}, f32[2,16,18,128]{3,2,1,0:T(8,128)}, f32[2,16,18,128]{3,2,1,0:T(8,128)},...) custom-call(f32[16,20,128]{2,1,0:T(8,128)} %pad_dynamic-slice_fusion., ...), custom_call_target="tpu_custom_call" | custom-call | tf_op jit(solution)/shard_map/pallas_call | solution.py:266
  129.0 5.6 %shard_map.86 = f32[2,16,18,128]{3,2,1,0:T(8,128)} custom-call(f32[2,16,18,128]{3,2,1,0:T(8,128)} %concatenate.35.b_ref, f32[2,16,18,128]{3,2,1,0:T(8,128)} %get-tuple-element.42.fxl_ref, f32[2,16,18,128]{3,2,1,0:T(8,128)} %get-tuple-element.43.fxr_ref, f32[2,16,18,128]{3,2,1,0:T(8,128)} %get-tuple-element.44.fyl_ref, ...), custom_call_target="tpu_custom_call" | custom-call | tf_op jit(solution)/shard_map/pallas_call | solution.py:285
  138.1 3.4 %shard_map.87.w_ref = f32[2,16,8,256]{3,2,1,0:T(8,128)} custom-call(f32[2,16,10,256]{3,2,1,0:T(8,128)} %slice_add_fusion.w_ref, f32[2,16,12,256]{3,2,1,0:T(8,128)} %pad_maximum_fusion.5.w_ref.b_ref, f32[2,16,12,256]{3,2,1,0:T(8,128)} %get-tuple-element.34.fxl_ref, f32[2,16,12,256]{3,2,1,0:T(8,128)} %get-tuple-element.35.fxr_ref, ...), custom_call_target="tpu_custom_call" | custom-call | tf_op jit(solution)/shard_map/pallas_call | solution.py:191
  142.2 3.3 %shard_map.88 = f32[2,16,6,256]{3,2,1,0:T(8,128)} custom-call(f32[2,16,8,256]{3,2,1,0:T(8,128)} %shard_map.87.w_ref, f32[2,16,12,256]{3,2,1,0:T(8,128)} %pad_maximum_fusion.5.w_ref.b_ref, f32[2,16,12,256]{3,2,1,0:T(8,128)} %get-tuple-element.34.fxl_ref, f32[2,16,12,256]{3,2,1,0:T(8,128)} %get-tuple-element.35.fxr_ref, ...), custom_call_target="tpu_custom_call" | custom-call | tf_op jit(solution)/shard_map/pallas_call | solution.py:191
  149.2 6.0 %shard_map.89.w_ref = f32[2,16,10,512]{3,2,1,0:T(8,128)} custom-call(f32[2,16,12,512]{3,2,1,0:T(8,128)} %copy_add_fusion.w_ref, f32[2,16,16,512]{3,2,1,0:T(8,128)} %get-tuple-element.66.b_ref, f32[2,16,14,512]{3,2,1,0:T(8,128)} %get-tuple-element.26.fxl_ref, f32[2,16,14,512]{3,2,1,0:T(8,128)} %get-tuple-element.27.fxr_ref, ...), custom_call_target="tpu_custom_call" | custom-call | tf_op jit(solution)/shard_map/pallas_call | solution.py:191
  155.2 5.6 %shard_map.90 = f32[2,16,8,512]{3,2,1,0:T(8,128)} custom-call(f32[2,16,10,512]{3,2,1,0:T(8,128)} %shard_map.89.w_ref, f32[2,16,16,512]{3,2,1,0:T(8,128)} %get-tuple-element.66.b_ref, f32[2,16,14,512]{3,2,1,0:T(8,128)} %get-tuple-element.26.fxl_ref, f32[2,16,14,512]{3,2,1,0:T(8,128)} %get-tuple-element.27.fxr_ref, ...), custom_call_target="tpu_custom_call" | custom-call | tf_op jit(solution)/shard_map/pallas_call | solution.py:191
  (154 shorter events, 53.0 us)
Async XLA Ops:
  7.2 3.1 %copy-start.2 = (f32[2,16,8,512]{3,2,1,0:T(8,128)S(1)}, f32[2,16,8,512]{3,2,1,0:T(8,128)}, u32[]{:S(2)}) copy-start(f32[2,16,8,512]{3,2,1,0:T(8,128)} %param.6) | copy-start | bytes 1572868
  7.2 63.8 %all-gather.4.cloned.1.call-start = ((), (), s32[]{:S(2)}) async-start(), calls=%async_computation | async-start | bytes 1566720 | tf_op jit(solution)/shard_map/all_gather | solution.py:399
  8.7 12.0 %copy-start.6 = (f32[16,8,512]{2,1,0:T(8,128)}, f32[16,8,512]{2,1,0:T(8,128)S(1)}, u32[]{:S(2)}) copy-start(f32[16,8,512]{2,1,0:T(8,128)S(1)} %multiply_add_fusion) | copy-start | bytes 786436
  8.7 1.7 copy-start.4
  11.4 13.3 %collective-permute-start = (f32[167936]{0:T(1024)}, f32[167936]{0:T(1024)S(1)}, u32[]{:S(2)}, u32[]{:S(2)}) collective-permute-start(f32[167936]{0:T(1024)} %pad_maximum_fusion.2), channel_id=1, source_target_pairs={{0,1},{1,2},{2,3},{3,4},{4,5},{5,6},{6,7},{7,8},{8,9},{9,10},{10,1... | collective-permute-start | bytes 2015240 | tf_op jit(solution)/shard_map/ppermute | solution.py:42
  13.6 12.9 %collective-permute-start.1 = (f32[167936]{0:T(1024)S(1)}, f32[167936]{0:T(1024)S(1)}, u32[]{:S(2)}, u32[]{:S(2)}) collective-permute-start(f32[167936]{0:T(1024)S(1)} %pad_maximum_fusion.3), channel_id=1, source_target_pairs={{1,0},{2,1},{3,2},{4,3},{5,4},{6,5},{7,6},{8,7},{9,8},{10,9},{11,1... | collective-permute-start | bytes 2015240 | tf_op jit(solution)/shard_map/ppermute | solution.py:43
  18.1 1.7 %copy-start.11 = (s32[256]{0:T(256)}, s32[256]{0:T(256)S(1)}, u32[]{:S(2)}) copy-start(s32[256]{0:T(256)S(1)} %and_select_fusion) | copy-start | bytes 3076
  28.6 6.8 %copy-start.3 = (f32[2,16,8,512]{3,2,1,0:T(8,128)S(1)}, f32[2,16,8,512]{3,2,1,0:T(8,128)}, u32[]{:S(2)}) copy-start(f32[2,16,8,512]{3,2,1,0:T(8,128)} %param.7) | copy-start | bytes 1572868
  50.9 5.1 %copy-start.9 = (s32[512]{0:T(512)S(1)}, s32[512]{0:T(512)}, u32[]{:S(2)}) copy-start(s32[512]{0:T(512)} %copy-done.8) | copy-start | bytes 6148
  58.1 9.7 %collective-permute-start.2 = (f32[2,16,4,256]{3,2,1,0:T(4,128)S(1)}, f32[2,16,4,256]{3,2,1,0:T(4,128)S(1)}, u32[]{:S(2)}, u32[]{:S(2)}) collective-permute-start(f32[2,16,4,256]{3,2,1,0:T(4,128)S(1)} %broadcast_multiply_fusion), channel_id=1, source_target_pairs={{0,1},{1,2},{2,3},{3,4},{4,5},{5,6},{6,7},{7,8},{8,9},{9,10},{10,1... | collective-permute-start | bytes 393224 | tf_op jit(solution)/shard_map/ppermute | solution.py:27
  65.6 4.4 %collective-permute-start.3 = (f32[2,16,4,256]{3,2,1,0:T(4,128)S(1)}, f32[2,16,4,256]{3,2,1,0:T(4,128)S(1)}, u32[]{:S(2)}, u32[]{:S(2)}) collective-permute-start(f32[2,16,4,256]{3,2,1,0:T(4,128)S(1)} %broadcast_multiply_fusion), channel_id=1, source_target_pairs={{1,0},{2,1},{3,2},{4,3},{5,4},{6,5},{7,6},{8,7},{9,8},{10,9},{11,1... | collective-permute-start | bytes 393224 | tf_op jit(solution)/shard_map/ppermute | solution.py:29
  91.8 3.1 %copy-start.12 = (s32[256]{0:T(256)S(1)}, s32[256]{0:T(256)}, u32[]{:S(2)}) copy-start(s32[256]{0:T(256)} %copy-done.11) | copy-start | bytes 3076
  96.2 17.6 %collective-permute-start.10 = (f32[2,16,2,128]{3,2,1,0:T(2,128)S(1)}, f32[2,16,2,128]{3,2,1,0:T(2,128)S(1)}, u32[]{:S(2)}, u32[]{:S(2)}) collective-permute-start(f32[2,16,2,128]{3,2,1,0:T(2,128)S(1)} %copy_multiply_fusion), channel_id=1, source_target_pairs={{3,0},{4,1},{5,2},{6,3},{7,4},{8,5},{9,6},{10,7},{11,8},{12,9},{13... | collective-permute-start | bytes 98312 | tf_op jit(solution)/shard_map/ppermute | solution.py:383
  100.4 15.4 %collective-permute-start.11 = (f32[2,16,2,128]{3,2,1,0:T(2,128)S(1)}, f32[2,16,2,128]{3,2,1,0:T(2,128)S(1)}, u32[]{:S(2)}, u32[]{:S(2)}) collective-permute-start(f32[2,16,2,128]{3,2,1,0:T(2,128)S(1)} %copy_multiply_fusion), channel_id=1, source_target_pairs={{4,0},{5,1},{6,2},{7,3},{8,4},{9,5},{10,6},{11,7},{12,8},{13,9},{1... | collective-permute-start | bytes 98312 | tf_op jit(solution)/shard_map/ppermute | solution.py:383
  102.3 18.0 %collective-permute-start.4 = (f32[2,16,2,128]{3,2,1,0:T(2,128)S(1)}, f32[2,16,2,128]{3,2,1,0:T(2,128)S(1)}, u32[]{:S(2)}, u32[]{:S(2)}) collective-permute-start(f32[2,16,2,128]{3,2,1,0:T(2,128)S(1)} %copy_multiply_fusion), channel_id=1, source_target_pairs={{0,4},{1,5},{2,6},{3,7},{4,8},{5,9},{6,10},{7,11},{8,12},{9,13},{1... | collective-permute-start | bytes 98312 | tf_op jit(solution)/shard_map/ppermute | solution.py:382
  106.3 19.3 %collective-permute-start.5 = (f32[2,16,2,128]{3,2,1,0:T(2,128)S(1)}, f32[2,16,2,128]{3,2,1,0:T(2,128)S(1)}, u32[]{:S(2)}, u32[]{:S(2)}) collective-permute-start(f32[2,16,2,128]{3,2,1,0:T(2,128)S(1)} %copy_multiply_fusion), channel_id=1, source_target_pairs={{0,3},{1,4},{2,5},{3,6},{4,7},{5,8},{6,9},{7,10},{8,11},{9,12},{10... | collective-permute-start | bytes 98312 | tf_op jit(solution)/shard_map/ppermute | solution.py:382
  108.6 17.0 %collective-permute-start.6 = (f32[2,16,2,128]{3,2,1,0:T(2,128)S(1)}, f32[2,16,2,128]{3,2,1,0:T(2,128)S(1)}, u32[]{:S(2)}, u32[]{:S(2)}) collective-permute-start(f32[2,16,2,128]{3,2,1,0:T(2,128)S(1)} %copy_multiply_fusion), channel_id=1, source_target_pairs={{0,2},{1,3},{2,4},{3,5},{4,6},{5,7},{6,8},{7,9},{8,10},{9,11},{10,... | collective-permute-start | bytes 98312 | tf_op jit(solution)/shard_map/ppermute | solution.py:382
  113.8 11.7 %collective-permute-start.7 = (f32[2,16,2,128]{3,2,1,0:T(2,128)S(1)}, f32[2,16,2,128]{3,2,1,0:T(2,128)S(1)}, u32[]{:S(2)}, u32[]{:S(2)}) collective-permute-start(f32[2,16,2,128]{3,2,1,0:T(2,128)S(1)} %copy_multiply_fusion), channel_id=1, source_target_pairs={{0,1},{1,2},{2,3},{3,4},{4,5},{5,6},{6,7},{7,8},{8,9},{9,10},{10,1... | collective-permute-start | bytes 98312 | tf_op jit(solution)/shard_map/ppermute | solution.py:382
  115.8 9.8 %collective-permute-start.8 = (f32[2,16,2,128]{3,2,1,0:T(2,128)S(1)}, f32[2,16,2,128]{3,2,1,0:T(2,128)S(1)}, u32[]{:S(2)}, u32[]{:S(2)}) collective-permute-start(f32[2,16,2,128]{3,2,1,0:T(2,128)S(1)} %copy_multiply_fusion), channel_id=1, source_target_pairs={{1,0},{2,1},{3,2},{4,3},{5,4},{6,5},{7,6},{8,7},{9,8},{10,9},{11,1... | collective-permute-start | bytes 98312 | tf_op jit(solution)/shard_map/ppermute | solution.py:383
  120.3 5.8 %collective-permute-start.9 = (f32[2,16,2,128]{3,2,1,0:T(2,128)S(1)}, f32[2,16,2,128]{3,2,1,0:T(2,128)S(1)}, u32[]{:S(2)}, u32[]{:S(2)}) collective-permute-start(f32[2,16,2,128]{3,2,1,0:T(2,128)S(1)} %copy_multiply_fusion), channel_id=1, source_target_pairs={{2,0},{3,1},{4,2},{5,3},{6,4},{7,5},{8,6},{9,7},{10,8},{11,9},{12,... | collective-permute-start | bytes 98312 | tf_op jit(solution)/shard_map/ppermute | solution.py:383
  134.6 1.9 %copy-start.1 = (f32[2,16,10,256]{3,2,1,0:T(8,128)S(1)}, f32[2,16,10,256]{3,2,1,0:T(8,128)}, u32[]{:S(2)}) copy-start(f32[2,16,10,256]{3,2,1,0:T(8,128)} %shard_map.83.w_ref) | copy-start | bytes 983044
  145.5 1.5 copy-start
  155.2 5.6 %copy-start.7 = (f32[2,8,512]{2,1,0:T(8,128)S(1)}, f32[2,8,512]{2,1,0:T(8,128)}, u32[]{:S(2)}) copy-start(f32[2,8,512]{2,1,0:T(8,128)} %param.11) | copy-start | bytes 98308
  155.2 5.6 %copy-start.10 = (pred[8,512]{1,0:T(8,128)(4,1)S(1)}, pred[8,512]{1,0:T(8,128)(4,1)}, u32[]{:S(2)}) copy-start(pred[8,512]{1,0:T(8,128)(4,1)} %get-tuple-element.51) | copy-start | bytes 12292
  (3 other events, 2.9 us)
Sparse Core Ops, SparseCore 0:
  20.8 38.6 all-gather.3

commit v4 on v3

--- a/solution.py
+++ b/solution.py
@@ -391,10 +391,8 @@
     react_pair = react_fine[:2]
 
     eta_1 = block_mean(viscosity, 2)
-    eta_2 = block_mean(viscosity, 4)
     react_1 = block_mean(react_pair, 2)
-    react_2 = block_mean(react_pair, 4)
-    pieces = [eta_1, react_1, eta_2, react_2]
+    pieces = [eta_1, react_1]
     packed = jnp.concatenate([p.reshape(-1) for p in pieces])
     gathered = lax.all_gather(packed[None], "gx", axis=0, tiled=True)
     count = gathered.shape[0]
@@ -404,7 +402,9 @@
         block = gathered[:, offset : offset + p.size].reshape((count,) + p.shape)
         offset += p.size
         unpacked.append(jnp.moveaxis(block, 0, 1).reshape((p.shape[0], count * p.shape[1], p.shape[2])))
-    eta_1_all, react_1_all, eta_2_all, react_2_all = unpacked
+    eta_1_all, react_1_all = unpacked
+    eta_2_all = block_mean(eta_1_all, 2)
+    react_2_all = block_mean(react_1_all, 2)
 
     halo = 4
     eta_wide, guess_wide, misfit_wide, react_wide = trade(

time: 170 us -> 169 us (level)
  local copies, waits for them, and re-layouts: 25.6 us -> 22.5 us
    transpose x4, local copies, waits for them, and re-layouts: 2.63 us -> 0.53 us  [shards(): jnp.moveaxis(block, 0, 1)]
    unnamed x40 -> x36, local copies, waits for them, and re-layouts: 3.57 us -> 3.05 us
  transfers between devices with their start and end apart: 13 -> 13, of which waited for: 4 -> 4; matrix products, arithmetic and copies ran while one was open for 8% -> 9% of each run, Pallas kernels for 14% -> 14%
where the time goes in v4:
time: 169 us; the launch traced here: 168 us
  Pallas kernels  61.3 us (36%)
  starting transfers between devices  41.6 us (25%)
  local copies, waits for them, and re-layouts  22.5 us (13%)
  between operations  14.8 us (9%)
  other arithmetic  11.6 us (7%)
  waiting for transfers between devices  8.86 us (5%)
  matrix products  7.82 us (5%)
    pallas_call x10, Pallas kernels, kernel_sweep(): pl.pallas_call(body, grid=(parts,), in_specs=specs, out_specs=pl.BlockSpe...  44.7 us
    ppermute x4, starting transfers between devices, nearby(): lax.ppermute(cells, 'gx', [(i + step, i) for i in range(count - step)])  13 us
    ppermute x4, starting transfers between devices, nearby(): lax.ppermute(cells, 'gx', [(i, i + step) for i in range(count - step)])  11.7 us
    pallas_call x3, Pallas kernels, kernel_operator(): pl.pallas_call(body, grid=(2,), in_specs=[whole(eta_level), whole(react_l...  11 us
    ppermute x1, starting transfers between devices, with_halo(): lax.ppermute(tail, axis, [(i, (i + 1) % count) for i in range(ends)])  8.33 us
    broadcast_in_dim x10, local copies, waits for them, and re-layouts, rows_inside(): jnp.broadcast_to(inside(cells, halo, extent)[0, 0], (extent, cols))  6.71 us
    pallas_call x1, Pallas kernels, kernel_coarse(): pl.pallas_call(body, grid=(parts,), in_specs=specs, out_specs=pl.BlockSpe...  5.58 us
    dot_general x6, matrix products, block_mean(): jnp.einsum('...y,yz->...z', field, pairs, precision=lax.Precision.HIGHEST)  5.12 us
  transfers between devices with their start and end apart: 13, of which 4 were waited for; matrix products, arithmetic and copies ran while one was open for 9% of the time, Pallas kernels for 14%

profile of v4, /device:TPU:10, one launch (start us, length us, event | category | flops | bytes accessed | tf_op | source)
XLA Modules:
  0.0 168.5 jit_solution(8011631506710671038)
XLA Ops:
  14.3 4.5 %collective-permute-start.1 = (f32[167936]{0:T(1024)S(1)}, f32[167936]{0:T(1024)S(1)}, u32[]{:S(2)}, u32[]{:S(2)}) collective-permute-start(f32[167936]{0:T(1024)S(1)} %pad_maximum_fusion.3), channel_id=1, source_target_pairs={{1,0},{2,1},{3,2},{4,3},{5,4},{6,5},{7,6},{8,7},{9,8},{10,9},{11,1... | collective-permute-start | bytes 2015240 | tf_op jit(solution)/shard_map/ppermute | solution.py:43
  20.9 4.5 %collective-permute-done = f32[167936]{0:T(1024)S(1)} collective-permute-done((f32[167936]{0:T(1024)}, f32[167936]{0:T(1024)S(1)}, u32[]{:S(2)}, u32[]{:S(2)}) %collective-permute-start) | collective-permute-done | bytes 671776 | tf_op jit(solution)/shard_map/ppermute | solution.py:42
  31.1 5.0 %shard_map.77 = (f32[2,16,14,512]{3,2,1,0:T(8,128)}, f32[2,16,14,512]{3,2,1,0:T(8,128)}, f32[2,16,14,512]{3,2,1,0:T(8,128)}, f32[2,16,14,512]{3,2,1,0:T(8,128)},...) custom-call(f32[16,16,512]{2,1,0:T(8,128)} %pad_maximum_fusion.4.eta_, ...), custom_call_target="tpu_custom_call" | custom-call | tf_op jit(solution)/shard_map/pallas_call | solution.py:266
  38.6 5.7 %shard_map.78.w_ref = f32[2,16,14,512]{3,2,1,0:T(8,128)} custom-call(f32[2,16,16,512]{3,2,1,0:T(8,128)} %get-tuple-element.65.w_ref, f32[2,16,16,512]{3,2,1,0:T(8,128)} %get-tuple-element.66.b_ref, f32[2,16,14,512]{3,2,1,0:T(8,128)} %get-tuple-element.26.fxl_ref, f32[2,16,14,512]{3,2,1,0:T(8,128)} %get-tuple-element.27.fxr_ref, ...), custom_call_target="tpu_custom_call" | custom-call | tf_op jit(solution)/shard_map/pallas_call | solution.py:191
  45.0 5.9 %shard_map.79.w_ref = f32[2,16,12,512]{3,2,1,0:T(8,128)} custom-call(f32[2,16,14,512]{3,2,1,0:T(8,128)} %shard_map.78.w_ref, f32[2,16,16,512]{3,2,1,0:T(8,128)} %get-tuple-element.66.b_ref, f32[2,16,14,512]{3,2,1,0:T(8,128)} %get-tuple-element.26.fxl_ref, f32[2,16,14,512]{3,2,1,0:T(8,128)} %get-tuple-element.27.fxr_ref, ...), custom_call_target="tpu_custom_call" | custom-call | tf_op jit(solution)/shard_map/pallas_call | solution.py:191
  51.5 5.1 %shard_map.80 = f32[2,16,8,512]{3,2,1,0:T(8,128)} custom-call(f32[2,16,12,512]{3,2,1,0:T(8,128)} %shard_map.79.w_ref, f32[2,16,16,512]{3,2,1,0:T(8,128)} %get-tuple-element.66.b_ref, f32[2,16,14,512]{3,2,1,0:T(8,128)} %get-tuple-element.26.fxl_ref, f32[2,16,14,512]{3,2,1,0:T(8,128)} %get-tuple-element.27.fxr_ref, ...), custom_call_target="tpu_custom_call" | custom-call | tf_op jit(solution)/shard_map/pallas_call | solution.py:191
  58.7 8.3 %collective-permute-start.2 = (f32[2,16,4,256]{3,2,1,0:T(4,128)S(1)}, f32[2,16,4,256]{3,2,1,0:T(4,128)S(1)}, u32[]{:S(2)}, u32[]{:S(2)}) collective-permute-start(f32[2,16,4,256]{3,2,1,0:T(4,128)S(1)} %broadcast_multiply_fusion.1), channel_id=1, source_target_pairs={{0,1},{1,2},{2,3},{3,4},{4,5},{5,6},{6,7},{7,8},{8,9},{9,10},{10,1... | collective-permute-start | bytes 393224 | tf_op jit(solution)/shard_map/ppermute | solution.py:27
  69.2 2.3 %collective-permute-done.3 = f32[2,16,4,256]{3,2,1,0:T(4,128)S(1)} collective-permute-done((f32[2,16,4,256]{3,2,1,0:T(4,128)S(1)}, f32[2,16,4,256]{3,2,1,0:T(4,128)S(1)}, u32[]{:S(2)}, u32[]{:S(2)}) %collective-permute-start.3) | collective-permute-done | bytes 131104 | tf_op jit(solution)/shard_map/ppermute | solution.py:29
  78.3 3.3 %shard_map.81 = (f32[2,16,12,256]{3,2,1,0:T(8,128)}, f32[2,16,12,256]{3,2,1,0:T(8,128)}, f32[2,16,12,256]{3,2,1,0:T(8,128)}, f32[2,16,12,256]{3,2,1,0:T(8,128)},...) custom-call(f32[16,14,256]{2,1,0:T(8,128)} %pad_dynamic-slice_fusion., ...), custom_call_target="tpu_custom_call" | custom-call | tf_op jit(solution)/shard_map/pallas_call | solution.py:266
  82.2 3.1 %shard_map.82.w_ref = f32[2,16,12,256]{3,2,1,0:T(8,128)} custom-call(f32[2,16,12,256]{3,2,1,0:T(8,128)} %pad_maximum_fusion.5.w_ref.b_ref, f32[2,16,12,256]{3,2,1,0:T(8,128)} %pad_maximum_fusion.5.w_ref.b_ref, f32[2,16,12,256]{3,2,1,0:T(8,128)} %get-tuple-element.34.fxl_ref, f32[2,16,12,256]{3,2,1,0:T(8,128)} %get-tuple-element.35.fxr_ref, ...), custom_call_target="tpu_custom_call" | custom-call | tf_op jit(solution)/shard_map/pallas_call | solution.py:191
  86.0 3.6 %shard_map.83.w_ref = f32[2,16,10,256]{3,2,1,0:T(8,128)} custom-call(f32[2,16,12,256]{3,2,1,0:T(8,128)} %shard_map.82.w_ref, f32[2,16,12,256]{3,2,1,0:T(8,128)} %pad_maximum_fusion.5.w_ref.b_ref, f32[2,16,12,256]{3,2,1,0:T(8,128)} %get-tuple-element.34.fxl_ref, f32[2,16,12,256]{3,2,1,0:T(8,128)} %get-tuple-element.35.fxr_ref, ...), custom_call_target="tpu_custom_call" | custom-call | tf_op jit(solution)/shard_map/pallas_call | solution.py:191
  90.3 3.1 %shard_map.84 = f32[2,16,4,256]{3,2,1,0:T(4,128)} custom-call(f32[2,16,10,256]{3,2,1,0:T(8,128)} %shard_map.83.w_ref, f32[2,16,12,256]{3,2,1,0:T(8,128)} %pad_maximum_fusion.5.w_ref.b_ref, f32[2,16,12,256]{3,2,1,0:T(8,128)} %get-tuple-element.34.fxl_ref, f32[2,16,12,256]{3,2,1,0:T(8,128)} %get-tuple-element.35.fxr_ref, ...), custom_call_target="tpu_custom_call" | custom-call | tf_op jit(solution)/shard_map/pallas_call | solution.py:191
  94.6 4.4 %collective-permute-start.10 = (f32[2,16,2,128]{3,2,1,0:T(2,128)S(1)}, f32[2,16,2,128]{3,2,1,0:T(2,128)S(1)}, u32[]{:S(2)}, u32[]{:S(2)}) collective-permute-start(f32[2,16,2,128]{3,2,1,0:T(2,128)S(1)} %copy_multiply_fusion), channel_id=1, source_target_pairs={{3,0},{4,1},{5,2},{6,3},{7,4},{8,5},{9,6},{10,7},{11,8},{12,9},{13... | collective-permute-start | bytes 98312 | tf_op jit(solution)/shard_map/ppermute | solution.py:383
  100.9 3.9 %collective-permute-start.4 = (f32[2,16,2,128]{3,2,1,0:T(2,128)S(1)}, f32[2,16,2,128]{3,2,1,0:T(2,128)S(1)}, u32[]{:S(2)}, u32[]{:S(2)}) collective-permute-start(f32[2,16,2,128]{3,2,1,0:T(2,128)S(1)} %copy_multiply_fusion), channel_id=1, source_target_pairs={{0,4},{1,5},{2,6},{3,7},{4,8},{5,9},{6,10},{7,11},{8,12},{9,13},{1... | collective-permute-start | bytes 98312 | tf_op jit(solution)/shard_map/ppermute | solution.py:382
  106.8 4.0 %collective-permute-start.6 = (f32[2,16,2,128]{3,2,1,0:T(2,128)S(1)}, f32[2,16,2,128]{3,2,1,0:T(2,128)S(1)}, u32[]{:S(2)}, u32[]{:S(2)}) collective-permute-start(f32[2,16,2,128]{3,2,1,0:T(2,128)S(1)} %copy_multiply_fusion), channel_id=1, source_target_pairs={{0,2},{1,3},{2,4},{3,5},{4,6},{5,7},{6,8},{7,9},{8,10},{9,11},{10,... | collective-permute-start | bytes 98312 | tf_op jit(solution)/shard_map/ppermute | solution.py:382
  115.2 4.5 %collective-permute-start.8 = (f32[2,16,2,128]{3,2,1,0:T(2,128)S(1)}, f32[2,16,2,128]{3,2,1,0:T(2,128)S(1)}, u32[]{:S(2)}, u32[]{:S(2)}) collective-permute-start(f32[2,16,2,128]{3,2,1,0:T(2,128)S(1)} %copy_multiply_fusion), channel_id=1, source_target_pairs={{1,0},{2,1},{3,2},{4,3},{5,4},{6,5},{7,6},{8,7},{9,8},{10,9},{11,1... | collective-permute-start | bytes 98312 | tf_op jit(solution)/shard_map/ppermute | solution.py:383
  119.8 2.1 %collective-permute-start.9 = (f32[2,16,2,128]{3,2,1,0:T(2,128)S(1)}, f32[2,16,2,128]{3,2,1,0:T(2,128)S(1)}, u32[]{:S(2)}, u32[]{:S(2)}) collective-permute-start(f32[2,16,2,128]{3,2,1,0:T(2,128)S(1)} %copy_multiply_fusion), channel_id=1, source_target_pairs={{2,0},{3,1},{4,2},{5,3},{6,4},{7,5},{8,6},{9,7},{10,8},{11,9},{12,... | collective-permute-start | bytes 98312 | tf_op jit(solution)/shard_map/ppermute | solution.py:383
  122.5 2.7 %shard_map.85 = (f32[2,16,18,128]{3,2,1,0:T(8,128)}, f32[2,16,18,128]{3,2,1,0:T(8,128)}, f32[2,16,18,128]{3,2,1,0:T(8,128)}, f32[2,16,18,128]{3,2,1,0:T(8,128)},...) custom-call(f32[16,20,128]{2,1,0:T(8,128)} %pad_dynamic-slice_fusion., ...), custom_call_target="tpu_custom_call" | custom-call | tf_op jit(solution)/shard_map/pallas_call | solution.py:266
  125.6 2.2 %concatenate.35.b_ref = f32[2,16,18,128]{3,2,1,0:T(8,128)} concatenate(f32[2,16,2,128]{3,2,1,0:T(2,128)S(1)} %collective-permute-done.4, f32[2,16,2,128]{3,2,1,0:T(2,128)S(1)} %collective-permute-done.5, f32[2,16,2,128]{3,2,1,0:T(2,128)S(1)} %collective-permute-done.6, f32[2,16,2,128]{3,2,1,0:T(2,128)S(1)} %collective-permute-done.7, f32[2,16,2,128]{3,2,1,0:T(2,128)S(1)} %copy_multiply_fusion, ...), dimensions={2} | concatenate | bytes 589824 | tf_op jit(solution)/shard_map/concatenate | solution.py:384
  128.4 5.6 %shard_map.86 = f32[2,16,18,128]{3,2,1,0:T(8,128)} custom-call(f32[2,16,18,128]{3,2,1,0:T(8,128)} %concatenate.35.b_ref, f32[2,16,18,128]{3,2,1,0:T(8,128)} %get-tuple-element.42.fxl_ref, f32[2,16,18,128]{3,2,1,0:T(8,128)} %get-tuple-element.43.fxr_ref, f32[2,16,18,128]{3,2,1,0:T(8,128)} %get-tuple-element.44.fyl_ref, ...), custom_call_target="tpu_custom_call" | custom-call | tf_op jit(solution)/shard_map/pallas_call | solution.py:285
  137.5 3.4 %shard_map.87.w_ref = f32[2,16,8,256]{3,2,1,0:T(8,128)} custom-call(f32[2,16,10,256]{3,2,1,0:T(8,128)} %slice_add_fusion.w_ref, f32[2,16,12,256]{3,2,1,0:T(8,128)} %pad_maximum_fusion.5.w_ref.b_ref, f32[2,16,12,256]{3,2,1,0:T(8,128)} %get-tuple-element.34.fxl_ref, f32[2,16,12,256]{3,2,1,0:T(8,128)} %get-tuple-element.35.fxr_ref, ...), custom_call_target="tpu_custom_call" | custom-call | tf_op jit(solution)/shard_map/pallas_call | solution.py:191
  141.6 3.3 %shard_map.88 = f32[2,16,6,256]{3,2,1,0:T(8,128)} custom-call(f32[2,16,8,256]{3,2,1,0:T(8,128)} %shard_map.87.w_ref, f32[2,16,12,256]{3,2,1,0:T(8,128)} %pad_maximum_fusion.5.w_ref.b_ref, f32[2,16,12,256]{3,2,1,0:T(8,128)} %get-tuple-element.34.fxl_ref, f32[2,16,12,256]{3,2,1,0:T(8,128)} %get-tuple-element.35.fxr_ref, ...), custom_call_target="tpu_custom_call" | custom-call | tf_op jit(solution)/shard_map/pallas_call | solution.py:191
  148.7 6.0 %shard_map.89.w_ref = f32[2,16,10,512]{3,2,1,0:T(8,128)} custom-call(f32[2,16,12,512]{3,2,1,0:T(8,128)} %copy_add_fusion.w_ref, f32[2,16,16,512]{3,2,1,0:T(8,128)} %get-tuple-element.66.b_ref, f32[2,16,14,512]{3,2,1,0:T(8,128)} %get-tuple-element.26.fxl_ref, f32[2,16,14,512]{3,2,1,0:T(8,128)} %get-tuple-element.27.fxr_ref, ...), custom_call_target="tpu_custom_call" | custom-call | tf_op jit(solution)/shard_map/pallas_call | solution.py:191
  154.7 5.6 %shard_map.90 = f32[2,16,8,512]{3,2,1,0:T(8,128)} custom-call(f32[2,16,10,512]{3,2,1,0:T(8,128)} %shard_map.89.w_ref, f32[2,16,16,512]{3,2,1,0:T(8,128)} %get-tuple-element.66.b_ref, f32[2,16,14,512]{3,2,1,0:T(8,128)} %get-tuple-element.26.fxl_ref, f32[2,16,14,512]{3,2,1,0:T(8,128)} %get-tuple-element.27.fxr_ref, ...), custom_call_target="tpu_custom_call" | custom-call | tf_op jit(solution)/shard_map/pallas_call | solution.py:191
  (146 shorter events, 51.6 us)
Async XLA Ops:
  7.2 3.1 %copy-start.3 = (f32[2,16,8,512]{3,2,1,0:T(8,128)S(1)}, f32[2,16,8,512]{3,2,1,0:T(8,128)}, u32[]{:S(2)}) copy-start(f32[2,16,8,512]{3,2,1,0:T(8,128)} %param.6) | copy-start | bytes 1572868
  7.2 65.2 %all-gather.3.cloned.1.call-start = ((), (), s32[]{:S(2)}) async-start(), calls=%async_computation | async-start | bytes 1253376 | tf_op jit(solution)/shard_map/all_gather | solution.py:397
  8.7 12.0 %copy-start.7 = (f32[16,8,512]{2,1,0:T(8,128)}, f32[16,8,512]{2,1,0:T(8,128)S(1)}, u32[]{:S(2)}) copy-start(f32[16,8,512]{2,1,0:T(8,128)S(1)} %multiply_add_fusion) | copy-start | bytes 786436
  10.1 1.0 copy-start.5
  12.1 13.3 %collective-permute-start = (f32[167936]{0:T(1024)}, f32[167936]{0:T(1024)S(1)}, u32[]{:S(2)}, u32[]{:S(2)}) collective-permute-start(f32[167936]{0:T(1024)} %pad_maximum_fusion.2), channel_id=1, source_target_pairs={{0,1},{1,2},{2,3},{3,4},{4,5},{5,6},{6,7},{7,8},{8,9},{9,10},{10,1... | collective-permute-start | bytes 2015240 | tf_op jit(solution)/shard_map/ppermute | solution.py:42
  14.3 12.9 %collective-permute-start.1 = (f32[167936]{0:T(1024)S(1)}, f32[167936]{0:T(1024)S(1)}, u32[]{:S(2)}, u32[]{:S(2)}) collective-permute-start(f32[167936]{0:T(1024)S(1)} %pad_maximum_fusion.3), channel_id=1, source_target_pairs={{1,0},{2,1},{3,2},{4,3},{5,4},{6,5},{7,6},{8,7},{9,8},{10,9},{11,1... | collective-permute-start | bytes 2015240 | tf_op jit(solution)/shard_map/ppermute | solution.py:43
  28.2 1.4 slice-start.1
  29.4 6.7 %copy-start.4 = (f32[2,16,8,512]{3,2,1,0:T(8,128)S(1)}, f32[2,16,8,512]{3,2,1,0:T(8,128)}, u32[]{:S(2)}) copy-start(f32[2,16,8,512]{3,2,1,0:T(8,128)} %param.7) | copy-start | bytes 1572868
  51.5 5.1 %copy-start.10 = (s32[512]{0:T(512)S(1)}, s32[512]{0:T(512)}, u32[]{:S(2)}) copy-start(s32[512]{0:T(512)} %copy-done.9) | copy-start | bytes 6148
  58.7 10.5 %collective-permute-start.2 = (f32[2,16,4,256]{3,2,1,0:T(4,128)S(1)}, f32[2,16,4,256]{3,2,1,0:T(4,128)S(1)}, u32[]{:S(2)}, u32[]{:S(2)}) collective-permute-start(f32[2,16,4,256]{3,2,1,0:T(4,128)S(1)} %broadcast_multiply_fusion.1), channel_id=1, source_target_pairs={{0,1},{1,2},{2,3},{3,4},{4,5},{5,6},{6,7},{7,8},{8,9},{9,10},{10,1... | collective-permute-start | bytes 393224 | tf_op jit(solution)/shard_map/ppermute | solution.py:27
  67.0 4.4 %collective-permute-start.3 = (f32[2,16,4,256]{3,2,1,0:T(4,128)S(1)}, f32[2,16,4,256]{3,2,1,0:T(4,128)S(1)}, u32[]{:S(2)}, u32[]{:S(2)}) collective-permute-start(f32[2,16,4,256]{3,2,1,0:T(4,128)S(1)} %broadcast_multiply_fusion.1), channel_id=1, source_target_pairs={{1,0},{2,1},{3,2},{4,3},{5,4},{6,5},{7,6},{8,7},{9,8},{10,9},{11,1... | collective-permute-start | bytes 393224 | tf_op jit(solution)/shard_map/ppermute | solution.py:29
  73.8 1.0 copy-start.1
  94.6 18.7 %collective-permute-start.10 = (f32[2,16,2,128]{3,2,1,0:T(2,128)S(1)}, f32[2,16,2,128]{3,2,1,0:T(2,128)S(1)}, u32[]{:S(2)}, u32[]{:S(2)}) collective-permute-start(f32[2,16,2,128]{3,2,1,0:T(2,128)S(1)} %copy_multiply_fusion), channel_id=1, source_target_pairs={{3,0},{4,1},{5,2},{6,3},{7,4},{8,5},{9,6},{10,7},{11,8},{12,9},{13... | collective-permute-start | bytes 98312 | tf_op jit(solution)/shard_map/ppermute | solution.py:383
  99.0 16.2 %collective-permute-start.11 = (f32[2,16,2,128]{3,2,1,0:T(2,128)S(1)}, f32[2,16,2,128]{3,2,1,0:T(2,128)S(1)}, u32[]{:S(2)}, u32[]{:S(2)}) collective-permute-start(f32[2,16,2,128]{3,2,1,0:T(2,128)S(1)} %copy_multiply_fusion), channel_id=1, source_target_pairs={{4,0},{5,1},{6,2},{7,3},{8,4},{9,5},{10,6},{11,7},{12,8},{13,9},{1... | collective-permute-start | bytes 98312 | tf_op jit(solution)/shard_map/ppermute | solution.py:383
  100.9 18.9 %collective-permute-start.4 = (f32[2,16,2,128]{3,2,1,0:T(2,128)S(1)}, f32[2,16,2,128]{3,2,1,0:T(2,128)S(1)}, u32[]{:S(2)}, u32[]{:S(2)}) collective-permute-start(f32[2,16,2,128]{3,2,1,0:T(2,128)S(1)} %copy_multiply_fusion), channel_id=1, source_target_pairs={{0,4},{1,5},{2,6},{3,7},{4,8},{5,9},{6,10},{7,11},{8,12},{9,13},{1... | collective-permute-start | bytes 98312 | tf_op jit(solution)/shard_map/ppermute | solution.py:382
  104.8 20.4 %collective-permute-start.5 = (f32[2,16,2,128]{3,2,1,0:T(2,128)S(1)}, f32[2,16,2,128]{3,2,1,0:T(2,128)S(1)}, u32[]{:S(2)}, u32[]{:S(2)}) collective-permute-start(f32[2,16,2,128]{3,2,1,0:T(2,128)S(1)} %copy_multiply_fusion), channel_id=1, source_target_pairs={{0,3},{1,4},{2,5},{3,6},{4,7},{5,8},{6,9},{7,10},{8,11},{9,12},{10... | collective-permute-start | bytes 98312 | tf_op jit(solution)/shard_map/ppermute | solution.py:382
  106.8 18.5 %collective-permute-start.6 = (f32[2,16,2,128]{3,2,1,0:T(2,128)S(1)}, f32[2,16,2,128]{3,2,1,0:T(2,128)S(1)}, u32[]{:S(2)}, u32[]{:S(2)}) collective-permute-start(f32[2,16,2,128]{3,2,1,0:T(2,128)S(1)} %copy_multiply_fusion), channel_id=1, source_target_pairs={{0,2},{1,3},{2,4},{3,5},{4,6},{5,7},{6,8},{7,9},{8,10},{9,11},{10,... | collective-permute-start | bytes 98312 | tf_op jit(solution)/shard_map/ppermute | solution.py:382
  113.3 11.9 %collective-permute-start.7 = (f32[2,16,2,128]{3,2,1,0:T(2,128)S(1)}, f32[2,16,2,128]{3,2,1,0:T(2,128)S(1)}, u32[]{:S(2)}, u32[]{:S(2)}) collective-permute-start(f32[2,16,2,128]{3,2,1,0:T(2,128)S(1)} %copy_multiply_fusion), channel_id=1, source_target_pairs={{0,1},{1,2},{2,3},{3,4},{4,5},{5,6},{6,7},{7,8},{8,9},{9,10},{10,1... | collective-permute-start | bytes 98312 | tf_op jit(solution)/shard_map/ppermute | solution.py:382
  115.2 10.0 %collective-permute-start.8 = (f32[2,16,2,128]{3,2,1,0:T(2,128)S(1)}, f32[2,16,2,128]{3,2,1,0:T(2,128)S(1)}, u32[]{:S(2)}, u32[]{:S(2)}) collective-permute-start(f32[2,16,2,128]{3,2,1,0:T(2,128)S(1)} %copy_multiply_fusion), channel_id=1, source_target_pairs={{1,0},{2,1},{3,2},{4,3},{5,4},{6,5},{7,6},{8,7},{9,8},{10,9},{11,1... | collective-permute-start | bytes 98312 | tf_op jit(solution)/shard_map/ppermute | solution.py:383
  119.8 5.8 %collective-permute-start.9 = (f32[2,16,2,128]{3,2,1,0:T(2,128)S(1)}, f32[2,16,2,128]{3,2,1,0:T(2,128)S(1)}, u32[]{:S(2)}, u32[]{:S(2)}) collective-permute-start(f32[2,16,2,128]{3,2,1,0:T(2,128)S(1)} %copy_multiply_fusion), channel_id=1, source_target_pairs={{2,0},{3,1},{4,2},{5,3},{6,4},{7,5},{8,6},{9,7},{10,8},{11,9},{12,... | collective-permute-start | bytes 98312 | tf_op jit(solution)/shard_map/ppermute | solution.py:383
  134.0 1.9 %copy-start.2 = (f32[2,16,10,256]{3,2,1,0:T(8,128)S(1)}, f32[2,16,10,256]{3,2,1,0:T(8,128)}, u32[]{:S(2)}) copy-start(f32[2,16,10,256]{3,2,1,0:T(8,128)} %shard_map.83.w_ref) | copy-start | bytes 983044
  144.9 1.5 copy-start
  154.7 5.6 %copy-start.8 = (f32[2,8,512]{2,1,0:T(8,128)S(1)}, f32[2,8,512]{2,1,0:T(8,128)}, u32[]{:S(2)}) copy-start(f32[2,8,512]{2,1,0:T(8,128)} %param.11) | copy-start | bytes 98308
  154.7 5.6 %copy-start.11 = (pred[8,512]{1,0:T(8,128)(4,1)S(1)}, pred[8,512]{1,0:T(8,128)(4,1)}, u32[]{:S(2)}) copy-start(pred[8,512]{1,0:T(8,128)(4,1)} %get-tuple-element.51) | copy-start | bytes 12292
  (3 other events, 2.3 us)
Sparse Core Ops, SparseCore 0:
  20.9 37.7 all-gather.2

commit v5 on v4

--- a/solution.py
+++ b/solution.py
@@ -102,14 +102,14 @@
 
 
 def sweep_kernel(w_ref, b_ref, fxl_ref, fxr_ref, fyl_ref, fyr_ref, fz_ref, re_ref, inv_ref, rat_ref, mask_ref, out_ref,
-                 *, rows, cut_w, cut_b, cut_op, mode):
-    relax(w_ref, b_ref, (fxl_ref, fxr_ref, fyl_ref, fyr_ref, fz_ref, re_ref, inv_ref, rat_ref), mask_ref, out_ref,
+                 *, rows, cut_w, cut_b, cut_op, mode, scale):
+    relax(w_ref, b_ref, (fxl_ref, fxr_ref, fyl_ref, fyr_ref, fz_ref, re_ref, inv_ref, rat_ref, scale), mask_ref, out_ref,
           rows=rows, cut_w=cut_w, cut_b=cut_b, cut_op=cut_op, mode=mode)
 
 
 def coarse_kernel(b_ref, fxl_ref, fxr_ref, fyl_ref, fyr_ref, fz_ref, re_ref, inv_ref, rat_ref, mask_ref, out_ref, w_ref,
-                  *, rows, turns):
-    lanes = (fxl_ref, fxr_ref, fyl_ref, fyr_ref, fz_ref, re_ref, inv_ref, rat_ref)
+                  *, rows, turns, scale):
+    lanes = (fxl_ref, fxr_ref, fyl_ref, fyr_ref, fz_ref, re_ref, inv_ref, rat_ref, scale)
     w_ref[...] = jnp.zeros(w_ref.shape, jnp.float32)
     for turn in range(turns):
         relax(w_ref, b_ref, lanes, mask_ref, out_ref, rows=rows, cut_w=7, cut_b=0, cut_op=0, mode="sweep")
@@ -119,7 +119,7 @@
 
 
 def relax(w_ref, b_ref, lanes, mask_ref, out_ref, *, rows, cut_w, cut_b, cut_op, mode):
-    fxl_ref, fxr_ref, fyl_ref, fyr_ref, fz_ref, re_ref, inv_ref, rat_ref = lanes
+    fxl_ref, fxr_ref, fyl_ref, fyr_ref, fz_ref, re_ref, inv_ref, rat_ref, scale = lanes
     layers = out_ref.shape[1]
     cols = out_ref.shape[3]
     lane = lax.broadcasted_iota(jnp.int32, (rows, cols), 1)
@@ -131,6 +131,13 @@
     def cell(ref, k, cut):
         return ref[0, k, pl.ds(cut, rows), :]
 
+    component = pl.program_id(0)
+    weight_x = jnp.where(component == 0, 4.0, 1.0) * scale
+    weight_y = jnp.where(component == 0, 1.0, 4.0) * scale
+
+    def face(ref, weight, k):
+        return weight * ref[k, pl.ds(cut_op, rows), :]
+
     def field(k):
         return w_ref[0, k, pl.ds(cut_w + 1, rows), :]
 
@@ -138,14 +145,14 @@
         w = field(k)
         west = w_ref[0, k, pl.ds(cut_w, rows), :]
         east = w_ref[0, k, pl.ds(cut_w + 2, rows), :]
-        result = -(cell(fxr_ref, k, cut_op) * (east - w) - cell(fxl_ref, k, cut_op) * (w - west))
+        result = -(face(fxr_ref, weight_x, k) * (east - w) - face(fxl_ref, weight_x, k) * (w - west))
         ahead = pltpu.roll(w, 1, 1)
         behind = pltpu.roll(w, cols - 1, 1)
         south = jnp.where(forward_roll, ahead, behind)
         north = jnp.where(forward_roll, behind, ahead)
         south = jnp.where(first_col, 0.0, south)
         north = jnp.where(last_col, 0.0, north)
-        result = result - (cell(fyr_ref, k, cut_op) * (north - w) - cell(fyl_ref, k, cut_op) * (w - south))
+        result = result - (face(fyr_ref, weight_y, k) * (north - w) - face(fyl_ref, weight_y, k) * (w - south))
         up = fz_ref[k, pl.ds(cut_op, rows), :] * (field(k + 1) - w) if k < layers - 1 else 0.0
         down = fz_ref[k - 1, pl.ds(cut_op, rows), :] * (w - field(k - 1)) if k > 0 else 0.0
         result = result - (up - down)
@@ -181,13 +188,13 @@
 def kernel_sweep(field_rim, target, lanes, cut_b, cut_op, mask, mode="sweep", cut_w=0, rows=None):
     parts, layers, rows_rim, cols = field_rim.shape
     rows = rows_rim - 2 if rows is None else rows
-    fxl, fxr, fyl, fyr, fz, re, inv, rat = lanes
+    fxl, fxr, fyl, fyr, fz, re, inv, rat, scale = lanes
     per_part = lambda a: pl.BlockSpec((1,) + a.shape[1:], lambda c: (c,) + (0,) * (a.ndim - 1))
     whole = lambda a: pl.BlockSpec(a.shape, lambda c: (0,) * a.ndim)
     operands = [field_rim, target, fxl, fxr, fyl, fyr, fz, re, inv, rat, mask]
-    specs = [per_part(field_rim), per_part(target), per_part(fxl), per_part(fxr), per_part(fyl), per_part(fyr),
+    specs = [per_part(field_rim), per_part(target), whole(fxl), whole(fxr), whole(fyl), whole(fyr),
              whole(fz), whole(re), per_part(inv), per_part(rat), whole(mask)]
-    body = functools.partial(sweep_kernel, rows=rows, cut_w=cut_w, cut_b=cut_b, cut_op=cut_op, mode=mode)
+    body = functools.partial(sweep_kernel, rows=rows, cut_w=cut_w, cut_b=cut_b, cut_op=cut_op, mode=mode, scale=scale)
     return pl.pallas_call(
         body,
         grid=(parts,),
@@ -223,10 +230,14 @@
         behind = pltpu.roll(middle, cols - 1, 1)
         south = jnp.where(first_col, 0.0, jnp.where(forward_roll, ahead, behind))
         north = jnp.where(last_col, 0.0, jnp.where(forward_roll, behind, ahead))
-        face_w = weight_x * (0.5 * (middle + west))
-        face_e = weight_x * (0.5 * (east + middle))
-        face_s = weight_y * (0.5 * (middle + south))
-        face_n = weight_y * (0.5 * (north + middle))
+        base_w = 0.5 * (middle + west)
+        base_e = 0.5 * (east + middle)
+        base_s = 0.5 * (middle + south)
+        base_n = 0.5 * (north + middle)
+        face_w = weight_x * base_w
+        face_e = weight_x * base_e
+        face_s = weight_y * base_s
+        face_n = weight_y * base_n
         react = re_ref[min(k, re_ref.shape[0] - 1), pl.ds(cut_re, rows), :]
         up = faces_z[k] if k < layers - 1 else 0.0
         down = faces_z[k - 1] if k > 0 else 0.0
@@ -235,10 +246,10 @@
         if k > 0:
             diagonal = diagonal - faces_z[k - 1] * ratio
         inverse = 1.0 / diagonal
-        fxl_ref[0, k] = face_w
-        fxr_ref[0, k] = face_e
-        fyl_ref[0, k] = face_s
-        fyr_ref[0, k] = face_n
+        fxl_ref[k] = base_w
+        fxr_ref[k] = base_e
+        fyl_ref[k] = base_s
+        fyr_ref[k] = base_n
         reo_ref[k] = react
         inv_ref[0, k] = inverse
         if k < layers - 1:
@@ -255,8 +266,8 @@
     cell = (layers, rows, cols)
     faces = (layers - 1, rows, cols)
     body = functools.partial(build_kernel, rows=rows, cut_re=cut_re, scale=horizontal_scale / 4.0**level_index)
-    shapes = [(2,) + cell] * 4 + [faces, cell, (2,) + cell, (2,) + faces]
-    specs = [per_part(cell)] * 4 + [
+    shapes = [cell] * 4 + [faces, cell, (2,) + cell, (2,) + faces]
+    specs = [pl.BlockSpec(cell, lambda c: (0, 0, 0))] * 4 + [
         pl.BlockSpec(faces, lambda c: (0, 0, 0)),
         pl.BlockSpec(cell, lambda c: (0, 0, 0)),
         per_part(cell),
@@ -270,18 +281,18 @@
             out_specs=specs,
             out_shape=[jax.ShapeDtypeStruct(s, jnp.float32) for s in shapes],
         )(eta_level, react_level)
-    )
+    ) + (horizontal_scale / 4.0**level_index,)
 
 
 def kernel_coarse(target, lanes, mask, turns):
     parts, layers, rows, cols = target.shape
-    fxl, fxr, fyl, fyr, fz, re, inv, rat = lanes
+    fxl, fxr, fyl, fyr, fz, re, inv, rat, scale = lanes
     per_part = lambda a: pl.BlockSpec((1,) + a.shape[1:], lambda c: (c,) + (0,) * (a.ndim - 1))
     whole = lambda a: pl.BlockSpec(a.shape, lambda c: (0,) * a.ndim)
     operands = [target, fxl, fxr, fyl, fyr, fz, re, inv, rat, mask]
-    specs = [per_part(target), per_part(fxl), per_part(fxr), per_part(fyl), per_part(fyr),
+    specs = [per_part(target), whole(fxl), whole(fxr), whole(fyl), whole(fyr),
              whole(fz), whole(re), per_part(inv), per_part(rat), whole(mask)]
-    body = functools.partial(coarse_kernel, rows=rows, turns=turns)
+    body = functools.partial(coarse_kernel, rows=rows, turns=turns, scale=scale)
     return pl.pallas_call(
         body,
         grid=(parts,),

time: 169 us -> 168 us (level)
  Pallas kernels: 61.3 us -> 59.5 us
where the time goes in v5:
time: 168 us; the launch traced here: 167 us
  Pallas kernels  59.5 us (35%)
  starting transfers between devices  41.5 us (25%)
  local copies, waits for them, and re-layouts  22.6 us (13%)
  between operations  14.8 us (9%)
  other arithmetic  11.7 us (7%)
  waiting for transfers between devices  9.01 us (5%)
  matrix products  7.79 us (5%)
    pallas_call x10, Pallas kernels, kernel_sweep(): pl.pallas_call(body, grid=(parts,), in_specs=specs, out_specs=pl.BlockSpe...  43.1 us
    ppermute x4, starting transfers between devices, nearby(): lax.ppermute(cells, 'gx', [(i + step, i) for i in range(count - step)])  13 us
    ppermute x4, starting transfers between devices, nearby(): lax.ppermute(cells, 'gx', [(i, i + step) for i in range(count - step)])  11.7 us
    pallas_call x3, Pallas kernels, kernel_operator(): pl.pallas_call(body, grid=(2,), in_specs=[whole(eta_level), whole(react_l...  10.8 us
    ppermute x1, starting transfers between devices, with_halo(): lax.ppermute(tail, axis, [(i, (i + 1) % count) for i in range(ends)])  8.27 us
    broadcast_in_dim x10, local copies, waits for them, and re-layouts, rows_inside(): jnp.broadcast_to(inside(cells, halo, extent)[0, 0], (extent, cols))  6.71 us
    pallas_call x1, Pallas kernels, kernel_coarse(): pl.pallas_call(body, grid=(parts,), in_specs=specs, out_specs=pl.BlockSpe...  5.62 us
    dot_general x6, matrix products, block_mean(): jnp.einsum('...y,yz->...z', field, pairs, precision=lax.Precision.HIGHEST)  5.1 us
  transfers between devices with their start and end apart: 13, of which 4 were waited for; matrix products, arithmetic and copies ran while one was open for 9% of the time, Pallas kernels for 14%

profile of v5, /device:TPU:10, one launch (start us, length us, event | category | flops | bytes accessed | tf_op | source)
XLA Modules:
  0.0 166.9 jit_solution(14858039111148732930)
XLA Ops:
  14.3 4.5 %collective-permute-start.1 = (f32[167936]{0:T(1024)S(1)}, f32[167936]{0:T(1024)S(1)}, u32[]{:S(2)}, u32[]{:S(2)}) collective-permute-start(f32[167936]{0:T(1024)S(1)} %pad_maximum_fusion.3), channel_id=1, source_target_pairs={{1,0},{2,1},{3,2},{4,3},{5,4},{6,5},{7,6},{8,7},{9,8},{10,9},{11,1... | collective-permute-start | bytes 2015240 | tf_op jit(solution)/shard_map/ppermute | solution.py:43
  20.9 4.4 %collective-permute-done = f32[167936]{0:T(1024)S(1)} collective-permute-done((f32[167936]{0:T(1024)}, f32[167936]{0:T(1024)S(1)}, u32[]{:S(2)}, u32[]{:S(2)}) %collective-permute-start) | collective-permute-done | bytes 671776 | tf_op jit(solution)/shard_map/ppermute | solution.py:42
  31.1 5.0 %shard_map.77 = (f32[16,14,512]{2,1,0:T(8,128)}, f32[16,14,512]{2,1,0:T(8,128)}, f32[16,14,512]{2,1,0:T(8,128)}, f32[16,14,512]{2,1,0:T(8,128)}, f32[15,14,512]{...) custom-call(f32[16,16,512]{2,1,0:T(8,128)} %pad_maximum_fusion.4.eta_ref, ...), custom_call_target="tpu_custom_call" | custom-call | tf_op jit(solution)/shard_map/pallas_call | solution.py:277
  38.6 5.6 %shard_map.78.w_ref = f32[2,16,14,512]{3,2,1,0:T(8,128)} custom-call(f32[2,16,16,512]{3,2,1,0:T(8,128)} %get-tuple-element.65.w_ref, f32[2,16,16,512]{3,2,1,0:T(8,128)} %get-tuple-element.66.b_ref, f32[16,14,512]{2,1,0:T(8,128)} %get-tuple-element.26.fxl_ref, f32[16,14,512]{2,1,0:T(8,128)} %get-tuple-element.27.fxr_ref, ...), custom_call_target="tpu_custom_call" | custom-call | tf_op jit(solution)/shard_map/pallas_call | solution.py:198
  44.8 5.8 %shard_map.79.w_ref = f32[2,16,12,512]{3,2,1,0:T(8,128)} custom-call(f32[2,16,14,512]{3,2,1,0:T(8,128)} %shard_map.78.w_ref, f32[2,16,16,512]{3,2,1,0:T(8,128)} %get-tuple-element.66.b_ref, f32[16,14,512]{2,1,0:T(8,128)} %get-tuple-element.26.fxl_ref, f32[16,14,512]{2,1,0:T(8,128)} %get-tuple-element.27.fxr_ref, f32[16,14,512]{2,1,0:T(8,128)} %get-tuple-element.28.fyl_ref, ...), custom_call_target="tpu_custom_call" | custom-call | tf_op jit(solution)/shard_map/pallas_call | solution.py:198
  51.2 4.8 %shard_map.80 = f32[2,16,8,512]{3,2,1,0:T(8,128)} custom-call(f32[2,16,12,512]{3,2,1,0:T(8,128)} %shard_map.79.w_ref, f32[2,16,16,512]{3,2,1,0:T(8,128)} %get-tuple-element.66.b_ref, f32[16,14,512]{2,1,0:T(8,128)} %get-tuple-element.26.fxl_ref, f32[16,14,512]{2,1,0:T(8,128)} %get-tuple-element.27.fxr_ref, f32[16,14,512]{2,1,0:T(8,128)} %get-tuple-element.28.fyl_ref, ...), custom_call_target="tpu_custom_call" | custom-call | tf_op jit(solution)/shard_map/pallas_call | solution.py:198
  58.2 8.3 %collective-permute-start.2 = (f32[2,16,4,256]{3,2,1,0:T(4,128)S(1)}, f32[2,16,4,256]{3,2,1,0:T(4,128)S(1)}, u32[]{:S(2)}, u32[]{:S(2)}) collective-permute-start(f32[2,16,4,256]{3,2,1,0:T(4,128)S(1)} %broadcast_multiply_fusion.1), channel_id=1, source_target_pairs={{0,1},{1,2},{2,3},{3,4},{4,5},{5,6},{6,7},{7,8},{8,9},{9,10},{10,1... | collective-permute-start | bytes 393224 | tf_op jit(solution)/shard_map/ppermute | solution.py:27
  68.6 2.3 %collective-permute-done.3 = f32[2,16,4,256]{3,2,1,0:T(4,128)S(1)} collective-permute-done((f32[2,16,4,256]{3,2,1,0:T(4,128)S(1)}, f32[2,16,4,256]{3,2,1,0:T(4,128)S(1)}, u32[]{:S(2)}, u32[]{:S(2)}) %collective-permute-start.3) | collective-permute-done | bytes 131104 | tf_op jit(solution)/shard_map/ppermute | solution.py:29
  77.8 3.3 %shard_map.81 = (f32[16,12,256]{2,1,0:T(8,128)}, f32[16,12,256]{2,1,0:T(8,128)}, f32[16,12,256]{2,1,0:T(8,128)}, f32[16,12,256]{2,1,0:T(8,128)}, f32[15,12,256]{...) custom-call(f32[16,14,256]{2,1,0:T(8,128)} %pad_dynamic-slice_fusion.eta_ref, ...), custom_call_target="tpu_custom_call" | custom-call | tf_op jit(solution)/shard_map/pallas_call | solution.py:277
  81.7 2.8 %shard_map.82.w_ref = f32[2,16,12,256]{3,2,1,0:T(8,128)} custom-call(f32[2,16,12,256]{3,2,1,0:T(8,128)} %pad_maximum_fusion.5.w_ref.b_ref, f32[2,16,12,256]{3,2,1,0:T(8,128)} %pad_maximum_fusion.5.w_ref.b_ref, f32[16,12,256]{2,1,0:T(8,128)} %get-tuple-element.34.fxl_ref, f32[16,12,256]{2,1,0:T(8,128)} %get-tuple-element.35.fxr_ref, ...), custom_call_target="tpu_custom_call" | custom-call | tf_op jit(solution)/shard_map/pallas_call | solution.py:198
  85.2 3.5 %shard_map.83.w_ref = f32[2,16,10,256]{3,2,1,0:T(8,128)} custom-call(f32[2,16,12,256]{3,2,1,0:T(8,128)} %shard_map.82.w_ref, f32[2,16,12,256]{3,2,1,0:T(8,128)} %pad_maximum_fusion.5.w_ref.b_ref, f32[16,12,256]{2,1,0:T(8,128)} %get-tuple-element.34.fxl_ref, f32[16,12,256]{2,1,0:T(8,128)} %get-tuple-element.35.fxr_ref, ...), custom_call_target="tpu_custom_call" | custom-call | tf_op jit(solution)/shard_map/pallas_call | solution.py:198
  89.4 2.8 %shard_map.84 = f32[2,16,4,256]{3,2,1,0:T(4,128)} custom-call(f32[2,16,10,256]{3,2,1,0:T(8,128)} %shard_map.83.w_ref, f32[2,16,12,256]{3,2,1,0:T(8,128)} %pad_maximum_fusion.5.w_ref.b_ref, f32[16,12,256]{2,1,0:T(8,128)} %get-tuple-element.34.fxl_ref, f32[16,12,256]{2,1,0:T(8,128)} %get-tuple-element.35.fxr_ref, f32[16,12,256]{2,1,0:T(8,128)} %get-tuple-element.36.fyl_ref, ...), custom_call_target="tpu_custom_call" | custom-call | tf_op jit(solution)/shard_map/pallas_call | solution.py:198
  93.5 4.4 %collective-permute-start.10 = (f32[2,16,2,128]{3,2,1,0:T(2,128)S(1)}, f32[2,16,2,128]{3,2,1,0:T(2,128)S(1)}, u32[]{:S(2)}, u32[]{:S(2)}) collective-permute-start(f32[2,16,2,128]{3,2,1,0:T(2,128)S(1)} %copy_multiply_fusion), channel_id=1, source_target_pairs={{3,0},{4,1},{5,2},{6,3},{7,4},{8,5},{9,6},{10,7},{11,8},{12,9},{13... | collective-permute-start | bytes 98312 | tf_op jit(solution)/shard_map/ppermute | solution.py:394
  99.8 3.9 %collective-permute-start.4 = (f32[2,16,2,128]{3,2,1,0:T(2,128)S(1)}, f32[2,16,2,128]{3,2,1,0:T(2,128)S(1)}, u32[]{:S(2)}, u32[]{:S(2)}) collective-permute-start(f32[2,16,2,128]{3,2,1,0:T(2,128)S(1)} %copy_multiply_fusion), channel_id=1, source_target_pairs={{0,4},{1,5},{2,6},{3,7},{4,8},{5,9},{6,10},{7,11},{8,12},{9,13},{1... | collective-permute-start | bytes 98312 | tf_op jit(solution)/shard_map/ppermute | solution.py:393
  105.6 3.9 %collective-permute-start.6 = (f32[2,16,2,128]{3,2,1,0:T(2,128)S(1)}, f32[2,16,2,128]{3,2,1,0:T(2,128)S(1)}, u32[]{:S(2)}, u32[]{:S(2)}) collective-permute-start(f32[2,16,2,128]{3,2,1,0:T(2,128)S(1)} %copy_multiply_fusion), channel_id=1, source_target_pairs={{0,2},{1,3},{2,4},{3,5},{4,6},{5,7},{6,8},{7,9},{8,10},{9,11},{10,... | collective-permute-start | bytes 98312 | tf_op jit(solution)/shard_map/ppermute | solution.py:393
  114.0 4.5 %collective-permute-start.8 = (f32[2,16,2,128]{3,2,1,0:T(2,128)S(1)}, f32[2,16,2,128]{3,2,1,0:T(2,128)S(1)}, u32[]{:S(2)}, u32[]{:S(2)}) collective-permute-start(f32[2,16,2,128]{3,2,1,0:T(2,128)S(1)} %copy_multiply_fusion), channel_id=1, source_target_pairs={{1,0},{2,1},{3,2},{4,3},{5,4},{6,5},{7,6},{8,7},{9,8},{10,9},{11,1... | collective-permute-start | bytes 98312 | tf_op jit(solution)/shard_map/ppermute | solution.py:394
  118.6 2.1 %collective-permute-start.9 = (f32[2,16,2,128]{3,2,1,0:T(2,128)S(1)}, f32[2,16,2,128]{3,2,1,0:T(2,128)S(1)}, u32[]{:S(2)}, u32[]{:S(2)}) collective-permute-start(f32[2,16,2,128]{3,2,1,0:T(2,128)S(1)} %copy_multiply_fusion), channel_id=1, source_target_pairs={{2,0},{3,1},{4,2},{5,3},{6,4},{7,5},{8,6},{9,7},{10,8},{11,9},{12,... | collective-permute-start | bytes 98312 | tf_op jit(solution)/shard_map/ppermute | solution.py:394
  121.4 2.5 %shard_map.85 = (f32[16,18,128]{2,1,0:T(8,128)}, f32[16,18,128]{2,1,0:T(8,128)}, f32[16,18,128]{2,1,0:T(8,128)}, f32[16,18,128]{2,1,0:T(8,128)}, f32[15,18,128]{...) custom-call(f32[16,20,128]{2,1,0:T(8,128)} %pad_dynamic-slice_fusion.1.eta_ref, ...), custom_call_target="tpu_custom_call" | custom-call | tf_op jit(solution)/shard_map/pallas_call | solution.py:277
  124.4 2.2 %concatenate.35.b_ref = f32[2,16,18,128]{3,2,1,0:T(8,128)} concatenate(f32[2,16,2,128]{3,2,1,0:T(2,128)S(1)} %collective-permute-done.4, f32[2,16,2,128]{3,2,1,0:T(2,128)S(1)} %collective-permute-done.5, f32[2,16,2,128]{3,2,1,0:T(2,128)S(1)} %collective-permute-done.6, f32[2,16,2,128]{3,2,1,0:T(2,128)S(1)} %collective-permute-done.7, f32[2,16,2,128]{3,2,1,0:T(2,128)S(1)} %copy_multiply_fusion, ...), dimensions={2} | concatenate | bytes 589824 | tf_op jit(solution)/shard_map/concatenate | solution.py:395
  127.3 5.6 %shard_map.86 = f32[2,16,18,128]{3,2,1,0:T(8,128)} custom-call(f32[2,16,18,128]{3,2,1,0:T(8,128)} %concatenate.35.b_ref, f32[16,18,128]{2,1,0:T(8,128)} %get-tuple-element.42.fxl_ref, f32[16,18,128]{2,1,0:T(8,128)} %get-tuple-element.43.fxr_ref, f32[16,18,128]{2,1,0:T(8,128)} %get-tuple-element.44.fyl_ref, f32[16,18,128]{2,1,0:T(8,128)} %get-tuple-element.45.fyr_ref, ...), custom_call_target="tpu_custom_call" | custom-call | tf_op jit(solution)/shard_map/pallas_call | solution.py:296
  136.5 3.3 %shard_map.87.w_ref = f32[2,16,8,256]{3,2,1,0:T(8,128)} custom-call(f32[2,16,10,256]{3,2,1,0:T(8,128)} %slice_add_fusion.w_ref, f32[2,16,12,256]{3,2,1,0:T(8,128)} %pad_maximum_fusion.5.w_ref.b_ref, f32[16,12,256]{2,1,0:T(8,128)} %get-tuple-element.34.fxl_ref, f32[16,12,256]{2,1,0:T(8,128)} %get-tuple-element.35.fxr_ref, ...), custom_call_target="tpu_custom_call" | custom-call | tf_op jit(solution)/shard_map/pallas_call | solution.py:198
  140.5 3.2 %shard_map.88 = f32[2,16,6,256]{3,2,1,0:T(8,128)} custom-call(f32[2,16,8,256]{3,2,1,0:T(8,128)} %shard_map.87.w_ref, f32[2,16,12,256]{3,2,1,0:T(8,128)} %pad_maximum_fusion.5.w_ref.b_ref, f32[16,12,256]{2,1,0:T(8,128)} %get-tuple-element.34.fxl_ref, f32[16,12,256]{2,1,0:T(8,128)} %get-tuple-element.35.fxr_ref, f32[16,12,256]{2,1,0:T(8,128)} %get-tuple-element.36.fyl_ref, ...), custom_call_target="tpu_custom_call" | custom-call | tf_op jit(solution)/shard_map/pallas_call | solution.py:198
  147.5 5.8 %shard_map.89.w_ref = f32[2,16,10,512]{3,2,1,0:T(8,128)} custom-call(f32[2,16,12,512]{3,2,1,0:T(8,128)} %copy_add_fusion.w_ref, f32[2,16,16,512]{3,2,1,0:T(8,128)} %get-tuple-element.66.b_ref, f32[16,14,512]{2,1,0:T(8,128)} %get-tuple-element.26.fxl_ref, f32[16,14,512]{2,1,0:T(8,128)} %get-tuple-element.27.fxr_ref, ...), custom_call_target="tpu_custom_call" | custom-call | tf_op jit(solution)/shard_map/pallas_call | solution.py:198
  153.3 5.4 %shard_map.90 = f32[2,16,8,512]{3,2,1,0:T(8,128)} custom-call(f32[2,16,10,512]{3,2,1,0:T(8,128)} %shard_map.89.w_ref, f32[2,16,16,512]{3,2,1,0:T(8,128)} %get-tuple-element.66.b_ref, f32[16,14,512]{2,1,0:T(8,128)} %get-tuple-element.26.fxl_ref, f32[16,14,512]{2,1,0:T(8,128)} %get-tuple-element.27.fxr_ref, f32[16,14,512]{2,1,0:T(8,128)} %get-tuple-element.28.fyl_ref, ...), custom_call_target="tpu_custom_call" | custom-call | tf_op jit(solution)/shard_map/pallas_call | solution.py:198
  (146 shorter events, 52.0 us)
Async XLA Ops:
  7.2 3.1 %copy-start.3 = (f32[2,16,8,512]{3,2,1,0:T(8,128)S(1)}, f32[2,16,8,512]{3,2,1,0:T(8,128)}, u32[]{:S(2)}) copy-start(f32[2,16,8,512]{3,2,1,0:T(8,128)} %param.6) | copy-start | bytes 1572868
  7.2 64.6 %all-gather.3.cloned.1.call-start = ((), (), s32[]{:S(2)}) async-start(), calls=%async_computation | async-start | bytes 1253376 | tf_op jit(solution)/shard_map/all_gather | solution.py:408
  8.7 12.1 %copy-start.7 = (f32[16,8,512]{2,1,0:T(8,128)}, f32[16,8,512]{2,1,0:T(8,128)S(1)}, u32[]{:S(2)}) copy-start(f32[16,8,512]{2,1,0:T(8,128)S(1)} %multiply_add_fusion) | copy-start | bytes 786436
  10.1 1.0 copy-start.5
  12.1 13.3 %collective-permute-start = (f32[167936]{0:T(1024)}, f32[167936]{0:T(1024)S(1)}, u32[]{:S(2)}, u32[]{:S(2)}) collective-permute-start(f32[167936]{0:T(1024)} %pad_maximum_fusion.2), channel_id=1, source_target_pairs={{0,1},{1,2},{2,3},{3,4},{4,5},{5,6},{6,7},{7,8},{8,9},{9,10},{10,1... | collective-permute-start | bytes 2015240 | tf_op jit(solution)/shard_map/ppermute | solution.py:42
  14.3 12.9 %collective-permute-start.1 = (f32[167936]{0:T(1024)S(1)}, f32[167936]{0:T(1024)S(1)}, u32[]{:S(2)}, u32[]{:S(2)}) collective-permute-start(f32[167936]{0:T(1024)S(1)} %pad_maximum_fusion.3), channel_id=1, source_target_pairs={{1,0},{2,1},{3,2},{4,3},{5,4},{6,5},{7,6},{8,7},{9,8},{10,9},{11,1... | collective-permute-start | bytes 2015240 | tf_op jit(solution)/shard_map/ppermute | solution.py:43
  28.2 1.4 slice-start.1
  29.4 6.6 %copy-start.4 = (f32[2,16,8,512]{3,2,1,0:T(8,128)S(1)}, f32[2,16,8,512]{3,2,1,0:T(8,128)}, u32[]{:S(2)}) copy-start(f32[2,16,8,512]{3,2,1,0:T(8,128)} %param.7) | copy-start | bytes 1572868
  51.2 4.8 %copy-start.10 = (s32[512]{0:T(512)S(1)}, s32[512]{0:T(512)}, u32[]{:S(2)}) copy-start(s32[512]{0:T(512)} %copy-done.9) | copy-start | bytes 6148
  58.2 10.4 %collective-permute-start.2 = (f32[2,16,4,256]{3,2,1,0:T(4,128)S(1)}, f32[2,16,4,256]{3,2,1,0:T(4,128)S(1)}, u32[]{:S(2)}, u32[]{:S(2)}) collective-permute-start(f32[2,16,4,256]{3,2,1,0:T(4,128)S(1)} %broadcast_multiply_fusion.1), channel_id=1, source_target_pairs={{0,1},{1,2},{2,3},{3,4},{4,5},{5,6},{6,7},{7,8},{8,9},{9,10},{10,1... | collective-permute-start | bytes 393224 | tf_op jit(solution)/shard_map/ppermute | solution.py:27
  66.4 4.4 %collective-permute-start.3 = (f32[2,16,4,256]{3,2,1,0:T(4,128)S(1)}, f32[2,16,4,256]{3,2,1,0:T(4,128)S(1)}, u32[]{:S(2)}, u32[]{:S(2)}) collective-permute-start(f32[2,16,4,256]{3,2,1,0:T(4,128)S(1)} %broadcast_multiply_fusion.1), channel_id=1, source_target_pairs={{1,0},{2,1},{3,2},{4,3},{5,4},{6,5},{7,6},{8,7},{9,8},{10,9},{11,1... | collective-permute-start | bytes 393224 | tf_op jit(solution)/shard_map/ppermute | solution.py:29
  73.2 1.1 copy-start.1
  93.5 18.6 %collective-permute-start.10 = (f32[2,16,2,128]{3,2,1,0:T(2,128)S(1)}, f32[2,16,2,128]{3,2,1,0:T(2,128)S(1)}, u32[]{:S(2)}, u32[]{:S(2)}) collective-permute-start(f32[2,16,2,128]{3,2,1,0:T(2,128)S(1)} %copy_multiply_fusion), channel_id=1, source_target_pairs={{3,0},{4,1},{5,2},{6,3},{7,4},{8,5},{9,6},{10,7},{11,8},{12,9},{13... | collective-permute-start | bytes 98312 | tf_op jit(solution)/shard_map/ppermute | solution.py:394
  97.9 16.2 %collective-permute-start.11 = (f32[2,16,2,128]{3,2,1,0:T(2,128)S(1)}, f32[2,16,2,128]{3,2,1,0:T(2,128)S(1)}, u32[]{:S(2)}, u32[]{:S(2)}) collective-permute-start(f32[2,16,2,128]{3,2,1,0:T(2,128)S(1)} %copy_multiply_fusion), channel_id=1, source_target_pairs={{4,0},{5,1},{6,2},{7,3},{8,4},{9,5},{10,6},{11,7},{12,8},{13,9},{1... | collective-permute-start | bytes 98312 | tf_op jit(solution)/shard_map/ppermute | solution.py:394
  99.8 18.8 %collective-permute-start.4 = (f32[2,16,2,128]{3,2,1,0:T(2,128)S(1)}, f32[2,16,2,128]{3,2,1,0:T(2,128)S(1)}, u32[]{:S(2)}, u32[]{:S(2)}) collective-permute-start(f32[2,16,2,128]{3,2,1,0:T(2,128)S(1)} %copy_multiply_fusion), channel_id=1, source_target_pairs={{0,4},{1,5},{2,6},{3,7},{4,8},{5,9},{6,10},{7,11},{8,12},{9,13},{1... | collective-permute-start | bytes 98312 | tf_op jit(solution)/shard_map/ppermute | solution.py:393
  103.7 20.2 %collective-permute-start.5 = (f32[2,16,2,128]{3,2,1,0:T(2,128)S(1)}, f32[2,16,2,128]{3,2,1,0:T(2,128)S(1)}, u32[]{:S(2)}, u32[]{:S(2)}) collective-permute-start(f32[2,16,2,128]{3,2,1,0:T(2,128)S(1)} %copy_multiply_fusion), channel_id=1, source_target_pairs={{0,3},{1,4},{2,5},{3,6},{4,7},{5,8},{6,9},{7,10},{8,11},{9,12},{10... | collective-permute-start | bytes 98312 | tf_op jit(solution)/shard_map/ppermute | solution.py:393
  105.6 18.2 %collective-permute-start.6 = (f32[2,16,2,128]{3,2,1,0:T(2,128)S(1)}, f32[2,16,2,128]{3,2,1,0:T(2,128)S(1)}, u32[]{:S(2)}, u32[]{:S(2)}) collective-permute-start(f32[2,16,2,128]{3,2,1,0:T(2,128)S(1)} %copy_multiply_fusion), channel_id=1, source_target_pairs={{0,2},{1,3},{2,4},{3,5},{4,6},{5,7},{6,8},{7,9},{8,10},{9,11},{10,... | collective-permute-start | bytes 98312 | tf_op jit(solution)/shard_map/ppermute | solution.py:393
  112.1 11.8 %collective-permute-start.7 = (f32[2,16,2,128]{3,2,1,0:T(2,128)S(1)}, f32[2,16,2,128]{3,2,1,0:T(2,128)S(1)}, u32[]{:S(2)}, u32[]{:S(2)}) collective-permute-start(f32[2,16,2,128]{3,2,1,0:T(2,128)S(1)} %copy_multiply_fusion), channel_id=1, source_target_pairs={{0,1},{1,2},{2,3},{3,4},{4,5},{5,6},{6,7},{7,8},{8,9},{9,10},{10,1... | collective-permute-start | bytes 98312 | tf_op jit(solution)/shard_map/ppermute | solution.py:393
  114.0 9.8 %collective-permute-start.8 = (f32[2,16,2,128]{3,2,1,0:T(2,128)S(1)}, f32[2,16,2,128]{3,2,1,0:T(2,128)S(1)}, u32[]{:S(2)}, u32[]{:S(2)}) collective-permute-start(f32[2,16,2,128]{3,2,1,0:T(2,128)S(1)} %copy_multiply_fusion), channel_id=1, source_target_pairs={{1,0},{2,1},{3,2},{4,3},{5,4},{6,5},{7,6},{8,7},{9,8},{10,9},{11,1... | collective-permute-start | bytes 98312 | tf_op jit(solution)/shard_map/ppermute | solution.py:394
  118.6 5.8 %collective-permute-start.9 = (f32[2,16,2,128]{3,2,1,0:T(2,128)S(1)}, f32[2,16,2,128]{3,2,1,0:T(2,128)S(1)}, u32[]{:S(2)}, u32[]{:S(2)}) collective-permute-start(f32[2,16,2,128]{3,2,1,0:T(2,128)S(1)} %copy_multiply_fusion), channel_id=1, source_target_pairs={{2,0},{3,1},{4,2},{5,3},{6,4},{7,5},{8,6},{9,7},{10,8},{11,9},{12,... | collective-permute-start | bytes 98312 | tf_op jit(solution)/shard_map/ppermute | solution.py:394
  132.9 1.9 %copy-start.2 = (f32[2,16,10,256]{3,2,1,0:T(8,128)S(1)}, f32[2,16,10,256]{3,2,1,0:T(8,128)}, u32[]{:S(2)}) copy-start(f32[2,16,10,256]{3,2,1,0:T(8,128)} %shard_map.83.w_ref) | copy-start | bytes 983044
  143.7 1.5 copy-start
  153.3 5.4 %copy-start.8 = (f32[2,8,512]{2,1,0:T(8,128)S(1)}, f32[2,8,512]{2,1,0:T(8,128)}, u32[]{:S(2)}) copy-start(f32[2,8,512]{2,1,0:T(8,128)} %param.11) | copy-start | bytes 98308
  153.3 5.4 %copy-start.11 = (pred[8,512]{1,0:T(8,128)(4,1)S(1)}, pred[8,512]{1,0:T(8,128)(4,1)}, u32[]{:S(2)}) copy-start(pred[8,512]{1,0:T(8,128)(4,1)} %get-tuple-element.51) | copy-start | bytes 12292
  (3 other events, 2.3 us)
Sparse Core Ops, SparseCore 0:
  20.9 37.7 all-gather.2

commit v6 on v5

--- a/solution.py
+++ b/solution.py
@@ -102,9 +102,13 @@
 
 
 def sweep_kernel(w_ref, b_ref, fxl_ref, fxr_ref, fyl_ref, fyr_ref, fz_ref, re_ref, inv_ref, rat_ref, mask_ref, out_ref,
-                 *, rows, cut_w, cut_b, cut_op, mode, scale):
-    relax(w_ref, b_ref, (fxl_ref, fxr_ref, fyl_ref, fyr_ref, fz_ref, re_ref, inv_ref, rat_ref, scale), mask_ref, out_ref,
-          rows=rows, cut_w=cut_w, cut_b=cut_b, cut_op=cut_op, mode=mode)
+                 *more, rows, cut_w, cut_b, cut_op, mode, scale, then):
+    lanes = (fxl_ref, fxr_ref, fyl_ref, fyr_ref, fz_ref, re_ref, inv_ref, rat_ref, scale)
+    relax(w_ref, b_ref, lanes, mask_ref, out_ref, rows=rows, cut_w=cut_w, cut_b=cut_b, cut_op=cut_op, mode=mode)
+    if then is not None:
+        res_cut_w, res_rows, res_cut_b, res_cut_op = then
+        relax(out_ref, b_ref, lanes, mask_ref, more[0], rows=res_rows, cut_w=res_cut_w, cut_b=res_cut_b,
+              cut_op=res_cut_op, mode="residual")
 
 
 def coarse_kernel(b_ref, fxl_ref, fxr_ref, fyl_ref, fyr_ref, fz_ref, re_ref, inv_ref, rat_ref, mask_ref, out_ref, w_ref,
@@ -185,7 +189,7 @@
         out_ref[0, k] = jnp.where(keep, value, 0.0)
 
 
-def kernel_sweep(field_rim, target, lanes, cut_b, cut_op, mask, mode="sweep", cut_w=0, rows=None):
+def kernel_sweep(field_rim, target, lanes, cut_b, cut_op, mask, mode="sweep", cut_w=0, rows=None, then=None):
     parts, layers, rows_rim, cols = field_rim.shape
     rows = rows_rim - 2 if rows is None else rows
     fxl, fxr, fyl, fyr, fz, re, inv, rat, scale = lanes
@@ -194,14 +198,16 @@
     operands = [field_rim, target, fxl, fxr, fyl, fyr, fz, re, inv, rat, mask]
     specs = [per_part(field_rim), per_part(target), whole(fxl), whole(fxr), whole(fyl), whole(fyr),
              whole(fz), whole(re), per_part(inv), per_part(rat), whole(mask)]
-    body = functools.partial(sweep_kernel, rows=rows, cut_w=cut_w, cut_b=cut_b, cut_op=cut_op, mode=mode, scale=scale)
-    return pl.pallas_call(
-        body,
-        grid=(parts,),
-        in_specs=specs,
-        out_specs=pl.BlockSpec((1, layers, rows, cols), lambda c: (c, 0, 0, 0)),
-        out_shape=jax.ShapeDtypeStruct((parts, layers, rows, cols), jnp.float32),
-    )(*operands)
+    body = functools.partial(
+        sweep_kernel, rows=rows, cut_w=cut_w, cut_b=cut_b, cut_op=cut_op, mode=mode, scale=scale, then=then
+    )
+    out_specs = [pl.BlockSpec((1, layers, rows, cols), lambda c: (c, 0, 0, 0))]
+    out_shape = [jax.ShapeDtypeStruct((parts, layers, rows, cols), jnp.float32)]
+    if then is not None:
+        out_specs.append(pl.BlockSpec((1, layers, then[1], cols), lambda c: (c, 0, 0, 0)))
+        out_shape.append(jax.ShapeDtypeStruct((parts, layers, then[1], cols), jnp.float32))
+    outs = pl.pallas_call(body, grid=(parts,), in_specs=specs, out_specs=out_specs, out_shape=out_shape)(*operands)
+    return tuple(outs) if then is not None else outs[0]
 
 
 def build_kernel(eta_ref, re_ref, fxl_ref, fxr_ref, fyl_ref, fyr_ref, fz_ref, reo_ref, inv_ref, rat_ref,
@@ -423,8 +429,9 @@
     )
     op_0 = kernel_operator(eta_wide, react_wide, 0, 1)
     fine = kernel_sweep(guess_wide, misfit_wide, op_0, 1, 0, rows_inside(cells, 3, cells + 6, cols))
-    fine = kernel_sweep(fine, misfit_wide, op_0, 2, 1, rows_inside(cells, 2, cells + 4, cols))
-    residual = kernel_sweep(fine, misfit_wide, op_0, 4, 3, rows_inside(cells, 0, cells, cols), "residual", 1, cells)
+    fine, residual = kernel_sweep(
+        fine, misfit_wide, op_0, 2, 1, rows_inside(cells, 2, cells + 4, cols), then=(1, cells, 4, 3)
+    )
     middle_rhs = restrict(residual)
 
     half = cells // 2
@@ -434,8 +441,9 @@
     react_1_wide = window(react_1_all, 1, where * half, 3 * half, half)
     op_1 = kernel_operator(eta_1_wide, react_1_wide, 1)
     middle = kernel_sweep(rhs_wide, rhs_wide, op_1, 0, 0, rows_inside(half, half, 3 * half, wide), "zero", 0, 3 * half)
-    middle = kernel_sweep(middle, rhs_wide, op_1, 1, 1, rows_inside(half, half - 1, 3 * half - 2, wide))
-    residual = kernel_sweep(middle, rhs_wide, op_1, half, half, rows_inside(half, 0, half, wide), "residual", half - 2, half)
+    middle, residual = kernel_sweep(
+        middle, rhs_wide, op_1, 1, 1, rows_inside(half, half - 1, 3 * half - 2, wide), then=(half - 2, half, half, half)
+    )
     coarse_rhs = restrict(residual)
 
     quarter = cells // 4

time: 168 us -> 162 us (0.964); the launches traced: 167 us -> 159 us
  starting transfers between devices: 41.5 us -> 33.8 us
  Pallas kernels: 59.5 us -> 53.4 us
  waiting for transfers between devices: 9.01 us -> 14.6 us
    pallas_call x10 -> x8, Pallas kernels: 43.1 us -> 37 us  [kernel_sweep(): pl.pallas_call(body, grid=(parts,), in_specs=specs, out_specs=out_specs,...]
    ppermute x1, waiting for transfers between devices: 0.01 us -> 4.64 us  [with_halo(): lax.ppermute(tail, axis, [(i, (i + 1) % count) for i in range(ends)])]
    ppermute x1, starting transfers between devices: 8.27 us -> 5.41 us  [with_halo(): lax.ppermute(tail, axis, [(i, (i + 1) % count) for i in range(ends)])]
    slice x5, local copies, waits for them, and re-layouts: 0.11 us -> 2.83 us  [trade(): left = from_left[offset:offset + size].reshape(h.shape)]
    ppermute x4, starting transfers between devices: 13 us -> 10.6 us  [nearby(): lax.ppermute(cells, 'gx', [(i + step, i) for i in range(count - step)])]
    ppermute x1, waiting for transfers between devices: 2.28 us -> 0.01 us  [with_halo(): lax.ppermute(head, axis, [((i + 1) % count, i) for i in range(ends)])]
    ppermute x1, waiting for transfers between devices: 1.73 us -> 3.7 us  [trade(): lax.ppermute(pack(heads), 'gx', [(i + 1, i) for i in range(ends)])]
    ppermute x1, starting transfers between devices: 4.54 us -> 2.74 us  [trade(): lax.ppermute(pack(heads), 'gx', [(i + 1, i) for i in range(ends)])]
  transfers between devices with their start and end apart: 13 -> 13, of which waited for: 4 -> 4; matrix products, arithmetic and copies ran while one was open for 9% -> 11% of each run, Pallas kernels for 14% -> 13%
where the time goes in v6:
time: 162 us; the launch traced here: 159 us
  Pallas kernels  53.4 us (33%)
  starting transfers between devices  33.8 us (21%)
  local copies, waits for them, and re-layouts  22.7 us (14%)
  between operations  14.8 us (9%)
  waiting for transfers between devices  14.6 us (9%)
  other arithmetic  12 us (7%)
  matrix products  7.8 us (5%)
    pallas_call x8, Pallas kernels, kernel_sweep(): pl.pallas_call(body, grid=(parts,), in_specs=specs, out_specs=out_specs,...  37 us
    ppermute x4, starting transfers between devices, nearby(): lax.ppermute(cells, 'gx', [(i, i + step) for i in range(count - step)])  11.2 us
    pallas_call x3, Pallas kernels, kernel_operator(): pl.pallas_call(body, grid=(2,), in_specs=[whole(eta_level), whole(react_l...  10.9 us
    ppermute x4, starting transfers between devices, nearby(): lax.ppermute(cells, 'gx', [(i + step, i) for i in range(count - step)])  10.6 us
    broadcast_in_dim x9, local copies, waits for them, and re-layouts, rows_inside(): jnp.broadcast_to(inside(cells, halo, extent)[0, 0], (extent, cols))  6.07 us
    ppermute x1, waiting for transfers between devices, trade(): lax.ppermute(pack(tails), 'gx', [(i, i + 1) for i in range(ends)])  5.74 us
    pallas_call x1, Pallas kernels, kernel_coarse(): pl.pallas_call(body, grid=(parts,), in_specs=specs, out_specs=pl.BlockSpe...  5.61 us
    ppermute x1, starting transfers between devices, with_halo(): lax.ppermute(tail, axis, [(i, (i + 1) % count) for i in range(ends)])  5.41 us
  transfers between devices with their start and end apart: 13, of which 4 were waited for; matrix products, arithmetic and copies ran while one was open for 11% of the time, Pallas kernels for 13%

profile of v6, /device:TPU:10, one launch (start us, length us, event | category | flops | bytes accessed | tf_op | source)
XLA Modules:
  0.0 159.1 jit_solution(6713812790042314945)
XLA Ops:
  11.5 2.7 %collective-permute-start.1 = (f32[167936]{0:T(1024)}, f32[167936]{0:T(1024)S(1)}, u32[]{:S(2)}, u32[]{:S(2)}) collective-permute-start(f32[167936]{0:T(1024)} %pad_maximum_fusion.3), channel_id=1, source_target_pairs={{1,0},{2,1},{3,2},{4,3},{5,4},{6,5},{7,6},{8,7},{9,8},{10,9},{11,1... | collective-permute-start | bytes 2015240 | tf_op jit(solution)/shard_map/ppermute | solution.py:43
  19.2 3.7 %collective-permute-done.1 = f32[167936]{0:T(1024)S(1)} collective-permute-done((f32[167936]{0:T(1024)}, f32[167936]{0:T(1024)S(1)}, u32[]{:S(2)}, u32[]{:S(2)}) %collective-permute-start.1) | collective-permute-done | bytes 671776 | tf_op jit(solution)/shard_map/ppermute | solution.py:43
  23.0 5.7 %collective-permute-done = f32[167936]{0:T(1024)} collective-permute-done((f32[167936]{0:T(1024)}, f32[167936]{0:T(1024)}, u32[]{:S(2)}, u32[]{:S(2)}) %collective-permute-start) | collective-permute-done | bytes 671776 | tf_op jit(solution)/shard_map/ppermute | solution.py:42
  33.6 5.0 %shard_map.77 = (f32[16,14,512]{2,1,0:T(8,128)}, f32[16,14,512]{2,1,0:T(8,128)}, f32[16,14,512]{2,1,0:T(8,128)}, f32[16,14,512]{2,1,0:T(8,128)}, f32[15,14,512]{...) custom-call(f32[16,16,512]{2,1,0:T(8,128)} %pad_maximum_fusion.4.eta_ref, ...), custom_call_target="tpu_custom_call" | custom-call | tf_op jit(solution)/shard_map/pallas_call | solution.py:283
  41.1 5.6 %shard_map.78.w_ref = f32[2,16,14,512]{3,2,1,0:T(8,128)} custom-call(f32[2,16,16,512]{3,2,1,0:T(8,128)} %get-tuple-element.73.w_ref, f32[2,16,16,512]{3,2,1,0:T(8,128)} %get-tuple-element.74.b_ref, f32[16,14,512]{2,1,0:T(8,128)} %get-tuple-element.30.fxl_ref, f32[16,14,512]{2,1,0:T(8,128)} %get-tuple-element.31.fxr_ref, ...), custom_call_target="tpu_custom_call" | custom-call | tf_op jit(solution)/shard_map/pallas_call | solution.py:209
  47.3 7.1 %shard_map.79 = (f32[2,16,12,512]{3,2,1,0:T(8,128)}, f32[2,16,8,512]{3,2,1,0:T(8,128)}) custom-call(f32[2,16,14,512]{3,2,1,0:T(8,128)} %shard_map.78.w_ref, f32[2,16,16,512]{3,2,1,0:T(8,128)} %get-tuple-element.74.b_ref, f32[16,14,512]{2,1,0:T(8,128)} %get-tuple-element.30.fxl_ref, f32[16,14,512]{2,1,0:T(8,128)} %get-tuple-element.31.fxr_ref, ...), custom_call_target="tpu_custom_call" | custom-call | tf_op jit(solution)/shard_map/pallas_call | solution.py:209
  58.4 5.4 %collective-permute-start.2 = (f32[2,16,4,256]{3,2,1,0:T(4,128)S(1)}, f32[2,16,4,256]{3,2,1,0:T(4,128)S(1)}, u32[]{:S(2)}, u32[]{:S(2)}) collective-permute-start(f32[2,16,4,256]{3,2,1,0:T(4,128)S(1)} %broadcast_multiply_fusion.1), channel_id=1, source_target_pairs={{0,1},{1,2},{2,3},{3,4},{4,5},{5,6},{6,7},{7,8},{8,9},{9,10},{10,1... | collective-permute-start | bytes 393224 | tf_op jit(solution)/shard_map/ppermute | solution.py:27
  63.8 4.6 %collective-permute-done.2 = f32[2,16,4,256]{3,2,1,0:T(4,128)S(1)} collective-permute-done((f32[2,16,4,256]{3,2,1,0:T(4,128)S(1)}, f32[2,16,4,256]{3,2,1,0:T(4,128)S(1)}, u32[]{:S(2)}, u32[]{:S(2)}) %collective-permute-start.2) | collective-permute-done | bytes 131104 | tf_op jit(solution)/shard_map/ppermute | solution.py:27
  75.3 3.3 %shard_map.80 = (f32[16,12,256]{2,1,0:T(8,128)}, f32[16,12,256]{2,1,0:T(8,128)}, f32[16,12,256]{2,1,0:T(8,128)}, f32[16,12,256]{2,1,0:T(8,128)}, f32[15,12,256]{...) custom-call(f32[16,14,256]{2,1,0:T(8,128)} %pad_dynamic-slice_fusion.eta_ref, ...), custom_call_target="tpu_custom_call" | custom-call | tf_op jit(solution)/shard_map/pallas_call | solution.py:283
  79.3 2.9 %shard_map.81.w_ref = f32[2,16,12,256]{3,2,1,0:T(8,128)} custom-call(f32[2,16,12,256]{3,2,1,0:T(8,128)} %pad_maximum_fusion.5.w_ref.b_ref, f32[2,16,12,256]{3,2,1,0:T(8,128)} %pad_maximum_fusion.5.w_ref.b_ref, f32[16,12,256]{2,1,0:T(8,128)} %get-tuple-element.40.fxl_ref, f32[16,12,256]{2,1,0:T(8,128)} %get-tuple-element.41.fxr_ref, ...), custom_call_target="tpu_custom_call" | custom-call | tf_op jit(solution)/shard_map/pallas_call | solution.py:209
  82.8 3.8 %shard_map.82 = (f32[2,16,10,256]{3,2,1,0:T(8,128)}, f32[2,16,4,256]{3,2,1,0:T(4,128)}) custom-call(f32[2,16,12,256]{3,2,1,0:T(8,128)} %shard_map.81.w_ref, f32[2,16,12,256]{3,2,1,0:T(8,128)} %pad_maximum_fusion.5.w_ref.b_ref, f32[16,12,256]{2,1,0:T(8,128)} %get-tuple-element.40.fxl_ref, f32[16,12,256]{2,1,0:T(8,128)} %get-tuple-element.41.fxr_ref, ...), custom_call_target="tpu_custom_call" | custom-call | tf_op jit(solution)/shard_map/pallas_call | solution.py:209
  87.9 3.5 %collective-permute-start.4 = (f32[2,16,2,128]{3,2,1,0:T(2,128)S(1)}, f32[2,16,2,128]{3,2,1,0:T(2,128)S(1)}, u32[]{:S(2)}, u32[]{:S(2)}) collective-permute-start(f32[2,16,2,128]{3,2,1,0:T(2,128)S(1)} %copy_multiply_fusion), channel_id=1, source_target_pairs={{0,4},{1,5},{2,6},{3,7},{4,8},{5,9},{6,10},{7,11},{8,12},{9,13},{1... | collective-permute-start | bytes 98312 | tf_op jit(solution)/shard_map/ppermute | solution.py:399
  93.3 3.7 %collective-permute-start.6 = (f32[2,16,2,128]{3,2,1,0:T(2,128)S(1)}, f32[2,16,2,128]{3,2,1,0:T(2,128)S(1)}, u32[]{:S(2)}, u32[]{:S(2)}) collective-permute-start(f32[2,16,2,128]{3,2,1,0:T(2,128)S(1)} %copy_multiply_fusion), channel_id=1, source_target_pairs={{0,2},{1,3},{2,4},{3,5},{4,6},{5,7},{6,8},{7,9},{8,10},{9,11},{10,... | collective-permute-start | bytes 98312 | tf_op jit(solution)/shard_map/ppermute | solution.py:399
  96.9 2.1 %collective-permute-start.7 = (f32[2,16,2,128]{3,2,1,0:T(2,128)S(1)}, f32[2,16,2,128]{3,2,1,0:T(2,128)S(1)}, u32[]{:S(2)}, u32[]{:S(2)}) collective-permute-start(f32[2,16,2,128]{3,2,1,0:T(2,128)S(1)} %copy_multiply_fusion), channel_id=1, source_target_pairs={{0,1},{1,2},{2,3},{3,4},{4,5},{5,6},{6,7},{7,8},{8,9},{9,10},{10,1... | collective-permute-start | bytes 98312 | tf_op jit(solution)/shard_map/ppermute | solution.py:399
  99.1 4.4 %collective-permute-start.8 = (f32[2,16,2,128]{3,2,1,0:T(2,128)S(1)}, f32[2,16,2,128]{3,2,1,0:T(2,128)S(1)}, u32[]{:S(2)}, u32[]{:S(2)}) collective-permute-start(f32[2,16,2,128]{3,2,1,0:T(2,128)S(1)} %copy_multiply_fusion), channel_id=1, source_target_pairs={{1,0},{2,1},{3,2},{4,3},{5,4},{6,5},{7,6},{8,7},{9,8},{10,9},{11,1... | collective-permute-start | bytes 98312 | tf_op jit(solution)/shard_map/ppermute | solution.py:400
  106.0 2.2 %collective-permute-start.9 = (f32[2,16,2,128]{3,2,1,0:T(2,128)S(1)}, f32[2,16,2,128]{3,2,1,0:T(2,128)S(1)}, u32[]{:S(2)}, u32[]{:S(2)}) collective-permute-start(f32[2,16,2,128]{3,2,1,0:T(2,128)S(1)} %copy_multiply_fusion), channel_id=1, source_target_pairs={{2,0},{3,1},{4,2},{5,3},{6,4},{7,5},{8,6},{9,7},{10,8},{11,9},{12,... | collective-permute-start | bytes 98312 | tf_op jit(solution)/shard_map/ppermute | solution.py:400
  110.1 2.1 %collective-permute-start.11 = (f32[2,16,2,128]{3,2,1,0:T(2,128)S(1)}, f32[2,16,2,128]{3,2,1,0:T(2,128)S(1)}, u32[]{:S(2)}, u32[]{:S(2)}) collective-permute-start(f32[2,16,2,128]{3,2,1,0:T(2,128)S(1)} %copy_multiply_fusion), channel_id=1, source_target_pairs={{4,0},{5,1},{6,2},{7,3},{8,4},{9,5},{10,6},{11,7},{12,8},{13,9},{1... | collective-permute-start | bytes 98312 | tf_op jit(solution)/shard_map/ppermute | solution.py:400
  112.9 2.5 %shard_map.83 = (f32[16,18,128]{2,1,0:T(8,128)}, f32[16,18,128]{2,1,0:T(8,128)}, f32[16,18,128]{2,1,0:T(8,128)}, f32[16,18,128]{2,1,0:T(8,128)}, f32[15,18,128]{...) custom-call(f32[16,20,128]{2,1,0:T(8,128)} %pad_dynamic-slice_fusion.1.eta_ref, ...), custom_call_target="tpu_custom_call" | custom-call | tf_op jit(solution)/shard_map/pallas_call | solution.py:283
  115.9 2.2 %concatenate.35.b_ref = f32[2,16,18,128]{3,2,1,0:T(8,128)} concatenate(f32[2,16,2,128]{3,2,1,0:T(2,128)S(1)} %collective-permute-done.4, f32[2,16,2,128]{3,2,1,0:T(2,128)S(1)} %collective-permute-done.5, f32[2,16,2,128]{3,2,1,0:T(2,128)S(1)} %collective-permute-done.6, f32[2,16,2,128]{3,2,1,0:T(2,128)S(1)} %collective-permute-done.7, f32[2,16,2,128]{3,2,1,0:T(2,128)S(1)} %copy_multiply_fusion, ...), dimensions={2} | concatenate | bytes 589824 | tf_op jit(solution)/shard_map/concatenate | solution.py:401
  118.8 5.6 %shard_map.84 = f32[2,16,18,128]{3,2,1,0:T(8,128)} custom-call(f32[2,16,18,128]{3,2,1,0:T(8,128)} %concatenate.35.b_ref, f32[16,18,128]{2,1,0:T(8,128)} %get-tuple-element.50.fxl_ref, f32[16,18,128]{2,1,0:T(8,128)} %get-tuple-element.51.fxr_ref, f32[16,18,128]{2,1,0:T(8,128)} %get-tuple-element.52.fyl_ref, f32[16,18,128]{2,1,0:T(8,128)} %get-tuple-element.53.fyr_ref, ...), custom_call_target="tpu_custom_call" | custom-call | tf_op jit(solution)/shard_map/pallas_call | solution.py:302
  128.0 3.3 %shard_map.85.w_ref = f32[2,16,8,256]{3,2,1,0:T(8,128)} custom-call(f32[2,16,10,256]{3,2,1,0:T(8,128)} %slice_add_fusion.w_ref, f32[2,16,12,256]{3,2,1,0:T(8,128)} %pad_maximum_fusion.5.w_ref.b_ref, f32[16,12,256]{2,1,0:T(8,128)} %get-tuple-element.40.fxl_ref, f32[16,12,256]{2,1,0:T(8,128)} %get-tuple-element.41.fxr_ref, ...), custom_call_target="tpu_custom_call" | custom-call | tf_op jit(solution)/shard_map/pallas_call | solution.py:209
  132.0 3.2 %shard_map.86 = f32[2,16,6,256]{3,2,1,0:T(8,128)} custom-call(f32[2,16,8,256]{3,2,1,0:T(8,128)} %shard_map.85.w_ref, f32[2,16,12,256]{3,2,1,0:T(8,128)} %pad_maximum_fusion.5.w_ref.b_ref, f32[16,12,256]{2,1,0:T(8,128)} %get-tuple-element.40.fxl_ref, f32[16,12,256]{2,1,0:T(8,128)} %get-tuple-element.41.fxr_ref, f32[16,12,256]{2,1,0:T(8,128)} %get-tuple-element.42.fyl_ref, ...), custom_call_target="tpu_custom_call" | custom-call | tf_op jit(solution)/shard_map/pallas_call | solution.py:209
  139.0 5.8 %shard_map.87.w_ref = f32[2,16,10,512]{3,2,1,0:T(8,128)} custom-call(f32[2,16,12,512]{3,2,1,0:T(8,128)} %copy_add_fusion.w_ref, f32[2,16,16,512]{3,2,1,0:T(8,128)} %get-tuple-element.74.b_ref, f32[16,14,512]{2,1,0:T(8,128)} %get-tuple-element.30.fxl_ref, f32[16,14,512]{2,1,0:T(8,128)} %get-tuple-element.31.fxr_ref, ...), custom_call_target="tpu_custom_call" | custom-call | tf_op jit(solution)/shard_map/pallas_call | solution.py:209
  145.4 5.4 %shard_map.88 = f32[2,16,8,512]{3,2,1,0:T(8,128)} custom-call(f32[2,16,10,512]{3,2,1,0:T(8,128)} %shard_map.87.w_ref, f32[2,16,16,512]{3,2,1,0:T(8,128)} %get-tuple-element.74.b_ref, f32[16,14,512]{2,1,0:T(8,128)} %get-tuple-element.30.fxl_ref, f32[16,14,512]{2,1,0:T(8,128)} %get-tuple-element.31.fxr_ref, f32[16,14,512]{2,1,0:T(8,128)} %get-tuple-element.32.fyl_ref, ...), custom_call_target="tpu_custom_call" | custom-call | tf_op jit(solution)/shard_map/pallas_call | solution.py:209
  (134 shorter events, 48.4 us)
Async XLA Ops:
  7.2 2.5 %copy-start.2 = (f32[2,16,8,512]{3,2,1,0:T(8,128)S(1)}, f32[2,16,8,512]{3,2,1,0:T(8,128)}, u32[]{:S(2)}) copy-start(f32[2,16,8,512]{3,2,1,0:T(8,128)} %param.7) | copy-start | bytes 1572868
  7.2 62.2 %all-gather.3.cloned.1.call-start = ((), (), s32[]{:S(2)}) async-start(), calls=%async_computation | async-start | bytes 1253376 | tf_op jit(solution)/shard_map/all_gather | solution.py:414
  8.1 10.9 %copy-start.6 = (f32[16,8,512]{2,1,0:T(8,128)}, f32[16,8,512]{2,1,0:T(8,128)S(1)}, u32[]{:S(2)}) copy-start(f32[16,8,512]{2,1,0:T(8,128)S(1)} %multiply_add_fusion) | copy-start | bytes 786436
  9.5 1.0 copy-start.3
  11.5 11.4 %collective-permute-start.1 = (f32[167936]{0:T(1024)}, f32[167936]{0:T(1024)S(1)}, u32[]{:S(2)}, u32[]{:S(2)}) collective-permute-start(f32[167936]{0:T(1024)} %pad_maximum_fusion.3), channel_id=1, source_target_pairs={{1,0},{2,1},{3,2},{4,3},{5,4},{6,5},{7,6},{8,7},{9,8},{10,9},{11,1... | collective-permute-start | bytes 2015240 | tf_op jit(solution)/shard_map/ppermute | solution.py:43
  15.4 13.4 %collective-permute-start = (f32[167936]{0:T(1024)}, f32[167936]{0:T(1024)}, u32[]{:S(2)}, u32[]{:S(2)}) collective-permute-start(f32[167936]{0:T(1024)} %pad_maximum_fusion.2), channel_id=1, source_target_pairs={{0,1},{1,2},{2,3},{3,4},{4,5},{5,6},{6,7},{7,8},{8,9},{9,10},{10,1... | collective-permute-start | bytes 2015240 | tf_op jit(solution)/shard_map/ppermute | solution.py:42
  29.9 2.1 %slice-start.1 = ((f32[16,8,512]{2,1,0:T(8,128)}), f32[2,8,512]{2,1,0:T(8,128)S(1)}, s32[]{:S(2)}) async-start(f32[16,8,512]{2,1,0:T(8,128)} %copy-done.6), calls=%async_computation.2 | async-start | bytes 65536 | tf_op jit(solution)/shard_map/slice | solution.py:408
  30.2 8.4 %copy-start.1 = (f32[2,16,8,512]{3,2,1,0:T(8,128)S(1)}, f32[2,16,8,512]{3,2,1,0:T(8,128)}, u32[]{:S(2)}) copy-start(f32[2,16,8,512]{3,2,1,0:T(8,128)} %param.6) | copy-start | bytes 1572868
  56.4 7.4 %collective-permute-start.3 = (f32[2,16,4,256]{3,2,1,0:T(4,128)S(1)}, f32[2,16,4,256]{3,2,1,0:T(4,128)S(1)}, u32[]{:S(2)}, u32[]{:S(2)}) collective-permute-start(f32[2,16,4,256]{3,2,1,0:T(4,128)S(1)} %broadcast_multiply_fusion.1), channel_id=1, source_target_pairs={{1,0},{2,1},{3,2},{4,3},{5,4},{6,5},{7,6},{8,7},{9,8},{10,9},{11,1... | collective-permute-start | bytes 393224 | tf_op jit(solution)/shard_map/ppermute | solution.py:29
  58.4 10.1 %collective-permute-start.2 = (f32[2,16,4,256]{3,2,1,0:T(4,128)S(1)}, f32[2,16,4,256]{3,2,1,0:T(4,128)S(1)}, u32[]{:S(2)}, u32[]{:S(2)}) collective-permute-start(f32[2,16,4,256]{3,2,1,0:T(4,128)S(1)} %broadcast_multiply_fusion.1), channel_id=1, source_target_pairs={{0,1},{1,2},{2,3},{3,4},{4,5},{5,6},{6,7},{7,8},{8,9},{9,10},{10,1... | collective-permute-start | bytes 393224 | tf_op jit(solution)/shard_map/ppermute | solution.py:27
  70.8 1.1 copy-start
  72.9 0.9 slice-start
  87.9 18.1 %collective-permute-start.4 = (f32[2,16,2,128]{3,2,1,0:T(2,128)S(1)}, f32[2,16,2,128]{3,2,1,0:T(2,128)S(1)}, u32[]{:S(2)}, u32[]{:S(2)}) collective-permute-start(f32[2,16,2,128]{3,2,1,0:T(2,128)S(1)} %copy_multiply_fusion), channel_id=1, source_target_pairs={{0,4},{1,5},{2,6},{3,7},{4,8},{5,9},{6,10},{7,11},{8,12},{9,13},{1... | collective-permute-start | bytes 98312 | tf_op jit(solution)/shard_map/ppermute | solution.py:399
  91.3 16.8 %collective-permute-start.5 = (f32[2,16,2,128]{3,2,1,0:T(2,128)S(1)}, f32[2,16,2,128]{3,2,1,0:T(2,128)S(1)}, u32[]{:S(2)}, u32[]{:S(2)}) collective-permute-start(f32[2,16,2,128]{3,2,1,0:T(2,128)S(1)} %copy_multiply_fusion), channel_id=1, source_target_pairs={{0,3},{1,4},{2,5},{3,6},{4,7},{5,8},{6,9},{7,10},{8,11},{9,12},{10... | collective-permute-start | bytes 98312 | tf_op jit(solution)/shard_map/ppermute | solution.py:399
  93.3 16.8 %collective-permute-start.6 = (f32[2,16,2,128]{3,2,1,0:T(2,128)S(1)}, f32[2,16,2,128]{3,2,1,0:T(2,128)S(1)}, u32[]{:S(2)}, u32[]{:S(2)}) collective-permute-start(f32[2,16,2,128]{3,2,1,0:T(2,128)S(1)} %copy_multiply_fusion), channel_id=1, source_target_pairs={{0,2},{1,3},{2,4},{3,5},{4,6},{5,7},{6,8},{7,9},{8,10},{9,11},{10,... | collective-permute-start | bytes 98312 | tf_op jit(solution)/shard_map/ppermute | solution.py:399
  96.9 18.4 %collective-permute-start.7 = (f32[2,16,2,128]{3,2,1,0:T(2,128)S(1)}, f32[2,16,2,128]{3,2,1,0:T(2,128)S(1)}, u32[]{:S(2)}, u32[]{:S(2)}) collective-permute-start(f32[2,16,2,128]{3,2,1,0:T(2,128)S(1)} %copy_multiply_fusion), channel_id=1, source_target_pairs={{0,1},{1,2},{2,3},{3,4},{4,5},{5,6},{6,7},{7,8},{8,9},{9,10},{10,1... | collective-permute-start | bytes 98312 | tf_op jit(solution)/shard_map/ppermute | solution.py:399
  99.1 16.3 %collective-permute-start.8 = (f32[2,16,2,128]{3,2,1,0:T(2,128)S(1)}, f32[2,16,2,128]{3,2,1,0:T(2,128)S(1)}, u32[]{:S(2)}, u32[]{:S(2)}) collective-permute-start(f32[2,16,2,128]{3,2,1,0:T(2,128)S(1)} %copy_multiply_fusion), channel_id=1, source_target_pairs={{1,0},{2,1},{3,2},{4,3},{5,4},{6,5},{7,6},{8,7},{9,8},{10,9},{11,1... | collective-permute-start | bytes 98312 | tf_op jit(solution)/shard_map/ppermute | solution.py:400
  106.0 9.4 %collective-permute-start.9 = (f32[2,16,2,128]{3,2,1,0:T(2,128)S(1)}, f32[2,16,2,128]{3,2,1,0:T(2,128)S(1)}, u32[]{:S(2)}, u32[]{:S(2)}) collective-permute-start(f32[2,16,2,128]{3,2,1,0:T(2,128)S(1)} %copy_multiply_fusion), channel_id=1, source_target_pairs={{2,0},{3,1},{4,2},{5,3},{6,4},{7,5},{8,6},{9,7},{10,8},{11,9},{12,... | collective-permute-start | bytes 98312 | tf_op jit(solution)/shard_map/ppermute | solution.py:400
  108.2 7.3 %collective-permute-start.10 = (f32[2,16,2,128]{3,2,1,0:T(2,128)S(1)}, f32[2,16,2,128]{3,2,1,0:T(2,128)S(1)}, u32[]{:S(2)}, u32[]{:S(2)}) collective-permute-start(f32[2,16,2,128]{3,2,1,0:T(2,128)S(1)} %copy_multiply_fusion), channel_id=1, source_target_pairs={{3,0},{4,1},{5,2},{6,3},{7,4},{8,5},{9,6},{10,7},{11,8},{12,9},{13... | collective-permute-start | bytes 98312 | tf_op jit(solution)/shard_map/ppermute | solution.py:400
  110.1 5.8 %collective-permute-start.11 = (f32[2,16,2,128]{3,2,1,0:T(2,128)S(1)}, f32[2,16,2,128]{3,2,1,0:T(2,128)S(1)}, u32[]{:S(2)}, u32[]{:S(2)}) collective-permute-start(f32[2,16,2,128]{3,2,1,0:T(2,128)S(1)} %copy_multiply_fusion), channel_id=1, source_target_pairs={{4,0},{5,1},{6,2},{7,3},{8,4},{9,5},{10,6},{11,7},{12,8},{13,9},{1... | collective-permute-start | bytes 98312 | tf_op jit(solution)/shard_map/ppermute | solution.py:400
  124.4 1.9 %copy-start.5 = (f32[2,16,10,256]{3,2,1,0:T(8,128)S(1)}, f32[2,16,10,256]{3,2,1,0:T(8,128)}, u32[]{:S(2)}) copy-start(f32[2,16,10,256]{3,2,1,0:T(8,128)} %get-tuple-element.48) | copy-start | bytes 983044
  135.2 1.5 copy-start.4
  145.4 5.4 %copy-start.7 = (f32[2,8,512]{2,1,0:T(8,128)S(1)}, f32[2,8,512]{2,1,0:T(8,128)}, u32[]{:S(2)}) copy-start(f32[2,8,512]{2,1,0:T(8,128)} %param.11) | copy-start | bytes 98308
Sparse Core Ops, SparseCore 0:
  19.1 38.8 all-gather.2

commit v7 on v6

--- a/solution.py
+++ b/solution.py
@@ -101,14 +101,15 @@
     return (face_x[:, :, :-1], face_x[:, :, 1:], face_y[..., :-1], face_y[..., 1:], face_z, react_level, inverses, ratios)
 
 
-def sweep_kernel(w_ref, b_ref, fxl_ref, fxr_ref, fyl_ref, fyr_ref, fz_ref, re_ref, inv_ref, rat_ref, mask_ref, out_ref,
-                 *more, rows, cut_w, cut_b, cut_op, mode, scale, then):
+def sweep_kernel(w_ref, b_ref, fxl_ref, fxr_ref, fyl_ref, fyr_ref, fz_ref, re_ref, inv_ref, rat_ref, mask_ref, *more,
+                 rows, cut_w, cut_b, cut_op, mode, scale, then):
     lanes = (fxl_ref, fxr_ref, fyl_ref, fyr_ref, fz_ref, re_ref, inv_ref, rat_ref, scale)
+    out_ref = more[-2] if then is not None else more[-1]
     relax(w_ref, b_ref, lanes, mask_ref, out_ref, rows=rows, cut_w=cut_w, cut_b=cut_b, cut_op=cut_op, mode=mode)
     if then is not None:
-        res_cut_w, res_rows, res_cut_b, res_cut_op = then
-        relax(out_ref, b_ref, lanes, mask_ref, more[0], rows=res_rows, cut_w=res_cut_w, cut_b=res_cut_b,
-              cut_op=res_cut_op, mode="residual")
+        next_cut_w, next_rows, next_cut_b, next_cut_op, next_mode = then
+        relax(out_ref, b_ref, lanes, more[0], more[-1], rows=next_rows, cut_w=next_cut_w, cut_b=next_cut_b,
+              cut_op=next_cut_op, mode=next_mode)
 
 
 def coarse_kernel(b_ref, fxl_ref, fxr_ref, fyl_ref, fyr_ref, fz_ref, re_ref, inv_ref, rat_ref, mask_ref, out_ref, w_ref,
@@ -189,7 +190,8 @@
         out_ref[0, k] = jnp.where(keep, value, 0.0)
 
 
-def kernel_sweep(field_rim, target, lanes, cut_b, cut_op, mask, mode="sweep", cut_w=0, rows=None, then=None):
+def kernel_sweep(field_rim, target, lanes, cut_b, cut_op, mask, mode="sweep", cut_w=0, rows=None, then=None,
+                 next_mask=None):
     parts, layers, rows_rim, cols = field_rim.shape
     rows = rows_rim - 2 if rows is None else rows
     fxl, fxr, fyl, fyr, fz, re, inv, rat, scale = lanes
@@ -198,6 +200,10 @@
     operands = [field_rim, target, fxl, fxr, fyl, fyr, fz, re, inv, rat, mask]
     specs = [per_part(field_rim), per_part(target), whole(fxl), whole(fxr), whole(fyl), whole(fyr),
              whole(fz), whole(re), per_part(inv), per_part(rat), whole(mask)]
+    if then is not None:
+        next_mask = mask if next_mask is None else next_mask
+        operands.append(next_mask)
+        specs.append(whole(next_mask))
     body = functools.partial(
         sweep_kernel, rows=rows, cut_w=cut_w, cut_b=cut_b, cut_op=cut_op, mode=mode, scale=scale, then=then
     )
@@ -430,7 +436,7 @@
     op_0 = kernel_operator(eta_wide, react_wide, 0, 1)
     fine = kernel_sweep(guess_wide, misfit_wide, op_0, 1, 0, rows_inside(cells, 3, cells + 6, cols))
     fine, residual = kernel_sweep(
-        fine, misfit_wide, op_0, 2, 1, rows_inside(cells, 2, cells + 4, cols), then=(1, cells, 4, 3)
+        fine, misfit_wide, op_0, 2, 1, rows_inside(cells, 2, cells + 4, cols), then=(1, cells, 4, 3, "residual")
     )
     middle_rhs = restrict(residual)
 
@@ -442,7 +448,7 @@
     op_1 = kernel_operator(eta_1_wide, react_1_wide, 1)
     middle = kernel_sweep(rhs_wide, rhs_wide, op_1, 0, 0, rows_inside(half, half, 3 * half, wide), "zero", 0, 3 * half)
     middle, residual = kernel_sweep(
-        middle, rhs_wide, op_1, 1, 1, rows_inside(half, half - 1, 3 * half - 2, wide), then=(half - 2, half, half, half)
+        middle, rhs_wide, op_1, 1, 1, rows_inside(half, half - 1, 3 * half - 2, wide), then=(half - 2, half, half, half, "residual")
     )
     coarse_rhs = restrict(residual)
 
@@ -462,11 +468,15 @@
     lift = prolong(coarse_near)
     trim = 2 * reach - (half - 1)
     middle = middle + lift[:, :, trim : lift.shape[2] - trim]
-    middle = kernel_sweep(middle, rhs_wide, op_1, 2, 2, rows_inside(half, half - 2, 3 * half - 4, wide))
-    middle = kernel_sweep(middle, rhs_wide, op_1, 3, 3, rows_inside(half, half - 3, 3 * half - 6, wide))
+    middle = kernel_sweep(
+        middle, rhs_wide, op_1, 2, 2, rows_inside(half, half - 2, 3 * half - 4, wide),
+        then=(0, 3 * half - 6, 3, 3, "sweep"), next_mask=rows_inside(half, half - 3, 3 * half - 6, wide),
+    )[1]
     fine = fine + prolong(middle)
-    fine = kernel_sweep(fine, misfit_wide, op_0, 3, 2, rows_inside(cells, 1, cells + 2, cols))
-    fine = kernel_sweep(fine, misfit_wide, op_0, 4, 3, rows_inside(cells, 0, cells, cols))
+    fine = kernel_sweep(
+        fine, misfit_wide, op_0, 3, 2, rows_inside(cells, 1, cells + 2, cols),
+        then=(0, cells, 4, 3, "sweep"), next_mask=rows_inside(cells, 0, cells, cols),
+    )[1]
     grounded = (ice_mask == 2).astype(jnp.float32)
     gradient = -grounded * (forward_bed[0] * fine[0, 0] + forward_bed[1] * fine[1, 0])
     return (fine, gradient)

time: 162 us -> 156 us (0.963)
  Pallas kernels: 53.4 us -> 48.2 us
    pallas_call x8 -> x6, Pallas kernels: 37 us -> 31.8 us  [kernel_sweep(): pl.pallas_call(body, grid=(parts,), in_specs=specs, out_specs=out_specs,...]
where the time goes in v7:
time: 156 us; the launch traced here: 154 us
  Pallas kernels  48.2 us (31%)
  starting transfers between devices  33.8 us (22%)
  local copies, waits for them, and re-layouts  22.7 us (15%)
  between operations  14.8 us (9%)
  waiting for transfers between devices  14.6 us (9%)
  other arithmetic  11.9 us (8%)
  matrix products  7.8 us (5%)
    pallas_call x6, Pallas kernels, kernel_sweep(): pl.pallas_call(body, grid=(parts,), in_specs=specs, out_specs=out_specs,...  31.8 us
    ppermute x4, starting transfers between devices, nearby(): lax.ppermute(cells, 'gx', [(i, i + step) for i in range(count - step)])  11.2 us
    pallas_call x3, Pallas kernels, kernel_operator(): pl.pallas_call(body, grid=(2,), in_specs=[whole(eta_level), whole(react_l...  10.8 us
    ppermute x4, starting transfers between devices, nearby(): lax.ppermute(cells, 'gx', [(i + step, i) for i in range(count - step)])  10.6 us
    broadcast_in_dim x9, local copies, waits for them, and re-layouts, rows_inside(): jnp.broadcast_to(inside(cells, halo, extent)[0, 0], (extent, cols))  6.06 us
    ppermute x1, waiting for transfers between devices, trade(): lax.ppermute(pack(tails), 'gx', [(i, i + 1) for i in range(ends)])  5.77 us
    pallas_call x1, Pallas kernels, kernel_coarse(): pl.pallas_call(body, grid=(parts,), in_specs=specs, out_specs=pl.BlockSpe...  5.64 us
    ppermute x1, starting transfers between devices, with_halo(): lax.ppermute(tail, axis, [(i, (i + 1) % count) for i in range(ends)])  5.37 us
  transfers between devices with their start and end apart: 13, of which 4 were waited for; matrix products, arithmetic and copies ran while one was open for 11% of the time, Pallas kernels for 13%

profile of v7, /device:TPU:10, one launch (start us, length us, event | category | flops | bytes accessed | tf_op | source)
XLA Modules:
  0.0 153.8 jit_solution(15304724464492598098)
XLA Ops:
  11.5 2.7 %collective-permute-start.1 = (f32[167936]{0:T(1024)}, f32[167936]{0:T(1024)S(1)}, u32[]{:S(2)}, u32[]{:S(2)}) collective-permute-start(f32[167936]{0:T(1024)} %pad_maximum_fusion.3), channel_id=1, source_target_pairs={{1,0},{2,1},{3,2},{4,3},{5,4},{6,5},{7,6},{8,7},{9,8},{10,9},{11,1... | collective-permute-start | bytes 2015240 | tf_op jit(solution)/shard_map/ppermute | solution.py:43
  19.2 3.7 %collective-permute-done.1 = f32[167936]{0:T(1024)S(1)} collective-permute-done((f32[167936]{0:T(1024)}, f32[167936]{0:T(1024)S(1)}, u32[]{:S(2)}, u32[]{:S(2)}) %collective-permute-start.1) | collective-permute-done | bytes 671776 | tf_op jit(solution)/shard_map/ppermute | solution.py:43
  23.0 5.8 %collective-permute-done = f32[167936]{0:T(1024)} collective-permute-done((f32[167936]{0:T(1024)}, f32[167936]{0:T(1024)}, u32[]{:S(2)}, u32[]{:S(2)}) %collective-permute-start) | collective-permute-done | bytes 671776 | tf_op jit(solution)/shard_map/ppermute | solution.py:42
  33.6 5.0 %shard_map.77 = (f32[16,14,512]{2,1,0:T(8,128)}, f32[16,14,512]{2,1,0:T(8,128)}, f32[16,14,512]{2,1,0:T(8,128)}, f32[16,14,512]{2,1,0:T(8,128)}, f32[15,14,512]{...) custom-call(f32[16,16,512]{2,1,0:T(8,128)} %pad_maximum_fusion.4.eta_ref, ...), custom_call_target="tpu_custom_call" | custom-call | tf_op jit(solution)/shard_map/pallas_call | solution.py:289
  41.1 5.6 %shard_map.78.w_ref = f32[2,16,14,512]{3,2,1,0:T(8,128)} custom-call(f32[2,16,16,512]{3,2,1,0:T(8,128)} %get-tuple-element.77.w_ref, f32[2,16,16,512]{3,2,1,0:T(8,128)} %get-tuple-element.78.b_ref, f32[16,14,512]{2,1,0:T(8,128)} %get-tuple-element.32.fxl_ref, f32[16,14,512]{2,1,0:T(8,128)} %get-tuple-element.33.fxr_ref, ...), custom_call_target="tpu_custom_call" | custom-call | tf_op jit(solution)/shard_map/pallas_call | solution.py:215
  47.3 7.4 %shard_map.79 = (f32[2,16,12,512]{3,2,1,0:T(8,128)}, f32[2,16,8,512]{3,2,1,0:T(8,128)}) custom-call(f32[2,16,14,512]{3,2,1,0:T(8,128)} %shard_map.78.w_ref, f32[2,16,16,512]{3,2,1,0:T(8,128)} %get-tuple-element.78.b_ref, f32[16,14,512]{2,1,0:T(8,128)} %get-tuple-element.32.fxl_ref, f32[16,14,512]{2,1,0:T(8,128)} %get-tuple-element.33.fxr_ref, ...), custom_call_target="tpu_custom_call" | custom-call | tf_op jit(solution)/shard_map/pallas_call | solution.py:215
  56.9 1.9 %collective-permute-start.3 = (f32[2,16,4,256]{3,2,1,0:T(4,128)S(1)}, f32[2,16,4,256]{3,2,1,0:T(4,128)S(1)}, u32[]{:S(2)}, u32[]{:S(2)}) collective-permute-start(f32[2,16,4,256]{3,2,1,0:T(4,128)S(1)} %broadcast_multiply_fusion.1), channel_id=1, source_target_pairs={{1,0},{2,1},{3,2},{4,3},{5,4},{6,5},{7,6},{8,7},{9,8},{10,9},{11,1... | collective-permute-start | bytes 393224 | tf_op jit(solution)/shard_map/ppermute | solution.py:29
  58.8 5.4 %collective-permute-start.2 = (f32[2,16,4,256]{3,2,1,0:T(4,128)S(1)}, f32[2,16,4,256]{3,2,1,0:T(4,128)S(1)}, u32[]{:S(2)}, u32[]{:S(2)}) collective-permute-start(f32[2,16,4,256]{3,2,1,0:T(4,128)S(1)} %broadcast_multiply_fusion.1), channel_id=1, source_target_pairs={{0,1},{1,2},{2,3},{3,4},{4,5},{5,6},{6,7},{7,8},{8,9},{9,10},{10,1... | collective-permute-start | bytes 393224 | tf_op jit(solution)/shard_map/ppermute | solution.py:27
  64.2 4.6 %collective-permute-done.2 = f32[2,16,4,256]{3,2,1,0:T(4,128)S(1)} collective-permute-done((f32[2,16,4,256]{3,2,1,0:T(4,128)S(1)}, f32[2,16,4,256]{3,2,1,0:T(4,128)S(1)}, u32[]{:S(2)}, u32[]{:S(2)}) %collective-permute-start.2) | collective-permute-done | bytes 131104 | tf_op jit(solution)/shard_map/ppermute | solution.py:27
  75.7 3.3 %shard_map.80 = (f32[16,12,256]{2,1,0:T(8,128)}, f32[16,12,256]{2,1,0:T(8,128)}, f32[16,12,256]{2,1,0:T(8,128)}, f32[16,12,256]{2,1,0:T(8,128)}, f32[15,12,256]{...) custom-call(f32[16,14,256]{2,1,0:T(8,128)} %pad_dynamic-slice_fusion.eta_ref, ...), custom_call_target="tpu_custom_call" | custom-call | tf_op jit(solution)/shard_map/pallas_call | solution.py:289
  79.7 2.9 %shard_map.81.w_ref = f32[2,16,12,256]{3,2,1,0:T(8,128)} custom-call(f32[2,16,12,256]{3,2,1,0:T(8,128)} %pad_maximum_fusion.5.w_ref.b_ref, f32[2,16,12,256]{3,2,1,0:T(8,128)} %pad_maximum_fusion.5.w_ref.b_ref, f32[16,12,256]{2,1,0:T(8,128)} %get-tuple-element.42.fxl_ref, f32[16,12,256]{2,1,0:T(8,128)} %get-tuple-element.43.fxr_ref, ...), custom_call_target="tpu_custom_call" | custom-call | tf_op jit(solution)/shard_map/pallas_call | solution.py:215
  83.3 4.0 %shard_map.82 = (f32[2,16,10,256]{3,2,1,0:T(8,128)}, f32[2,16,4,256]{3,2,1,0:T(4,128)}) custom-call(f32[2,16,12,256]{3,2,1,0:T(8,128)} %shard_map.81.w_ref, f32[2,16,12,256]{3,2,1,0:T(8,128)} %pad_maximum_fusion.5.w_ref.b_ref, f32[16,12,256]{2,1,0:T(8,128)} %get-tuple-element.42.fxl_ref, f32[16,12,256]{2,1,0:T(8,128)} %get-tuple-element.43.fxr_ref, ...), custom_call_target="tpu_custom_call" | custom-call | tf_op jit(solution)/shard_map/pallas_call | solution.py:215
  88.5 3.5 %collective-permute-start.4 = (f32[2,16,2,128]{3,2,1,0:T(2,128)S(1)}, f32[2,16,2,128]{3,2,1,0:T(2,128)S(1)}, u32[]{:S(2)}, u32[]{:S(2)}) collective-permute-start(f32[2,16,2,128]{3,2,1,0:T(2,128)S(1)} %copy_multiply_fusion), channel_id=1, source_target_pairs={{0,4},{1,5},{2,6},{3,7},{4,8},{5,9},{6,10},{7,11},{8,12},{9,13},{1... | collective-permute-start | bytes 98312 | tf_op jit(solution)/shard_map/ppermute | solution.py:405
  92.0 1.9 %collective-permute-start.5 = (f32[2,16,2,128]{3,2,1,0:T(2,128)S(1)}, f32[2,16,2,128]{3,2,1,0:T(2,128)S(1)}, u32[]{:S(2)}, u32[]{:S(2)}) collective-permute-start(f32[2,16,2,128]{3,2,1,0:T(2,128)S(1)} %copy_multiply_fusion), channel_id=1, source_target_pairs={{0,3},{1,4},{2,5},{3,6},{4,7},{5,8},{6,9},{7,10},{8,11},{9,12},{10... | collective-permute-start | bytes 98312 | tf_op jit(solution)/shard_map/ppermute | solution.py:405
  93.9 3.7 %collective-permute-start.6 = (f32[2,16,2,128]{3,2,1,0:T(2,128)S(1)}, f32[2,16,2,128]{3,2,1,0:T(2,128)S(1)}, u32[]{:S(2)}, u32[]{:S(2)}) collective-permute-start(f32[2,16,2,128]{3,2,1,0:T(2,128)S(1)} %copy_multiply_fusion), channel_id=1, source_target_pairs={{0,2},{1,3},{2,4},{3,5},{4,6},{5,7},{6,8},{7,9},{8,10},{9,11},{10,... | collective-permute-start | bytes 98312 | tf_op jit(solution)/shard_map/ppermute | solution.py:405
  97.6 2.1 %collective-permute-start.7 = (f32[2,16,2,128]{3,2,1,0:T(2,128)S(1)}, f32[2,16,2,128]{3,2,1,0:T(2,128)S(1)}, u32[]{:S(2)}, u32[]{:S(2)}) collective-permute-start(f32[2,16,2,128]{3,2,1,0:T(2,128)S(1)} %copy_multiply_fusion), channel_id=1, source_target_pairs={{0,1},{1,2},{2,3},{3,4},{4,5},{5,6},{6,7},{7,8},{8,9},{9,10},{10,1... | collective-permute-start | bytes 98312 | tf_op jit(solution)/shard_map/ppermute | solution.py:405
  99.7 4.3 %collective-permute-start.8 = (f32[2,16,2,128]{3,2,1,0:T(2,128)S(1)}, f32[2,16,2,128]{3,2,1,0:T(2,128)S(1)}, u32[]{:S(2)}, u32[]{:S(2)}) collective-permute-start(f32[2,16,2,128]{3,2,1,0:T(2,128)S(1)} %copy_multiply_fusion), channel_id=1, source_target_pairs={{1,0},{2,1},{3,2},{4,3},{5,4},{6,5},{7,6},{8,7},{9,8},{10,9},{11,1... | collective-permute-start | bytes 98312 | tf_op jit(solution)/shard_map/ppermute | solution.py:406
  106.6 2.2 %collective-permute-start.9 = (f32[2,16,2,128]{3,2,1,0:T(2,128)S(1)}, f32[2,16,2,128]{3,2,1,0:T(2,128)S(1)}, u32[]{:S(2)}, u32[]{:S(2)}) collective-permute-start(f32[2,16,2,128]{3,2,1,0:T(2,128)S(1)} %copy_multiply_fusion), channel_id=1, source_target_pairs={{2,0},{3,1},{4,2},{5,3},{6,4},{7,5},{8,6},{9,7},{10,8},{11,9},{12,... | collective-permute-start | bytes 98312 | tf_op jit(solution)/shard_map/ppermute | solution.py:406
  110.8 2.1 %collective-permute-start.11 = (f32[2,16,2,128]{3,2,1,0:T(2,128)S(1)}, f32[2,16,2,128]{3,2,1,0:T(2,128)S(1)}, u32[]{:S(2)}, u32[]{:S(2)}) collective-permute-start(f32[2,16,2,128]{3,2,1,0:T(2,128)S(1)} %copy_multiply_fusion), channel_id=1, source_target_pairs={{4,0},{5,1},{6,2},{7,3},{8,4},{9,5},{10,6},{11,7},{12,8},{13,9},{1... | collective-permute-start | bytes 98312 | tf_op jit(solution)/shard_map/ppermute | solution.py:406
  113.5 2.5 %shard_map.83 = (f32[16,18,128]{2,1,0:T(8,128)}, f32[16,18,128]{2,1,0:T(8,128)}, f32[16,18,128]{2,1,0:T(8,128)}, f32[16,18,128]{2,1,0:T(8,128)}, f32[15,18,128]{...) custom-call(f32[16,20,128]{2,1,0:T(8,128)} %pad_dynamic-slice_fusion.1.eta_ref, ...), custom_call_target="tpu_custom_call" | custom-call | tf_op jit(solution)/shard_map/pallas_call | solution.py:289
  116.6 2.2 %concatenate.35.b_ref = f32[2,16,18,128]{3,2,1,0:T(8,128)} concatenate(f32[2,16,2,128]{3,2,1,0:T(2,128)S(1)} %collective-permute-done.4, f32[2,16,2,128]{3,2,1,0:T(2,128)S(1)} %collective-permute-done.5, f32[2,16,2,128]{3,2,1,0:T(2,128)S(1)} %collective-permute-done.6, f32[2,16,2,128]{3,2,1,0:T(2,128)S(1)} %collective-permute-done.7, f32[2,16,2,128]{3,2,1,0:T(2,128)S(1)} %copy_multiply_fusion, ...), dimensions={2} | concatenate | bytes 589824 | tf_op jit(solution)/shard_map/concatenate | solution.py:407
  119.5 5.6 %shard_map.84 = f32[2,16,18,128]{3,2,1,0:T(8,128)} custom-call(f32[2,16,18,128]{3,2,1,0:T(8,128)} %concatenate.35.b_ref, f32[16,18,128]{2,1,0:T(8,128)} %get-tuple-element.52.fxl_ref, f32[16,18,128]{2,1,0:T(8,128)} %get-tuple-element.53.fxr_ref, f32[16,18,128]{2,1,0:T(8,128)} %get-tuple-element.54.fyl_ref, f32[16,18,128]{2,1,0:T(8,128)} %get-tuple-element.55.fyr_ref, ...), custom_call_target="tpu_custom_call" | custom-call | tf_op jit(solution)/shard_map/pallas_call | solution.py:308
  129.3 4.1 %shard_map.85 = (f32[2,16,8,256]{3,2,1,0:T(8,128)}, f32[2,16,6,256]{3,2,1,0:T(8,128)}) custom-call(f32[2,16,10,256]{3,2,1,0:T(8,128)} %slice_add_fusion.w_ref, f32[2,16,12,256]{3,2,1,0:T(8,128)} %pad_maximum_fusion.5.w_ref.b_ref, f32[16,12,256]{2,1,0:T(8,128)} %get-tuple-element.42.fxl_ref, f32[16,12,256]{2,1,0:T(8,128)} %get-tuple-element.43.fxr_ref, ...), custom_call_target="tpu_custom_call" | custom-call | tf_op jit(solution)/shard_map/pallas_call | solution.py:215
  137.9 7.8 %shard_map.86 = (f32[2,16,10,512]{3,2,1,0:T(8,128)}, f32[2,16,8,512]{3,2,1,0:T(8,128)}) custom-call(f32[2,16,12,512]{3,2,1,0:T(8,128)} %copy_add_fusion.w_ref, f32[2,16,16,512]{3,2,1,0:T(8,128)} %get-tuple-element.78.b_ref, f32[16,14,512]{2,1,0:T(8,128)} %get-tuple-element.32.fxl_ref, f32[16,14,512]{2,1,0:T(8,128)} %get-tuple-element.33.fxr_ref, ...), custom_call_target="tpu_custom_call" | custom-call | tf_op jit(solution)/shard_map/pallas_call | solution.py:215
  (132 shorter events, 44.6 us)
Async XLA Ops:
  7.2 2.5 %copy-start.2 = (f32[2,16,8,512]{3,2,1,0:T(8,128)S(1)}, f32[2,16,8,512]{3,2,1,0:T(8,128)}, u32[]{:S(2)}) copy-start(f32[2,16,8,512]{3,2,1,0:T(8,128)} %param.7) | copy-start | bytes 1572868
  7.2 62.5 %all-gather.3.cloned.1.call-start = ((), (), s32[]{:S(2)}) async-start(), calls=%async_computation | async-start | bytes 1253376 | tf_op jit(solution)/shard_map/all_gather | solution.py:420
  8.1 10.9 %copy-start.6 = (f32[16,8,512]{2,1,0:T(8,128)}, f32[16,8,512]{2,1,0:T(8,128)S(1)}, u32[]{:S(2)}) copy-start(f32[16,8,512]{2,1,0:T(8,128)S(1)} %multiply_add_fusion) | copy-start | bytes 786436
  9.5 1.0 copy-start.3
  11.5 11.4 %collective-permute-start.1 = (f32[167936]{0:T(1024)}, f32[167936]{0:T(1024)S(1)}, u32[]{:S(2)}, u32[]{:S(2)}) collective-permute-start(f32[167936]{0:T(1024)} %pad_maximum_fusion.3), channel_id=1, source_target_pairs={{1,0},{2,1},{3,2},{4,3},{5,4},{6,5},{7,6},{8,7},{9,8},{10,9},{11,1... | collective-permute-start | bytes 2015240 | tf_op jit(solution)/shard_map/ppermute | solution.py:43
  15.4 13.4 %collective-permute-start = (f32[167936]{0:T(1024)}, f32[167936]{0:T(1024)}, u32[]{:S(2)}, u32[]{:S(2)}) collective-permute-start(f32[167936]{0:T(1024)} %pad_maximum_fusion.2), channel_id=1, source_target_pairs={{0,1},{1,2},{2,3},{3,4},{4,5},{5,6},{6,7},{7,8},{8,9},{9,10},{10,1... | collective-permute-start | bytes 2015240 | tf_op jit(solution)/shard_map/ppermute | solution.py:42
  29.9 2.1 %slice-start.1 = ((f32[16,8,512]{2,1,0:T(8,128)}), f32[2,8,512]{2,1,0:T(8,128)S(1)}, s32[]{:S(2)}) async-start(f32[16,8,512]{2,1,0:T(8,128)} %copy-done.6), calls=%async_computation.2 | async-start | bytes 65536 | tf_op jit(solution)/shard_map/slice | solution.py:414
  30.2 8.4 %copy-start.1 = (f32[2,16,8,512]{3,2,1,0:T(8,128)S(1)}, f32[2,16,8,512]{3,2,1,0:T(8,128)}, u32[]{:S(2)}) copy-start(f32[2,16,8,512]{3,2,1,0:T(8,128)} %param.6) | copy-start | bytes 1572868
  56.9 7.3 %collective-permute-start.3 = (f32[2,16,4,256]{3,2,1,0:T(4,128)S(1)}, f32[2,16,4,256]{3,2,1,0:T(4,128)S(1)}, u32[]{:S(2)}, u32[]{:S(2)}) collective-permute-start(f32[2,16,4,256]{3,2,1,0:T(4,128)S(1)} %broadcast_multiply_fusion.1), channel_id=1, source_target_pairs={{1,0},{2,1},{3,2},{4,3},{5,4},{6,5},{7,6},{8,7},{9,8},{10,9},{11,1... | collective-permute-start | bytes 393224 | tf_op jit(solution)/shard_map/ppermute | solution.py:29
  58.8 10.0 %collective-permute-start.2 = (f32[2,16,4,256]{3,2,1,0:T(4,128)S(1)}, f32[2,16,4,256]{3,2,1,0:T(4,128)S(1)}, u32[]{:S(2)}, u32[]{:S(2)}) collective-permute-start(f32[2,16,4,256]{3,2,1,0:T(4,128)S(1)} %broadcast_multiply_fusion.1), channel_id=1, source_target_pairs={{0,1},{1,2},{2,3},{3,4},{4,5},{5,6},{6,7},{7,8},{8,9},{9,10},{10,1... | collective-permute-start | bytes 393224 | tf_op jit(solution)/shard_map/ppermute | solution.py:27
  71.2 1.1 copy-start
  73.3 0.9 slice-start
  88.5 18.1 %collective-permute-start.4 = (f32[2,16,2,128]{3,2,1,0:T(2,128)S(1)}, f32[2,16,2,128]{3,2,1,0:T(2,128)S(1)}, u32[]{:S(2)}, u32[]{:S(2)}) collective-permute-start(f32[2,16,2,128]{3,2,1,0:T(2,128)S(1)} %copy_multiply_fusion), channel_id=1, source_target_pairs={{0,4},{1,5},{2,6},{3,7},{4,8},{5,9},{6,10},{7,11},{8,12},{9,13},{1... | collective-permute-start | bytes 98312 | tf_op jit(solution)/shard_map/ppermute | solution.py:405
  92.0 16.8 %collective-permute-start.5 = (f32[2,16,2,128]{3,2,1,0:T(2,128)S(1)}, f32[2,16,2,128]{3,2,1,0:T(2,128)S(1)}, u32[]{:S(2)}, u32[]{:S(2)}) collective-permute-start(f32[2,16,2,128]{3,2,1,0:T(2,128)S(1)} %copy_multiply_fusion), channel_id=1, source_target_pairs={{0,3},{1,4},{2,5},{3,6},{4,7},{5,8},{6,9},{7,10},{8,11},{9,12},{10... | collective-permute-start | bytes 98312 | tf_op jit(solution)/shard_map/ppermute | solution.py:405
  93.9 16.8 %collective-permute-start.6 = (f32[2,16,2,128]{3,2,1,0:T(2,128)S(1)}, f32[2,16,2,128]{3,2,1,0:T(2,128)S(1)}, u32[]{:S(2)}, u32[]{:S(2)}) collective-permute-start(f32[2,16,2,128]{3,2,1,0:T(2,128)S(1)} %copy_multiply_fusion), channel_id=1, source_target_pairs={{0,2},{1,3},{2,4},{3,5},{4,6},{5,7},{6,8},{7,9},{8,10},{9,11},{10,... | collective-permute-start | bytes 98312 | tf_op jit(solution)/shard_map/ppermute | solution.py:405
  97.6 18.4 %collective-permute-start.7 = (f32[2,16,2,128]{3,2,1,0:T(2,128)S(1)}, f32[2,16,2,128]{3,2,1,0:T(2,128)S(1)}, u32[]{:S(2)}, u32[]{:S(2)}) collective-permute-start(f32[2,16,2,128]{3,2,1,0:T(2,128)S(1)} %copy_multiply_fusion), channel_id=1, source_target_pairs={{0,1},{1,2},{2,3},{3,4},{4,5},{5,6},{6,7},{7,8},{8,9},{9,10},{10,1... | collective-permute-start | bytes 98312 | tf_op jit(solution)/shard_map/ppermute | solution.py:405
  99.7 16.3 %collective-permute-start.8 = (f32[2,16,2,128]{3,2,1,0:T(2,128)S(1)}, f32[2,16,2,128]{3,2,1,0:T(2,128)S(1)}, u32[]{:S(2)}, u32[]{:S(2)}) collective-permute-start(f32[2,16,2,128]{3,2,1,0:T(2,128)S(1)} %copy_multiply_fusion), channel_id=1, source_target_pairs={{1,0},{2,1},{3,2},{4,3},{5,4},{6,5},{7,6},{8,7},{9,8},{10,9},{11,1... | collective-permute-start | bytes 98312 | tf_op jit(solution)/shard_map/ppermute | solution.py:406
  106.6 9.4 %collective-permute-start.9 = (f32[2,16,2,128]{3,2,1,0:T(2,128)S(1)}, f32[2,16,2,128]{3,2,1,0:T(2,128)S(1)}, u32[]{:S(2)}, u32[]{:S(2)}) collective-permute-start(f32[2,16,2,128]{3,2,1,0:T(2,128)S(1)} %copy_multiply_fusion), channel_id=1, source_target_pairs={{2,0},{3,1},{4,2},{5,3},{6,4},{7,5},{8,6},{9,7},{10,8},{11,9},{12,... | collective-permute-start | bytes 98312 | tf_op jit(solution)/shard_map/ppermute | solution.py:406
  108.8 7.2 %collective-permute-start.10 = (f32[2,16,2,128]{3,2,1,0:T(2,128)S(1)}, f32[2,16,2,128]{3,2,1,0:T(2,128)S(1)}, u32[]{:S(2)}, u32[]{:S(2)}) collective-permute-start(f32[2,16,2,128]{3,2,1,0:T(2,128)S(1)} %copy_multiply_fusion), channel_id=1, source_target_pairs={{3,0},{4,1},{5,2},{6,3},{7,4},{8,5},{9,6},{10,7},{11,8},{12,9},{13... | collective-permute-start | bytes 98312 | tf_op jit(solution)/shard_map/ppermute | solution.py:406
  110.8 5.8 %collective-permute-start.11 = (f32[2,16,2,128]{3,2,1,0:T(2,128)S(1)}, f32[2,16,2,128]{3,2,1,0:T(2,128)S(1)}, u32[]{:S(2)}, u32[]{:S(2)}) collective-permute-start(f32[2,16,2,128]{3,2,1,0:T(2,128)S(1)} %copy_multiply_fusion), channel_id=1, source_target_pairs={{4,0},{5,1},{6,2},{7,3},{8,4},{9,5},{10,6},{11,7},{12,8},{13,9},{1... | collective-permute-start | bytes 98312 | tf_op jit(solution)/shard_map/ppermute | solution.py:406
  125.1 1.9 %copy-start.5 = (f32[2,16,10,256]{3,2,1,0:T(8,128)S(1)}, f32[2,16,10,256]{3,2,1,0:T(8,128)}, u32[]{:S(2)}) copy-start(f32[2,16,10,256]{3,2,1,0:T(8,128)} %get-tuple-element.50) | copy-start | bytes 983044
  133.4 1.5 copy-start.4
  137.8 7.8 %copy-start.7 = (f32[2,8,512]{2,1,0:T(8,128)S(1)}, f32[2,8,512]{2,1,0:T(8,128)}, u32[]{:S(2)}) copy-start(f32[2,8,512]{2,1,0:T(8,128)} %param.11) | copy-start | bytes 98308
Sparse Core Ops, SparseCore 0:
  19.1 38.7 all-gather.2

commit v8 on v7

--- a/solution.py
+++ b/solution.py
@@ -104,12 +104,12 @@
 def sweep_kernel(w_ref, b_ref, fxl_ref, fxr_ref, fyl_ref, fyr_ref, fz_ref, re_ref, inv_ref, rat_ref, mask_ref, *more,
                  rows, cut_w, cut_b, cut_op, mode, scale, then):
     lanes = (fxl_ref, fxr_ref, fyl_ref, fyr_ref, fz_ref, re_ref, inv_ref, rat_ref, scale)
-    out_ref = more[-2] if then is not None else more[-1]
-    relax(w_ref, b_ref, lanes, mask_ref, out_ref, rows=rows, cut_w=cut_w, cut_b=cut_b, cut_op=cut_op, mode=mode)
-    if then is not None:
-        next_cut_w, next_rows, next_cut_b, next_cut_op, next_mode = then
-        relax(out_ref, b_ref, lanes, more[0], more[-1], rows=next_rows, cut_w=next_cut_w, cut_b=next_cut_b,
-              cut_op=next_cut_op, mode=next_mode)
+    steps = len(then)
+    masks, outs = more[:steps], more[steps:]
+    relax(w_ref, b_ref, lanes, mask_ref, outs[0], rows=rows, cut_w=cut_w, cut_b=cut_b, cut_op=cut_op, mode=mode)
+    for step, (next_cut_w, next_rows, next_cut_b, next_cut_op, next_mode) in enumerate(then):
+        relax(outs[step], b_ref, lanes, masks[step], outs[step + 1], rows=next_rows, cut_w=next_cut_w,
+              cut_b=next_cut_b, cut_op=next_cut_op, mode=next_mode)
 
 
 def coarse_kernel(b_ref, fxl_ref, fxr_ref, fyl_ref, fyr_ref, fz_ref, re_ref, inv_ref, rat_ref, mask_ref, out_ref, w_ref,
@@ -190,8 +190,8 @@
         out_ref[0, k] = jnp.where(keep, value, 0.0)
 
 
-def kernel_sweep(field_rim, target, lanes, cut_b, cut_op, mask, mode="sweep", cut_w=0, rows=None, then=None,
-                 next_mask=None):
+def kernel_sweep(field_rim, target, lanes, cut_b, cut_op, mask, mode="sweep", cut_w=0, rows=None, then=(),
+                 masks=()):
     parts, layers, rows_rim, cols = field_rim.shape
     rows = rows_rim - 2 if rows is None else rows
     fxl, fxr, fyl, fyr, fz, re, inv, rat, scale = lanes
@@ -200,20 +200,19 @@
     operands = [field_rim, target, fxl, fxr, fyl, fyr, fz, re, inv, rat, mask]
     specs = [per_part(field_rim), per_part(target), whole(fxl), whole(fxr), whole(fyl), whole(fyr),
              whole(fz), whole(re), per_part(inv), per_part(rat), whole(mask)]
-    if then is not None:
-        next_mask = mask if next_mask is None else next_mask
-        operands.append(next_mask)
-        specs.append(whole(next_mask))
+    masks = list(masks) + [mask] * (len(then) - len(masks))
+    operands += masks
+    specs += [whole(m) for m in masks]
     body = functools.partial(
         sweep_kernel, rows=rows, cut_w=cut_w, cut_b=cut_b, cut_op=cut_op, mode=mode, scale=scale, then=then
     )
     out_specs = [pl.BlockSpec((1, layers, rows, cols), lambda c: (c, 0, 0, 0))]
     out_shape = [jax.ShapeDtypeStruct((parts, layers, rows, cols), jnp.float32)]
-    if then is not None:
-        out_specs.append(pl.BlockSpec((1, layers, then[1], cols), lambda c: (c, 0, 0, 0)))
-        out_shape.append(jax.ShapeDtypeStruct((parts, layers, then[1], cols), jnp.float32))
+    for step in then:
+        out_specs.append(pl.BlockSpec((1, layers, step[1], cols), lambda c: (c, 0, 0, 0)))
+        out_shape.append(jax.ShapeDtypeStruct((parts, layers, step[1], cols), jnp.float32))
     outs = pl.pallas_call(body, grid=(parts,), in_specs=specs, out_specs=out_specs, out_shape=out_shape)(*operands)
-    return tuple(outs) if then is not None else outs[0]
+    return tuple(outs) if then else outs[0]
 
 
 def build_kernel(eta_ref, re_ref, fxl_ref, fxr_ref, fyl_ref, fyr_ref, fz_ref, reo_ref, inv_ref, rat_ref,
@@ -434,9 +433,10 @@
         [(viscosity, 1), (adjoint_guess, 2), (misfit, 2), (react_pair, 1)], halo
     )
     op_0 = kernel_operator(eta_wide, react_wide, 0, 1)
-    fine = kernel_sweep(guess_wide, misfit_wide, op_0, 1, 0, rows_inside(cells, 3, cells + 6, cols))
-    fine, residual = kernel_sweep(
-        fine, misfit_wide, op_0, 2, 1, rows_inside(cells, 2, cells + 4, cols), then=(1, cells, 4, 3, "residual")
+    _, fine, residual = kernel_sweep(
+        guess_wide, misfit_wide, op_0, 1, 0, rows_inside(cells, 3, cells + 6, cols),
+        then=((0, cells + 4, 2, 1, "sweep"), (1, cells, 4, 3, "residual")),
+        masks=(rows_inside(cells, 2, cells + 4, cols),),
     )
     middle_rhs = restrict(residual)
 
@@ -446,9 +446,10 @@
     eta_1_wide = window(eta_1_all, 1, where * half, 3 * half + 2, half + 1)
     react_1_wide = window(react_1_all, 1, where * half, 3 * half, half)
     op_1 = kernel_operator(eta_1_wide, react_1_wide, 1)
-    middle = kernel_sweep(rhs_wide, rhs_wide, op_1, 0, 0, rows_inside(half, half, 3 * half, wide), "zero", 0, 3 * half)
-    middle, residual = kernel_sweep(
-        middle, rhs_wide, op_1, 1, 1, rows_inside(half, half - 1, 3 * half - 2, wide), then=(half - 2, half, half, half, "residual")
+    _, middle, residual = kernel_sweep(
+        rhs_wide, rhs_wide, op_1, 0, 0, rows_inside(half, half, 3 * half, wide), "zero", 0, 3 * half,
+        then=((0, 3 * half - 2, 1, 1, "sweep"), (half - 2, half, half, half, "residual")),
+        masks=(rows_inside(half, half - 1, 3 * half - 2, wide),),
     )
     coarse_rhs = restrict(residual)
 
@@ -470,12 +471,12 @@
     middle = middle + lift[:, :, trim : lift.shape[2] - trim]
     middle = kernel_sweep(
         middle, rhs_wide, op_1, 2, 2, rows_inside(half, half - 2, 3 * half - 4, wide),
-        then=(0, 3 * half - 6, 3, 3, "sweep"), next_mask=rows_inside(half, half - 3, 3 * half - 6, wide),
+        then=((0, 3 * half - 6, 3, 3, "sweep"),), masks=(rows_inside(half, half - 3, 3 * half - 6, wide),),
     )[1]
     fine = fine + prolong(middle)
     fine = kernel_sweep(
         fine, misfit_wide, op_0, 3, 2, rows_inside(cells, 1, cells + 2, cols),
-        then=(0, cells, 4, 3, "sweep"), next_mask=rows_inside(cells, 0, cells, cols),
+        then=((0, cells, 4, 3, "sweep"),), masks=(rows_inside(cells, 0, cells, cols),),
     )[1]
     grounded = (ice_mask == 2).astype(jnp.float32)
     gradient = -grounded * (forward_bed[0] * fine[0, 0] + forward_bed[1] * fine[1, 0])

time: 156 us -> 150 us (0.962)
  Pallas kernels: 48.2 us -> 42.1 us
    pallas_call x6 -> x4, Pallas kernels: 31.8 us -> 25.6 us  [kernel_sweep(): pl.pallas_call(body, grid=(parts,), in_specs=specs, out_specs=out_specs,...]
  transfers between devices with their start and end apart: 13 -> 13, of which waited for: 4 -> 4; matrix products, arithmetic and copies ran while one was open for 11% -> 11% of each run, Pallas kernels for 13% -> 11%
where the time goes in v8:
time: 150 us; the launch traced here: 148 us
  Pallas kernels  42.1 us (28%)
  starting transfers between devices  33.6 us (22%)
  local copies, waits for them, and re-layouts  22.7 us (15%)
  waiting for transfers between devices  14.8 us (10%)
  between operations  14.8 us (10%)
  other arithmetic  12 us (8%)
  matrix products  7.8 us (5%)
    pallas_call x4, Pallas kernels, kernel_sweep(): pl.pallas_call(body, grid=(parts,), in_specs=specs, out_specs=out_specs,...  25.6 us
    ppermute x4, starting transfers between devices, nearby(): lax.ppermute(cells, 'gx', [(i, i + step) for i in range(count - step)])  11 us
    pallas_call x3, Pallas kernels, kernel_operator(): pl.pallas_call(body, grid=(2,), in_specs=[whole(eta_level), whole(react_l...  10.8 us
    ppermute x4, starting transfers between devices, nearby(): lax.ppermute(cells, 'gx', [(i + step, i) for i in range(count - step)])  10.7 us
    broadcast_in_dim x9, local copies, waits for them, and re-layouts, rows_inside(): jnp.broadcast_to(inside(cells, halo, extent)[0, 0], (extent, cols))  6.04 us
    ppermute x1, waiting for transfers between devices, trade(): lax.ppermute(pack(tails), 'gx', [(i, i + 1) for i in range(ends)])  5.77 us
    pallas_call x1, Pallas kernels, kernel_coarse(): pl.pallas_call(body, grid=(parts,), in_specs=specs, out_specs=pl.BlockSpe...  5.64 us
    ppermute x1, starting transfers between devices, with_halo(): lax.ppermute(tail, axis, [(i, (i + 1) % count) for i in range(ends)])  5.26 us
  transfers between devices with their start and end apart: 13, of which 4 were waited for; matrix products, arithmetic and copies ran while one was open for 11% of the time, Pallas kernels for 11%

profile of v8, /device:TPU:10, one launch (start us, length us, event | category | flops | bytes accessed | tf_op | source)
XLA Modules:
  0.0 147.7 jit_solution(3604516698046962073)
XLA Ops:
  11.5 2.7 %collective-permute-start.1 = (f32[167936]{0:T(1024)}, f32[167936]{0:T(1024)S(1)}, u32[]{:S(2)}, u32[]{:S(2)}) collective-permute-start(f32[167936]{0:T(1024)} %pad_maximum_fusion.3), channel_id=1, source_target_pairs={{1,0},{2,1},{3,2},{4,3},{5,4},{6,5},{7,6},{8,7},{9,8},{10,9},{11,1... | collective-permute-start | bytes 2015240 | tf_op jit(solution)/shard_map/ppermute | solution.py:43
  15.4 1.9 %collective-permute-start = (f32[167936]{0:T(1024)}, f32[167936]{0:T(1024)}, u32[]{:S(2)}, u32[]{:S(2)}) collective-permute-start(f32[167936]{0:T(1024)} %pad_maximum_fusion.2), channel_id=1, source_target_pairs={{0,1},{1,2},{2,3},{3,4},{4,5},{5,6},{6,7},{7,8},{8,9},{9,10},{10,1... | collective-permute-start | bytes 2015240 | tf_op jit(solution)/shard_map/ppermute | solution.py:42
  19.2 3.7 %collective-permute-done.1 = f32[167936]{0:T(1024)S(1)} collective-permute-done((f32[167936]{0:T(1024)}, f32[167936]{0:T(1024)S(1)}, u32[]{:S(2)}, u32[]{:S(2)}) %collective-permute-start.1) | collective-permute-done | bytes 671776 | tf_op jit(solution)/shard_map/ppermute | solution.py:43
  23.0 5.8 %collective-permute-done = f32[167936]{0:T(1024)} collective-permute-done((f32[167936]{0:T(1024)}, f32[167936]{0:T(1024)}, u32[]{:S(2)}, u32[]{:S(2)}) %collective-permute-start) | collective-permute-done | bytes 671776 | tf_op jit(solution)/shard_map/ppermute | solution.py:42
  33.6 5.0 %shard_map.77 = (f32[16,14,512]{2,1,0:T(8,128)}, f32[16,14,512]{2,1,0:T(8,128)}, f32[16,14,512]{2,1,0:T(8,128)}, f32[16,14,512]{2,1,0:T(8,128)}, f32[15,14,512]{...) custom-call(f32[16,16,512]{2,1,0:T(8,128)} %pad_maximum_fusion.4.eta_ref, ...), custom_call_target="tpu_custom_call" | custom-call | tf_op jit(solution)/shard_map/pallas_call | solution.py:288
  41.8 9.4 %shard_map.78 = (f32[2,16,14,512]{3,2,1,0:T(8,128)}, f32[2,16,12,512]{3,2,1,0:T(8,128)}, f32[2,16,8,512]{3,2,1,0:T(8,128)}) custom-call(f32[2,16,16,512]{3,2,1,0:T(8,128)} %get-tuple-element.77.w_ref, f32[2,16,16,512]{3,2,1,0:T(8,128)} %get-tuple-element.78.b_ref, f32[16,14,512]{2,1,0:T(8,128)} %get-tuple-element.32.fxl_ref, ...), custom_call_target="tpu_custom_call" | custom-call | tf_op jit(solution)/shard_map/pallas_call | solution.py:214
  53.3 1.9 %collective-permute-start.3 = (f32[2,16,4,256]{3,2,1,0:T(4,128)S(1)}, f32[2,16,4,256]{3,2,1,0:T(4,128)S(1)}, u32[]{:S(2)}, u32[]{:S(2)}) collective-permute-start(f32[2,16,4,256]{3,2,1,0:T(4,128)S(1)} %broadcast_multiply_fusion.1), channel_id=1, source_target_pairs={{1,0},{2,1},{3,2},{4,3},{5,4},{6,5},{7,6},{8,7},{9,8},{10,9},{11,1... | collective-permute-start | bytes 393224 | tf_op jit(solution)/shard_map/ppermute | solution.py:29
  55.2 5.3 %collective-permute-start.2 = (f32[2,16,4,256]{3,2,1,0:T(4,128)S(1)}, f32[2,16,4,256]{3,2,1,0:T(4,128)S(1)}, u32[]{:S(2)}, u32[]{:S(2)}) collective-permute-start(f32[2,16,4,256]{3,2,1,0:T(4,128)S(1)} %broadcast_multiply_fusion.1), channel_id=1, source_target_pairs={{0,1},{1,2},{2,3},{3,4},{4,5},{5,6},{6,7},{7,8},{8,9},{9,10},{10,1... | collective-permute-start | bytes 393224 | tf_op jit(solution)/shard_map/ppermute | solution.py:27
  60.5 4.8 %collective-permute-done.2 = f32[2,16,4,256]{3,2,1,0:T(4,128)S(1)} collective-permute-done((f32[2,16,4,256]{3,2,1,0:T(4,128)S(1)}, f32[2,16,4,256]{3,2,1,0:T(4,128)S(1)}, u32[]{:S(2)}, u32[]{:S(2)}) %collective-permute-start.2) | collective-permute-done | bytes 131104 | tf_op jit(solution)/shard_map/ppermute | solution.py:27
  72.1 3.3 %shard_map.79 = (f32[16,12,256]{2,1,0:T(8,128)}, f32[16,12,256]{2,1,0:T(8,128)}, f32[16,12,256]{2,1,0:T(8,128)}, f32[16,12,256]{2,1,0:T(8,128)}, f32[15,12,256]{...) custom-call(f32[16,14,256]{2,1,0:T(8,128)} %pad_dynamic-slice_fusion.eta_ref, ...), custom_call_target="tpu_custom_call" | custom-call | tf_op jit(solution)/shard_map/pallas_call | solution.py:288
  76.8 4.4 %shard_map.80 = (f32[2,16,12,256]{3,2,1,0:T(8,128)}, f32[2,16,10,256]{3,2,1,0:T(8,128)}, f32[2,16,4,256]{3,2,1,0:T(4,128)}) custom-call(f32[2,16,12,256]{3,2,1,0:T(8,128)} %pad_maximum_fusion.5.w_ref.b_ref, f32[2,16,12,256]{3,2,1,0:T(8,128)} %pad_maximum_fusion.5.w_ref.b_ref, f32[16,12,256]{2,1,0:T(8,128)} %get-tuple-element.42.fxl_ref, ...), custom_call_target="tpu_custom_call" | custom-call | tf_op jit(solution)/shard_map/pallas_call | solution.py:214
  82.4 3.5 %collective-permute-start.4 = (f32[2,16,2,128]{3,2,1,0:T(2,128)S(1)}, f32[2,16,2,128]{3,2,1,0:T(2,128)S(1)}, u32[]{:S(2)}, u32[]{:S(2)}) collective-permute-start(f32[2,16,2,128]{3,2,1,0:T(2,128)S(1)} %copy_multiply_fusion), channel_id=1, source_target_pairs={{0,4},{1,5},{2,6},{3,7},{4,8},{5,9},{6,10},{7,11},{8,12},{9,13},{1... | collective-permute-start | bytes 98312 | tf_op jit(solution)/shard_map/ppermute | solution.py:404
  85.9 1.9 %collective-permute-start.5 = (f32[2,16,2,128]{3,2,1,0:T(2,128)S(1)}, f32[2,16,2,128]{3,2,1,0:T(2,128)S(1)}, u32[]{:S(2)}, u32[]{:S(2)}) collective-permute-start(f32[2,16,2,128]{3,2,1,0:T(2,128)S(1)} %copy_multiply_fusion), channel_id=1, source_target_pairs={{0,3},{1,4},{2,5},{3,6},{4,7},{5,8},{6,9},{7,10},{8,11},{9,12},{10... | collective-permute-start | bytes 98312 | tf_op jit(solution)/shard_map/ppermute | solution.py:404
  87.8 3.7 %collective-permute-start.6 = (f32[2,16,2,128]{3,2,1,0:T(2,128)S(1)}, f32[2,16,2,128]{3,2,1,0:T(2,128)S(1)}, u32[]{:S(2)}, u32[]{:S(2)}) collective-permute-start(f32[2,16,2,128]{3,2,1,0:T(2,128)S(1)} %copy_multiply_fusion), channel_id=1, source_target_pairs={{0,2},{1,3},{2,4},{3,5},{4,6},{5,7},{6,8},{7,9},{8,10},{9,11},{10,... | collective-permute-start | bytes 98312 | tf_op jit(solution)/shard_map/ppermute | solution.py:404
  91.5 2.0 %collective-permute-start.7 = (f32[2,16,2,128]{3,2,1,0:T(2,128)S(1)}, f32[2,16,2,128]{3,2,1,0:T(2,128)S(1)}, u32[]{:S(2)}, u32[]{:S(2)}) collective-permute-start(f32[2,16,2,128]{3,2,1,0:T(2,128)S(1)} %copy_multiply_fusion), channel_id=1, source_target_pairs={{0,1},{1,2},{2,3},{3,4},{4,5},{5,6},{6,7},{7,8},{8,9},{9,10},{10,1... | collective-permute-start | bytes 98312 | tf_op jit(solution)/shard_map/ppermute | solution.py:404
  93.5 4.5 %collective-permute-start.8 = (f32[2,16,2,128]{3,2,1,0:T(2,128)S(1)}, f32[2,16,2,128]{3,2,1,0:T(2,128)S(1)}, u32[]{:S(2)}, u32[]{:S(2)}) collective-permute-start(f32[2,16,2,128]{3,2,1,0:T(2,128)S(1)} %copy_multiply_fusion), channel_id=1, source_target_pairs={{1,0},{2,1},{3,2},{4,3},{5,4},{6,5},{7,6},{8,7},{9,8},{10,9},{11,1... | collective-permute-start | bytes 98312 | tf_op jit(solution)/shard_map/ppermute | solution.py:405
  100.5 2.2 %collective-permute-start.9 = (f32[2,16,2,128]{3,2,1,0:T(2,128)S(1)}, f32[2,16,2,128]{3,2,1,0:T(2,128)S(1)}, u32[]{:S(2)}, u32[]{:S(2)}) collective-permute-start(f32[2,16,2,128]{3,2,1,0:T(2,128)S(1)} %copy_multiply_fusion), channel_id=1, source_target_pairs={{2,0},{3,1},{4,2},{5,3},{6,4},{7,5},{8,6},{9,7},{10,8},{11,9},{12,... | collective-permute-start | bytes 98312 | tf_op jit(solution)/shard_map/ppermute | solution.py:405
  102.7 1.9 %collective-permute-start.10 = (f32[2,16,2,128]{3,2,1,0:T(2,128)S(1)}, f32[2,16,2,128]{3,2,1,0:T(2,128)S(1)}, u32[]{:S(2)}, u32[]{:S(2)}) collective-permute-start(f32[2,16,2,128]{3,2,1,0:T(2,128)S(1)} %copy_multiply_fusion), channel_id=1, source_target_pairs={{3,0},{4,1},{5,2},{6,3},{7,4},{8,5},{9,6},{10,7},{11,8},{12,9},{13... | collective-permute-start | bytes 98312 | tf_op jit(solution)/shard_map/ppermute | solution.py:405
  104.6 2.1 %collective-permute-start.11 = (f32[2,16,2,128]{3,2,1,0:T(2,128)S(1)}, f32[2,16,2,128]{3,2,1,0:T(2,128)S(1)}, u32[]{:S(2)}, u32[]{:S(2)}) collective-permute-start(f32[2,16,2,128]{3,2,1,0:T(2,128)S(1)} %copy_multiply_fusion), channel_id=1, source_target_pairs={{4,0},{5,1},{6,2},{7,3},{8,4},{9,5},{10,6},{11,7},{12,8},{13,9},{1... | collective-permute-start | bytes 98312 | tf_op jit(solution)/shard_map/ppermute | solution.py:405
  107.4 2.5 %shard_map.81 = (f32[16,18,128]{2,1,0:T(8,128)}, f32[16,18,128]{2,1,0:T(8,128)}, f32[16,18,128]{2,1,0:T(8,128)}, f32[16,18,128]{2,1,0:T(8,128)}, f32[15,18,128]{...) custom-call(f32[16,20,128]{2,1,0:T(8,128)} %pad_dynamic-slice_fusion.1.eta_ref, ...), custom_call_target="tpu_custom_call" | custom-call | tf_op jit(solution)/shard_map/pallas_call | solution.py:288
  110.5 2.2 %concatenate.35.b_ref = f32[2,16,18,128]{3,2,1,0:T(8,128)} concatenate(f32[2,16,2,128]{3,2,1,0:T(2,128)S(1)} %collective-permute-done.4, f32[2,16,2,128]{3,2,1,0:T(2,128)S(1)} %collective-permute-done.5, f32[2,16,2,128]{3,2,1,0:T(2,128)S(1)} %collective-permute-done.6, f32[2,16,2,128]{3,2,1,0:T(2,128)S(1)} %collective-permute-done.7, f32[2,16,2,128]{3,2,1,0:T(2,128)S(1)} %copy_multiply_fusion, ...), dimensions={2} | concatenate | bytes 589824 | tf_op jit(solution)/shard_map/concatenate | solution.py:406
  113.4 5.6 %shard_map.82 = f32[2,16,18,128]{3,2,1,0:T(8,128)} custom-call(f32[2,16,18,128]{3,2,1,0:T(8,128)} %concatenate.35.b_ref, f32[16,18,128]{2,1,0:T(8,128)} %get-tuple-element.52.fxl_ref, f32[16,18,128]{2,1,0:T(8,128)} %get-tuple-element.53.fxr_ref, f32[16,18,128]{2,1,0:T(8,128)} %get-tuple-element.54.fyl_ref, f32[16,18,128]{2,1,0:T(8,128)} %get-tuple-element.55.fyr_ref, ...), custom_call_target="tpu_custom_call" | custom-call | tf_op jit(solution)/shard_map/pallas_call | solution.py:307
  123.2 4.1 %shard_map.83 = (f32[2,16,8,256]{3,2,1,0:T(8,128)}, f32[2,16,6,256]{3,2,1,0:T(8,128)}) custom-call(f32[2,16,10,256]{3,2,1,0:T(8,128)} %slice_add_fusion.w_ref, f32[2,16,12,256]{3,2,1,0:T(8,128)} %pad_maximum_fusion.5.w_ref.b_ref, f32[16,12,256]{2,1,0:T(8,128)} %get-tuple-element.42.fxl_ref, f32[16,12,256]{2,1,0:T(8,128)} %get-tuple-element.43.fxr_ref, ...), custom_call_target="tpu_custom_call" | custom-call | tf_op jit(solution)/shard_map/pallas_call | solution.py:214
  131.7 7.8 %shard_map.84 = (f32[2,16,10,512]{3,2,1,0:T(8,128)}, f32[2,16,8,512]{3,2,1,0:T(8,128)}) custom-call(f32[2,16,12,512]{3,2,1,0:T(8,128)} %copy_add_fusion.w_ref, f32[2,16,16,512]{3,2,1,0:T(8,128)} %get-tuple-element.78.b_ref, f32[16,14,512]{2,1,0:T(8,128)} %get-tuple-element.32.fxl_ref, f32[16,14,512]{2,1,0:T(8,128)} %get-tuple-element.33.fxr_ref, ...), custom_call_target="tpu_custom_call" | custom-call | tf_op jit(solution)/shard_map/pallas_call | solution.py:214
  (130 shorter events, 40.8 us)
Async XLA Ops:
  7.2 2.5 %copy-start.2 = (f32[2,16,8,512]{3,2,1,0:T(8,128)S(1)}, f32[2,16,8,512]{3,2,1,0:T(8,128)}, u32[]{:S(2)}) copy-start(f32[2,16,8,512]{3,2,1,0:T(8,128)} %param.7) | copy-start | bytes 1572868
  7.2 58.9 %all-gather.3.cloned.1.call-start = ((), (), s32[]{:S(2)}) async-start(), calls=%async_computation | async-start | bytes 1253376 | tf_op jit(solution)/shard_map/all_gather | solution.py:419
  8.1 10.9 %copy-start.6 = (f32[16,8,512]{2,1,0:T(8,128)}, f32[16,8,512]{2,1,0:T(8,128)S(1)}, u32[]{:S(2)}) copy-start(f32[16,8,512]{2,1,0:T(8,128)S(1)} %multiply_add_fusion) | copy-start | bytes 786436
  9.5 1.0 copy-start.3
  11.5 11.4 %collective-permute-start.1 = (f32[167936]{0:T(1024)}, f32[167936]{0:T(1024)S(1)}, u32[]{:S(2)}, u32[]{:S(2)}) collective-permute-start(f32[167936]{0:T(1024)} %pad_maximum_fusion.3), channel_id=1, source_target_pairs={{1,0},{2,1},{3,2},{4,3},{5,4},{6,5},{7,6},{8,7},{9,8},{10,9},{11,1... | collective-permute-start | bytes 2015240 | tf_op jit(solution)/shard_map/ppermute | solution.py:43
  15.4 13.4 %collective-permute-start = (f32[167936]{0:T(1024)}, f32[167936]{0:T(1024)}, u32[]{:S(2)}, u32[]{:S(2)}) collective-permute-start(f32[167936]{0:T(1024)} %pad_maximum_fusion.2), channel_id=1, source_target_pairs={{0,1},{1,2},{2,3},{3,4},{4,5},{5,6},{6,7},{7,8},{8,9},{9,10},{10,1... | collective-permute-start | bytes 2015240 | tf_op jit(solution)/shard_map/ppermute | solution.py:42
  29.9 2.1 %slice-start.1 = ((f32[16,8,512]{2,1,0:T(8,128)}), f32[2,8,512]{2,1,0:T(8,128)S(1)}, s32[]{:S(2)}) async-start(f32[16,8,512]{2,1,0:T(8,128)} %copy-done.6), calls=%async_computation.2 | async-start | bytes 65536 | tf_op jit(solution)/shard_map/slice | solution.py:413
  30.2 8.4 %copy-start.1 = (f32[2,16,8,512]{3,2,1,0:T(8,128)S(1)}, f32[2,16,8,512]{3,2,1,0:T(8,128)}, u32[]{:S(2)}) copy-start(f32[2,16,8,512]{3,2,1,0:T(8,128)} %param.6) | copy-start | bytes 1572868
  53.3 7.2 %collective-permute-start.3 = (f32[2,16,4,256]{3,2,1,0:T(4,128)S(1)}, f32[2,16,4,256]{3,2,1,0:T(4,128)S(1)}, u32[]{:S(2)}, u32[]{:S(2)}) collective-permute-start(f32[2,16,4,256]{3,2,1,0:T(4,128)S(1)} %broadcast_multiply_fusion.1), channel_id=1, source_target_pairs={{1,0},{2,1},{3,2},{4,3},{5,4},{6,5},{7,6},{8,7},{9,8},{10,9},{11,1... | collective-permute-start | bytes 393224 | tf_op jit(solution)/shard_map/ppermute | solution.py:29
  55.2 10.1 %collective-permute-start.2 = (f32[2,16,4,256]{3,2,1,0:T(4,128)S(1)}, f32[2,16,4,256]{3,2,1,0:T(4,128)S(1)}, u32[]{:S(2)}, u32[]{:S(2)}) collective-permute-start(f32[2,16,4,256]{3,2,1,0:T(4,128)S(1)} %broadcast_multiply_fusion.1), channel_id=1, source_target_pairs={{0,1},{1,2},{2,3},{3,4},{4,5},{5,6},{6,7},{7,8},{8,9},{9,10},{10,1... | collective-permute-start | bytes 393224 | tf_op jit(solution)/shard_map/ppermute | solution.py:27
  67.6 1.1 copy-start
  69.7 0.9 slice-start
  82.4 18.1 %collective-permute-start.4 = (f32[2,16,2,128]{3,2,1,0:T(2,128)S(1)}, f32[2,16,2,128]{3,2,1,0:T(2,128)S(1)}, u32[]{:S(2)}, u32[]{:S(2)}) collective-permute-start(f32[2,16,2,128]{3,2,1,0:T(2,128)S(1)} %copy_multiply_fusion), channel_id=1, source_target_pairs={{0,4},{1,5},{2,6},{3,7},{4,8},{5,9},{6,10},{7,11},{8,12},{9,13},{1... | collective-permute-start | bytes 98312 | tf_op jit(solution)/shard_map/ppermute | solution.py:404
  85.9 16.8 %collective-permute-start.5 = (f32[2,16,2,128]{3,2,1,0:T(2,128)S(1)}, f32[2,16,2,128]{3,2,1,0:T(2,128)S(1)}, u32[]{:S(2)}, u32[]{:S(2)}) collective-permute-start(f32[2,16,2,128]{3,2,1,0:T(2,128)S(1)} %copy_multiply_fusion), channel_id=1, source_target_pairs={{0,3},{1,4},{2,5},{3,6},{4,7},{5,8},{6,9},{7,10},{8,11},{9,12},{10... | collective-permute-start | bytes 98312 | tf_op jit(solution)/shard_map/ppermute | solution.py:404
  87.8 16.8 %collective-permute-start.6 = (f32[2,16,2,128]{3,2,1,0:T(2,128)S(1)}, f32[2,16,2,128]{3,2,1,0:T(2,128)S(1)}, u32[]{:S(2)}, u32[]{:S(2)}) collective-permute-start(f32[2,16,2,128]{3,2,1,0:T(2,128)S(1)} %copy_multiply_fusion), channel_id=1, source_target_pairs={{0,2},{1,3},{2,4},{3,5},{4,6},{5,7},{6,8},{7,9},{8,10},{9,11},{10,... | collective-permute-start | bytes 98312 | tf_op jit(solution)/shard_map/ppermute | solution.py:404
  91.5 18.4 %collective-permute-start.7 = (f32[2,16,2,128]{3,2,1,0:T(2,128)S(1)}, f32[2,16,2,128]{3,2,1,0:T(2,128)S(1)}, u32[]{:S(2)}, u32[]{:S(2)}) collective-permute-start(f32[2,16,2,128]{3,2,1,0:T(2,128)S(1)} %copy_multiply_fusion), channel_id=1, source_target_pairs={{0,1},{1,2},{2,3},{3,4},{4,5},{5,6},{6,7},{7,8},{8,9},{9,10},{10,1... | collective-permute-start | bytes 98312 | tf_op jit(solution)/shard_map/ppermute | solution.py:404
  93.5 16.4 %collective-permute-start.8 = (f32[2,16,2,128]{3,2,1,0:T(2,128)S(1)}, f32[2,16,2,128]{3,2,1,0:T(2,128)S(1)}, u32[]{:S(2)}, u32[]{:S(2)}) collective-permute-start(f32[2,16,2,128]{3,2,1,0:T(2,128)S(1)} %copy_multiply_fusion), channel_id=1, source_target_pairs={{1,0},{2,1},{3,2},{4,3},{5,4},{6,5},{7,6},{8,7},{9,8},{10,9},{11,1... | collective-permute-start | bytes 98312 | tf_op jit(solution)/shard_map/ppermute | solution.py:405
  100.5 9.4 %collective-permute-start.9 = (f32[2,16,2,128]{3,2,1,0:T(2,128)S(1)}, f32[2,16,2,128]{3,2,1,0:T(2,128)S(1)}, u32[]{:S(2)}, u32[]{:S(2)}) collective-permute-start(f32[2,16,2,128]{3,2,1,0:T(2,128)S(1)} %copy_multiply_fusion), channel_id=1, source_target_pairs={{2,0},{3,1},{4,2},{5,3},{6,4},{7,5},{8,6},{9,7},{10,8},{11,9},{12,... | collective-permute-start | bytes 98312 | tf_op jit(solution)/shard_map/ppermute | solution.py:405
  102.7 7.2 %collective-permute-start.10 = (f32[2,16,2,128]{3,2,1,0:T(2,128)S(1)}, f32[2,16,2,128]{3,2,1,0:T(2,128)S(1)}, u32[]{:S(2)}, u32[]{:S(2)}) collective-permute-start(f32[2,16,2,128]{3,2,1,0:T(2,128)S(1)} %copy_multiply_fusion), channel_id=1, source_target_pairs={{3,0},{4,1},{5,2},{6,3},{7,4},{8,5},{9,6},{10,7},{11,8},{12,9},{13... | collective-permute-start | bytes 98312 | tf_op jit(solution)/shard_map/ppermute | solution.py:405
  104.6 5.8 %collective-permute-start.11 = (f32[2,16,2,128]{3,2,1,0:T(2,128)S(1)}, f32[2,16,2,128]{3,2,1,0:T(2,128)S(1)}, u32[]{:S(2)}, u32[]{:S(2)}) collective-permute-start(f32[2,16,2,128]{3,2,1,0:T(2,128)S(1)} %copy_multiply_fusion), channel_id=1, source_target_pairs={{4,0},{5,1},{6,2},{7,3},{8,4},{9,5},{10,6},{11,7},{12,8},{13,9},{1... | collective-permute-start | bytes 98312 | tf_op jit(solution)/shard_map/ppermute | solution.py:405
  119.0 1.9 %copy-start.5 = (f32[2,16,10,256]{3,2,1,0:T(8,128)S(1)}, f32[2,16,10,256]{3,2,1,0:T(8,128)}, u32[]{:S(2)}) copy-start(f32[2,16,10,256]{3,2,1,0:T(8,128)} %get-tuple-element.50) | copy-start | bytes 983044
  127.3 1.5 %copy-start.4 = (f32[2,16,12,512]{3,2,1,0:T(8,128)S(1)}, f32[2,16,12,512]{3,2,1,0:T(8,128)}, u32[]{:S(2)}) copy-start(f32[2,16,12,512]{3,2,1,0:T(8,128)} %get-tuple-element.40) | copy-start | bytes 2359300
  131.7 7.8 %copy-start.7 = (f32[2,8,512]{2,1,0:T(8,128)S(1)}, f32[2,8,512]{2,1,0:T(8,128)}, u32[]{:S(2)}) copy-start(f32[2,8,512]{2,1,0:T(8,128)} %param.11) | copy-start | bytes 98308
Sparse Core Ops, SparseCore 0:
  19.1 38.8 all-gather.2

commit v9 on v8

--- a/solution.py
+++ b/solution.py
@@ -102,11 +102,14 @@
 
 
 def sweep_kernel(w_ref, b_ref, fxl_ref, fxr_ref, fyl_ref, fyr_ref, fz_ref, re_ref, inv_ref, rat_ref, mask_ref, *more,
-                 rows, cut_w, cut_b, cut_op, mode, scale, then):
+                 rows, cut_w, cut_b, cut_op, mode, scale, then, lifted):
     lanes = (fxl_ref, fxr_ref, fyl_ref, fyr_ref, fz_ref, re_ref, inv_ref, rat_ref, scale)
+    add_ref = more[0] if lifted else None
+    more = more[1:] if lifted else more
     steps = len(then)
     masks, outs = more[:steps], more[steps:]
-    relax(w_ref, b_ref, lanes, mask_ref, outs[0], rows=rows, cut_w=cut_w, cut_b=cut_b, cut_op=cut_op, mode=mode)
+    relax(w_ref, b_ref, lanes, mask_ref, outs[0], rows=rows, cut_w=cut_w, cut_b=cut_b, cut_op=cut_op, mode=mode,
+          add_ref=add_ref)
     for step, (next_cut_w, next_rows, next_cut_b, next_cut_op, next_mode) in enumerate(then):
         relax(outs[step], b_ref, lanes, masks[step], outs[step + 1], rows=next_rows, cut_w=next_cut_w,
               cut_b=next_cut_b, cut_op=next_cut_op, mode=next_mode)
@@ -123,7 +126,7 @@
                 w_ref[0, k, pl.ds(8, rows), :] = out_ref[0, k]
 
 
-def relax(w_ref, b_ref, lanes, mask_ref, out_ref, *, rows, cut_w, cut_b, cut_op, mode):
+def relax(w_ref, b_ref, lanes, mask_ref, out_ref, *, rows, cut_w, cut_b, cut_op, mode, add_ref=None):
     fxl_ref, fxr_ref, fyl_ref, fyr_ref, fz_ref, re_ref, inv_ref, rat_ref, scale = lanes
     layers = out_ref.shape[1]
     cols = out_ref.shape[3]
@@ -143,13 +146,17 @@
     def face(ref, weight, k):
         return weight * ref[k, pl.ds(cut_op, rows), :]
 
+    def rim(k, start):
+        value = w_ref[0, k, pl.ds(start, rows), :]
+        return value if add_ref is None else value + add_ref[0, k, pl.ds(start, rows), :]
+
     def field(k):
-        return w_ref[0, k, pl.ds(cut_w + 1, rows), :]
+        return rim(k, cut_w + 1)
 
     def applied(k):
         w = field(k)
-        west = w_ref[0, k, pl.ds(cut_w, rows), :]
-        east = w_ref[0, k, pl.ds(cut_w + 2, rows), :]
+        west = rim(k, cut_w)
+        east = rim(k, cut_w + 2)
         result = -(face(fxr_ref, weight_x, k) * (east - w) - face(fxl_ref, weight_x, k) * (w - west))
         ahead = pltpu.roll(w, 1, 1)
         behind = pltpu.roll(w, cols - 1, 1)
@@ -191,7 +198,7 @@
 
 
 def kernel_sweep(field_rim, target, lanes, cut_b, cut_op, mask, mode="sweep", cut_w=0, rows=None, then=(),
-                 masks=()):
+                 masks=(), lift=None):
     parts, layers, rows_rim, cols = field_rim.shape
     rows = rows_rim - 2 if rows is None else rows
     fxl, fxr, fyl, fyr, fz, re, inv, rat, scale = lanes
@@ -200,11 +207,15 @@
     operands = [field_rim, target, fxl, fxr, fyl, fyr, fz, re, inv, rat, mask]
     specs = [per_part(field_rim), per_part(target), whole(fxl), whole(fxr), whole(fyl), whole(fyr),
              whole(fz), whole(re), per_part(inv), per_part(rat), whole(mask)]
+    if lift is not None:
+        operands.append(lift)
+        specs.append(per_part(lift))
     masks = list(masks) + [mask] * (len(then) - len(masks))
     operands += masks
     specs += [whole(m) for m in masks]
     body = functools.partial(
-        sweep_kernel, rows=rows, cut_w=cut_w, cut_b=cut_b, cut_op=cut_op, mode=mode, scale=scale, then=then
+        sweep_kernel, rows=rows, cut_w=cut_w, cut_b=cut_b, cut_op=cut_op, mode=mode, scale=scale, then=then,
+        lifted=lift is not None,
     )
     out_specs = [pl.BlockSpec((1, layers, rows, cols), lambda c: (c, 0, 0, 0))]
     out_shape = [jax.ShapeDtypeStruct((parts, layers, rows, cols), jnp.float32)]
@@ -473,9 +484,8 @@
         middle, rhs_wide, op_1, 2, 2, rows_inside(half, half - 2, 3 * half - 4, wide),
         then=((0, 3 * half - 6, 3, 3, "sweep"),), masks=(rows_inside(half, half - 3, 3 * half - 6, wide),),
     )[1]
-    fine = fine + prolong(middle)
     fine = kernel_sweep(
-        fine, misfit_wide, op_0, 3, 2, rows_inside(cells, 1, cells + 2, cols),
+        fine, misfit_wide, op_0, 3, 2, rows_inside(cells, 1, cells + 2, cols), lift=prolong(middle),
         then=((0, cells, 4, 3, "sweep"),), masks=(rows_inside(cells, 0, cells, cols),),
     )[1]
     grounded = (ice_mask == 2).astype(jnp.float32)

time: 150 us -> 150 us (level); the launches traced: 148 us -> 149 us
  starting transfers between devices: 33.6 us -> 41.5 us
  waiting for transfers between devices: 14.8 us -> 9.02 us
  other arithmetic: 12 us -> 10 us
    ppermute x1, waiting for transfers between devices: 4.75 us -> 0.01 us  [with_halo(): lax.ppermute(tail, axis, [(i, (i + 1) % count) for i in range(ends)])]
    ppermute x1, starting transfers between devices: 5.26 us -> 8.26 us  [with_halo(): lax.ppermute(tail, axis, [(i, (i + 1) % count) for i in range(ends)])]
    slice x5, local copies, waits for them, and re-layouts: 2.83 us -> 0.11 us  [trade(): left = from_left[offset:offset + size].reshape(h.shape)]
    ppermute x1, waiting for transfers between devices: 0.01 us -> 2.28 us  [with_halo(): lax.ppermute(head, axis, [((i + 1) % count, i) for i in range(ends)])]
    ppermute x4, starting transfers between devices: 10.7 us -> 13 us  [nearby(): lax.ppermute(cells, 'gx', [(i + step, i) for i in range(count - step)])]
    ppermute x1, waiting for transfers between devices: 3.69 us -> 1.73 us  [trade(): lax.ppermute(pack(heads), 'gx', [(i + 1, i) for i in range(ends)])]
    ppermute x1, starting transfers between devices: 2.74 us -> 4.54 us  [trade(): lax.ppermute(pack(heads), 'gx', [(i + 1, i) for i in range(ends)])]
    add x1 -> x0, other arithmetic: 1.55 us -> none  [shards(): fine = fine + prolong(middle)]
  transfers between devices with their start and end apart: 13 -> 13, of which waited for: 4 -> 4; matrix products, arithmetic and copies ran while one was open for 11% -> 10% of each run, Pallas kernels for 11% -> 11%
where the time goes in v9:
time: 150 us; the launch traced here: 149 us
  Pallas kernels  42.8 us (29%)
  starting transfers between devices  41.5 us (28%)
  local copies, waits for them, and re-layouts  23.5 us (16%)
  between operations  14.8 us (10%)
  other arithmetic  10 us (7%)
  waiting for transfers between devices  9.02 us (6%)
  matrix products  7.7 us (5%)
    pallas_call x4, Pallas kernels, kernel_sweep(): pl.pallas_call(body, grid=(parts,), in_specs=specs, out_specs=out_specs,...  26.4 us
    ppermute x4, starting transfers between devices, nearby(): lax.ppermute(cells, 'gx', [(i + step, i) for i in range(count - step)])  13 us
    ppermute x4, starting transfers between devices, nearby(): lax.ppermute(cells, 'gx', [(i, i + step) for i in range(count - step)])  11.7 us
    pallas_call x3, Pallas kernels, kernel_operator(): pl.pallas_call(body, grid=(2,), in_specs=[whole(eta_level), whole(react_l...  10.8 us
    ppermute x1, starting transfers between devices, with_halo(): lax.ppermute(tail, axis, [(i, (i + 1) % count) for i in range(ends)])  8.26 us
    broadcast_in_dim x9, local copies, waits for them, and re-layouts, rows_inside(): jnp.broadcast_to(inside(cells, halo, extent)[0, 0], (extent, cols))  6.05 us
    pallas_call x1, Pallas kernels, kernel_coarse(): pl.pallas_call(body, grid=(parts,), in_specs=specs, out_specs=pl.BlockSpe...  5.63 us
    dot_general x6, matrix products, block_mean(): jnp.einsum('...y,yz->...z', field, pairs, precision=lax.Precision.HIGHEST)  5.1 us
  transfers between devices with their start and end apart: 13, of which 4 were waited for; matrix products, arithmetic and copies ran while one was open for 10% of the time, Pallas kernels for 11%

profile of v9, /device:TPU:10, one launch (start us, length us, event | category | flops | bytes accessed | tf_op | source)
XLA Modules:
  0.0 149.4 jit_solution(16653582303842943044)
XLA Ops:
  12.1 1.9 %collective-permute-start = (f32[167936]{0:T(1024)}, f32[167936]{0:T(1024)S(1)}, u32[]{:S(2)}, u32[]{:S(2)}) collective-permute-start(f32[167936]{0:T(1024)} %pad_maximum_fusion.2), channel_id=1, source_target_pairs={{0,1},{1,2},{2,3},{3,4},{4,5},{5,6},{6,7},{7,8},{8,9},{9,10},{10,1... | collective-permute-start | bytes 2015240 | tf_op jit(solution)/shard_map/ppermute | solution.py:42
  14.2 4.5 %collective-permute-start.1 = (f32[167936]{0:T(1024)S(1)}, f32[167936]{0:T(1024)S(1)}, u32[]{:S(2)}, u32[]{:S(2)}) collective-permute-start(f32[167936]{0:T(1024)S(1)} %pad_maximum_fusion.3), channel_id=1, source_target_pairs={{1,0},{2,1},{3,2},{4,3},{5,4},{6,5},{7,6},{8,7},{9,8},{10,9},{11,1... | collective-permute-start | bytes 2015240 | tf_op jit(solution)/shard_map/ppermute | solution.py:43
  20.9 4.4 %collective-permute-done = f32[167936]{0:T(1024)S(1)} collective-permute-done((f32[167936]{0:T(1024)}, f32[167936]{0:T(1024)S(1)}, u32[]{:S(2)}, u32[]{:S(2)}) %collective-permute-start) | collective-permute-done | bytes 671776 | tf_op jit(solution)/shard_map/ppermute | solution.py:42
  31.1 5.0 %shard_map.77 = (f32[16,14,512]{2,1,0:T(8,128)}, f32[16,14,512]{2,1,0:T(8,128)}, f32[16,14,512]{2,1,0:T(8,128)}, f32[16,14,512]{2,1,0:T(8,128)}, f32[15,14,512]{...) custom-call(f32[16,16,512]{2,1,0:T(8,128)} %pad_maximum_fusion.4.eta_ref, ...), custom_call_target="tpu_custom_call" | custom-call | tf_op jit(solution)/shard_map/pallas_call | solution.py:299
  36.1 1.8 %pad_maximum_fusion = (f32[2,16,16,512]{3,2,1,0:T(8,128)}, f32[2,16,16,512]{3,2,1,0:T(8,128)}) fusion(f32[2,16,4,512]{3,2,1,0:T(4,128)S(1)} %reshape.350, f32[2,16,8,512]{3,2,1,0:T(8,128)S(1)} %copy-done.2, f32[2,16,4,512]{3,2,1,0:T(4,128)S(1)} %reshape.345, f32[2,16,4,512]{3,2,1,0:T(4,128)S(1)} %reshape.352, f32[2,16,8,512]{3,2,1,0:T(8,128)S(1)} %copy-done.1, ...), kind=kLoop, calls=%fused_computation.3 | loop fusion | flops 1048576 | bytes 4194304 | tf_op jit(solution)/shard_map/concatenate | solution.py:51
  39.2 9.6 %shard_map.78 = (f32[2,16,14,512]{3,2,1,0:T(8,128)}, f32[2,16,12,512]{3,2,1,0:T(8,128)}, f32[2,16,8,512]{3,2,1,0:T(8,128)}) custom-call(f32[2,16,16,512]{3,2,1,0:T(8,128)} %get-tuple-element.77.w_ref, f32[2,16,16,512]{3,2,1,0:T(8,128)} %get-tuple-element.78.b_ref, f32[16,14,512]{2,1,0:T(8,128)} %get-tuple-element.32.fxl_ref, ...), custom_call_target="tpu_custom_call" | custom-call | tf_op jit(solution)/shard_map/pallas_call | solution.py:225
  50.9 8.3 %collective-permute-start.2 = (f32[2,16,4,256]{3,2,1,0:T(4,128)S(1)}, f32[2,16,4,256]{3,2,1,0:T(4,128)S(1)}, u32[]{:S(2)}, u32[]{:S(2)}) collective-permute-start(f32[2,16,4,256]{3,2,1,0:T(4,128)S(1)} %broadcast_multiply_fusion.1), channel_id=1, source_target_pairs={{0,1},{1,2},{2,3},{3,4},{4,5},{5,6},{6,7},{7,8},{8,9},{9,10},{10,1... | collective-permute-start | bytes 393224 | tf_op jit(solution)/shard_map/ppermute | solution.py:27
  59.2 2.1 %collective-permute-start.3 = (f32[2,16,4,256]{3,2,1,0:T(4,128)S(1)}, f32[2,16,4,256]{3,2,1,0:T(4,128)S(1)}, u32[]{:S(2)}, u32[]{:S(2)}) collective-permute-start(f32[2,16,4,256]{3,2,1,0:T(4,128)S(1)} %broadcast_multiply_fusion.1), channel_id=1, source_target_pairs={{1,0},{2,1},{3,2},{4,3},{5,4},{6,5},{7,6},{8,7},{9,8},{10,9},{11,1... | collective-permute-start | bytes 393224 | tf_op jit(solution)/shard_map/ppermute | solution.py:29
  61.3 2.3 %collective-permute-done.3 = f32[2,16,4,256]{3,2,1,0:T(4,128)S(1)} collective-permute-done((f32[2,16,4,256]{3,2,1,0:T(4,128)S(1)}, f32[2,16,4,256]{3,2,1,0:T(4,128)S(1)}, u32[]{:S(2)}, u32[]{:S(2)}) %collective-permute-start.3) | collective-permute-done | bytes 131104 | tf_op jit(solution)/shard_map/ppermute | solution.py:29
  70.5 3.3 %shard_map.79 = (f32[16,12,256]{2,1,0:T(8,128)}, f32[16,12,256]{2,1,0:T(8,128)}, f32[16,12,256]{2,1,0:T(8,128)}, f32[16,12,256]{2,1,0:T(8,128)}, f32[15,12,256]{...) custom-call(f32[16,14,256]{2,1,0:T(8,128)} %pad_dynamic-slice_fusion.eta_ref, ...), custom_call_target="tpu_custom_call" | custom-call | tf_op jit(solution)/shard_map/pallas_call | solution.py:299
  75.1 4.4 %shard_map.80 = (f32[2,16,12,256]{3,2,1,0:T(8,128)}, f32[2,16,10,256]{3,2,1,0:T(8,128)}, f32[2,16,4,256]{3,2,1,0:T(4,128)}) custom-call(f32[2,16,12,256]{3,2,1,0:T(8,128)} %pad_maximum_fusion.5.w_ref.b_ref, f32[2,16,12,256]{3,2,1,0:T(8,128)} %pad_maximum_fusion.5.w_ref.b_ref, f32[16,12,256]{2,1,0:T(8,128)} %get-tuple-element.42.fxl_ref, ...), custom_call_target="tpu_custom_call" | custom-call | tf_op jit(solution)/shard_map/pallas_call | solution.py:225
  80.8 4.4 %collective-permute-start.10 = (f32[2,16,2,128]{3,2,1,0:T(2,128)S(1)}, f32[2,16,2,128]{3,2,1,0:T(2,128)S(1)}, u32[]{:S(2)}, u32[]{:S(2)}) collective-permute-start(f32[2,16,2,128]{3,2,1,0:T(2,128)S(1)} %copy_multiply_fusion), channel_id=1, source_target_pairs={{3,0},{4,1},{5,2},{6,3},{7,4},{8,5},{9,6},{10,7},{11,8},{12,9},{13... | collective-permute-start | bytes 98312 | tf_op jit(solution)/shard_map/ppermute | solution.py:416
  85.1 1.9 %collective-permute-start.11 = (f32[2,16,2,128]{3,2,1,0:T(2,128)S(1)}, f32[2,16,2,128]{3,2,1,0:T(2,128)S(1)}, u32[]{:S(2)}, u32[]{:S(2)}) collective-permute-start(f32[2,16,2,128]{3,2,1,0:T(2,128)S(1)} %copy_multiply_fusion), channel_id=1, source_target_pairs={{4,0},{5,1},{6,2},{7,3},{8,4},{9,5},{10,6},{11,7},{12,8},{13,9},{1... | collective-permute-start | bytes 98312 | tf_op jit(solution)/shard_map/ppermute | solution.py:416
  87.1 3.9 %collective-permute-start.4 = (f32[2,16,2,128]{3,2,1,0:T(2,128)S(1)}, f32[2,16,2,128]{3,2,1,0:T(2,128)S(1)}, u32[]{:S(2)}, u32[]{:S(2)}) collective-permute-start(f32[2,16,2,128]{3,2,1,0:T(2,128)S(1)} %copy_multiply_fusion), channel_id=1, source_target_pairs={{0,4},{1,5},{2,6},{3,7},{4,8},{5,9},{6,10},{7,11},{8,12},{9,13},{1... | collective-permute-start | bytes 98312 | tf_op jit(solution)/shard_map/ppermute | solution.py:415
  91.0 1.9 %collective-permute-start.5 = (f32[2,16,2,128]{3,2,1,0:T(2,128)S(1)}, f32[2,16,2,128]{3,2,1,0:T(2,128)S(1)}, u32[]{:S(2)}, u32[]{:S(2)}) collective-permute-start(f32[2,16,2,128]{3,2,1,0:T(2,128)S(1)} %copy_multiply_fusion), channel_id=1, source_target_pairs={{0,3},{1,4},{2,5},{3,6},{4,7},{5,8},{6,9},{7,10},{8,11},{9,12},{10... | collective-permute-start | bytes 98312 | tf_op jit(solution)/shard_map/ppermute | solution.py:415
  92.9 3.9 %collective-permute-start.6 = (f32[2,16,2,128]{3,2,1,0:T(2,128)S(1)}, f32[2,16,2,128]{3,2,1,0:T(2,128)S(1)}, u32[]{:S(2)}, u32[]{:S(2)}) collective-permute-start(f32[2,16,2,128]{3,2,1,0:T(2,128)S(1)} %copy_multiply_fusion), channel_id=1, source_target_pairs={{0,2},{1,3},{2,4},{3,5},{4,6},{5,7},{6,8},{7,9},{8,10},{9,11},{10,... | collective-permute-start | bytes 98312 | tf_op jit(solution)/shard_map/ppermute | solution.py:415
  99.4 1.9 %collective-permute-start.7 = (f32[2,16,2,128]{3,2,1,0:T(2,128)S(1)}, f32[2,16,2,128]{3,2,1,0:T(2,128)S(1)}, u32[]{:S(2)}, u32[]{:S(2)}) collective-permute-start(f32[2,16,2,128]{3,2,1,0:T(2,128)S(1)} %copy_multiply_fusion), channel_id=1, source_target_pairs={{0,1},{1,2},{2,3},{3,4},{4,5},{5,6},{6,7},{7,8},{8,9},{9,10},{10,1... | collective-permute-start | bytes 98312 | tf_op jit(solution)/shard_map/ppermute | solution.py:415
  101.3 4.5 %collective-permute-start.8 = (f32[2,16,2,128]{3,2,1,0:T(2,128)S(1)}, f32[2,16,2,128]{3,2,1,0:T(2,128)S(1)}, u32[]{:S(2)}, u32[]{:S(2)}) collective-permute-start(f32[2,16,2,128]{3,2,1,0:T(2,128)S(1)} %copy_multiply_fusion), channel_id=1, source_target_pairs={{1,0},{2,1},{3,2},{4,3},{5,4},{6,5},{7,6},{8,7},{9,8},{10,9},{11,1... | collective-permute-start | bytes 98312 | tf_op jit(solution)/shard_map/ppermute | solution.py:416
  105.9 2.1 %collective-permute-start.9 = (f32[2,16,2,128]{3,2,1,0:T(2,128)S(1)}, f32[2,16,2,128]{3,2,1,0:T(2,128)S(1)}, u32[]{:S(2)}, u32[]{:S(2)}) collective-permute-start(f32[2,16,2,128]{3,2,1,0:T(2,128)S(1)} %copy_multiply_fusion), channel_id=1, source_target_pairs={{2,0},{3,1},{4,2},{5,3},{6,4},{7,5},{8,6},{9,7},{10,8},{11,9},{12,... | collective-permute-start | bytes 98312 | tf_op jit(solution)/shard_map/ppermute | solution.py:416
  108.7 2.5 %shard_map.81 = (f32[16,18,128]{2,1,0:T(8,128)}, f32[16,18,128]{2,1,0:T(8,128)}, f32[16,18,128]{2,1,0:T(8,128)}, f32[16,18,128]{2,1,0:T(8,128)}, f32[15,18,128]{...) custom-call(f32[16,20,128]{2,1,0:T(8,128)} %pad_dynamic-slice_fusion.1.eta_ref, ...), custom_call_target="tpu_custom_call" | custom-call | tf_op jit(solution)/shard_map/pallas_call | solution.py:299
  111.7 2.2 %concatenate.35.b_ref = f32[2,16,18,128]{3,2,1,0:T(8,128)} concatenate(f32[2,16,2,128]{3,2,1,0:T(2,128)S(1)} %collective-permute-done.4, f32[2,16,2,128]{3,2,1,0:T(2,128)S(1)} %collective-permute-done.5, f32[2,16,2,128]{3,2,1,0:T(2,128)S(1)} %collective-permute-done.6, f32[2,16,2,128]{3,2,1,0:T(2,128)S(1)} %collective-permute-done.7, f32[2,16,2,128]{3,2,1,0:T(2,128)S(1)} %copy_multiply_fusion, ...), dimensions={2} | concatenate | bytes 589824 | tf_op jit(solution)/shard_map/concatenate | solution.py:417
  114.6 5.6 %shard_map.82 = f32[2,16,18,128]{3,2,1,0:T(8,128)} custom-call(f32[2,16,18,128]{3,2,1,0:T(8,128)} %concatenate.35.b_ref, f32[16,18,128]{2,1,0:T(8,128)} %get-tuple-element.52.fxl_ref, f32[16,18,128]{2,1,0:T(8,128)} %get-tuple-element.53.fxr_ref, f32[16,18,128]{2,1,0:T(8,128)} %get-tuple-element.54.fyl_ref, f32[16,18,128]{2,1,0:T(8,128)} %get-tuple-element.55.fyr_ref, ...), custom_call_target="tpu_custom_call" | custom-call | tf_op jit(solution)/shard_map/pallas_call | solution.py:318
  124.4 4.1 %shard_map.83 = (f32[2,16,8,256]{3,2,1,0:T(8,128)}, f32[2,16,6,256]{3,2,1,0:T(8,128)}) custom-call(f32[2,16,10,256]{3,2,1,0:T(8,128)} %slice_add_fusion.w_ref, f32[2,16,12,256]{3,2,1,0:T(8,128)} %pad_maximum_fusion.5.w_ref.b_ref, f32[16,12,256]{2,1,0:T(8,128)} %get-tuple-element.42.fxl_ref, f32[16,12,256]{2,1,0:T(8,128)} %get-tuple-element.43.fxr_ref, ...), custom_call_target="tpu_custom_call" | custom-call | tf_op jit(solution)/shard_map/pallas_call | solution.py:225
  132.8 8.4 %shard_map.84 = (f32[2,16,10,512]{3,2,1,0:T(8,128)}, f32[2,16,8,512]{3,2,1,0:T(8,128)}) custom-call(f32[2,16,12,512]{3,2,1,0:T(8,128)} %get-tuple-element.40.w_ref, f32[2,16,16,512]{3,2,1,0:T(8,128)} %get-tuple-element.78.b_ref, f32[16,14,512]{2,1,0:T(8,128)} %get-tuple-element.32.fxl_ref, f32[16,14,512]{2,1,0:T(8,128)} %get-tuple-element.33.fxr_ref, ...), custom_call_target="tpu_custom_call" | custom-call | tf_op jit(solution)/shard_map/pallas_call | solution.py:225
  (136 shorter events, 39.5 us)
Async XLA Ops:
  7.2 3.1 %copy-start.1 = (f32[2,16,8,512]{3,2,1,0:T(8,128)S(1)}, f32[2,16,8,512]{3,2,1,0:T(8,128)}, u32[]{:S(2)}) copy-start(f32[2,16,8,512]{3,2,1,0:T(8,128)} %param.6) | copy-start | bytes 1572868
  7.2 57.3 %all-gather.3.cloned.1.call-start = ((), (), s32[]{:S(2)}) async-start(), calls=%async_computation | async-start | bytes 1253376 | tf_op jit(solution)/shard_map/all_gather | solution.py:430
  8.7 12.1 %copy-start.6 = (f32[16,8,512]{2,1,0:T(8,128)}, f32[16,8,512]{2,1,0:T(8,128)S(1)}, u32[]{:S(2)}) copy-start(f32[16,8,512]{2,1,0:T(8,128)S(1)} %multiply_add_fusion) | copy-start | bytes 786436
  10.1 1.0 copy-start.3
  12.1 13.3 %collective-permute-start = (f32[167936]{0:T(1024)}, f32[167936]{0:T(1024)S(1)}, u32[]{:S(2)}, u32[]{:S(2)}) collective-permute-start(f32[167936]{0:T(1024)} %pad_maximum_fusion.2), channel_id=1, source_target_pairs={{0,1},{1,2},{2,3},{3,4},{4,5},{5,6},{6,7},{7,8},{8,9},{9,10},{10,1... | collective-permute-start | bytes 2015240 | tf_op jit(solution)/shard_map/ppermute | solution.py:42
  14.2 12.9 %collective-permute-start.1 = (f32[167936]{0:T(1024)S(1)}, f32[167936]{0:T(1024)S(1)}, u32[]{:S(2)}, u32[]{:S(2)}) collective-permute-start(f32[167936]{0:T(1024)S(1)} %pad_maximum_fusion.3), channel_id=1, source_target_pairs={{1,0},{2,1},{3,2},{4,3},{5,4},{6,5},{7,6},{8,7},{9,8},{10,9},{11,1... | collective-permute-start | bytes 2015240 | tf_op jit(solution)/shard_map/ppermute | solution.py:43
  28.1 1.4 slice-start.1
  29.4 6.7 %copy-start.2 = (f32[2,16,8,512]{3,2,1,0:T(8,128)S(1)}, f32[2,16,8,512]{3,2,1,0:T(8,128)}, u32[]{:S(2)}) copy-start(f32[2,16,8,512]{3,2,1,0:T(8,128)} %param.7) | copy-start | bytes 1572868
  39.2 9.6 %copy-start.9 = (s32[512]{0:T(512)S(1)}, s32[512]{0:T(512)}, u32[]{:S(2)}) copy-start(s32[512]{0:T(512)} %copy-done.8) | copy-start | bytes 6148
  50.9 10.4 %collective-permute-start.2 = (f32[2,16,4,256]{3,2,1,0:T(4,128)S(1)}, f32[2,16,4,256]{3,2,1,0:T(4,128)S(1)}, u32[]{:S(2)}, u32[]{:S(2)}) collective-permute-start(f32[2,16,4,256]{3,2,1,0:T(4,128)S(1)} %broadcast_multiply_fusion.1), channel_id=1, source_target_pairs={{0,1},{1,2},{2,3},{3,4},{4,5},{5,6},{6,7},{7,8},{8,9},{9,10},{10,1... | collective-permute-start | bytes 393224 | tf_op jit(solution)/shard_map/ppermute | solution.py:27
  59.2 4.4 %collective-permute-start.3 = (f32[2,16,4,256]{3,2,1,0:T(4,128)S(1)}, f32[2,16,4,256]{3,2,1,0:T(4,128)S(1)}, u32[]{:S(2)}, u32[]{:S(2)}) collective-permute-start(f32[2,16,4,256]{3,2,1,0:T(4,128)S(1)} %broadcast_multiply_fusion.1), channel_id=1, source_target_pairs={{1,0},{2,1},{3,2},{4,3},{5,4},{6,5},{7,6},{8,7},{9,8},{10,9},{11,1... | collective-permute-start | bytes 393224 | tf_op jit(solution)/shard_map/ppermute | solution.py:29
  65.9 1.1 copy-start
  68.1 0.9 slice-start
  80.8 18.6 %collective-permute-start.10 = (f32[2,16,2,128]{3,2,1,0:T(2,128)S(1)}, f32[2,16,2,128]{3,2,1,0:T(2,128)S(1)}, u32[]{:S(2)}, u32[]{:S(2)}) collective-permute-start(f32[2,16,2,128]{3,2,1,0:T(2,128)S(1)} %copy_multiply_fusion), channel_id=1, source_target_pairs={{3,0},{4,1},{5,2},{6,3},{7,4},{8,5},{9,6},{10,7},{11,8},{12,9},{13... | collective-permute-start | bytes 98312 | tf_op jit(solution)/shard_map/ppermute | solution.py:416
  85.1 16.2 %collective-permute-start.11 = (f32[2,16,2,128]{3,2,1,0:T(2,128)S(1)}, f32[2,16,2,128]{3,2,1,0:T(2,128)S(1)}, u32[]{:S(2)}, u32[]{:S(2)}) collective-permute-start(f32[2,16,2,128]{3,2,1,0:T(2,128)S(1)} %copy_multiply_fusion), channel_id=1, source_target_pairs={{4,0},{5,1},{6,2},{7,3},{8,4},{9,5},{10,6},{11,7},{12,8},{13,9},{1... | collective-permute-start | bytes 98312 | tf_op jit(solution)/shard_map/ppermute | solution.py:416
  87.1 18.8 %collective-permute-start.4 = (f32[2,16,2,128]{3,2,1,0:T(2,128)S(1)}, f32[2,16,2,128]{3,2,1,0:T(2,128)S(1)}, u32[]{:S(2)}, u32[]{:S(2)}) collective-permute-start(f32[2,16,2,128]{3,2,1,0:T(2,128)S(1)} %copy_multiply_fusion), channel_id=1, source_target_pairs={{0,4},{1,5},{2,6},{3,7},{4,8},{5,9},{6,10},{7,11},{8,12},{9,13},{1... | collective-permute-start | bytes 98312 | tf_op jit(solution)/shard_map/ppermute | solution.py:415
  91.0 20.2 %collective-permute-start.5 = (f32[2,16,2,128]{3,2,1,0:T(2,128)S(1)}, f32[2,16,2,128]{3,2,1,0:T(2,128)S(1)}, u32[]{:S(2)}, u32[]{:S(2)}) collective-permute-start(f32[2,16,2,128]{3,2,1,0:T(2,128)S(1)} %copy_multiply_fusion), channel_id=1, source_target_pairs={{0,3},{1,4},{2,5},{3,6},{4,7},{5,8},{6,9},{7,10},{8,11},{9,12},{10... | collective-permute-start | bytes 98312 | tf_op jit(solution)/shard_map/ppermute | solution.py:415
  92.9 18.2 %collective-permute-start.6 = (f32[2,16,2,128]{3,2,1,0:T(2,128)S(1)}, f32[2,16,2,128]{3,2,1,0:T(2,128)S(1)}, u32[]{:S(2)}, u32[]{:S(2)}) collective-permute-start(f32[2,16,2,128]{3,2,1,0:T(2,128)S(1)} %copy_multiply_fusion), channel_id=1, source_target_pairs={{0,2},{1,3},{2,4},{3,5},{4,6},{5,7},{6,8},{7,9},{8,10},{9,11},{10,... | collective-permute-start | bytes 98312 | tf_op jit(solution)/shard_map/ppermute | solution.py:415
  99.4 11.8 %collective-permute-start.7 = (f32[2,16,2,128]{3,2,1,0:T(2,128)S(1)}, f32[2,16,2,128]{3,2,1,0:T(2,128)S(1)}, u32[]{:S(2)}, u32[]{:S(2)}) collective-permute-start(f32[2,16,2,128]{3,2,1,0:T(2,128)S(1)} %copy_multiply_fusion), channel_id=1, source_target_pairs={{0,1},{1,2},{2,3},{3,4},{4,5},{5,6},{6,7},{7,8},{8,9},{9,10},{10,1... | collective-permute-start | bytes 98312 | tf_op jit(solution)/shard_map/ppermute | solution.py:415
  101.3 9.8 %collective-permute-start.8 = (f32[2,16,2,128]{3,2,1,0:T(2,128)S(1)}, f32[2,16,2,128]{3,2,1,0:T(2,128)S(1)}, u32[]{:S(2)}, u32[]{:S(2)}) collective-permute-start(f32[2,16,2,128]{3,2,1,0:T(2,128)S(1)} %copy_multiply_fusion), channel_id=1, source_target_pairs={{1,0},{2,1},{3,2},{4,3},{5,4},{6,5},{7,6},{8,7},{9,8},{10,9},{11,1... | collective-permute-start | bytes 98312 | tf_op jit(solution)/shard_map/ppermute | solution.py:416
  105.9 5.8 %collective-permute-start.9 = (f32[2,16,2,128]{3,2,1,0:T(2,128)S(1)}, f32[2,16,2,128]{3,2,1,0:T(2,128)S(1)}, u32[]{:S(2)}, u32[]{:S(2)}) collective-permute-start(f32[2,16,2,128]{3,2,1,0:T(2,128)S(1)} %copy_multiply_fusion), channel_id=1, source_target_pairs={{2,0},{3,1},{4,2},{5,3},{6,4},{7,5},{8,6},{9,7},{10,8},{11,9},{12,... | collective-permute-start | bytes 98312 | tf_op jit(solution)/shard_map/ppermute | solution.py:416
  120.2 1.9 %copy-start.5 = (f32[2,16,10,256]{3,2,1,0:T(8,128)S(1)}, f32[2,16,10,256]{3,2,1,0:T(8,128)}, u32[]{:S(2)}) copy-start(f32[2,16,10,256]{3,2,1,0:T(8,128)} %get-tuple-element.50) | copy-start | bytes 983044
  132.8 8.4 %copy-start.7 = (f32[2,8,512]{2,1,0:T(8,128)S(1)}, f32[2,8,512]{2,1,0:T(8,128)}, u32[]{:S(2)}) copy-start(f32[2,8,512]{2,1,0:T(8,128)} %param.11) | copy-start | bytes 98308
  132.8 8.4 %copy-start.10 = (pred[8,512]{1,0:T(8,128)(4,1)S(1)}, pred[8,512]{1,0:T(8,128)(4,1)}, u32[]{:S(2)}) copy-start(pred[8,512]{1,0:T(8,128)(4,1)} %get-tuple-element.63) | copy-start | bytes 12292
  (2 other events, 1.4 us)
Sparse Core Ops, SparseCore 0:
  20.9 37.7 all-gather.2
